TPU v7x, 128 devices: a whole 4x4x4 slice. The times are simulated.
128 devices in a mesh: seq: 32 (over x, z, core), grp: 4 (over y).
Axes of the slice: x: 4, y: 4, z: 4, core: 2. Of those that a mesh axis runs over, the one named last changes fastest.
Arguments:
- queries: bfloat16 [65536, 768], P(('grp', 'seq')), parts along dimension 0, may hold values from -6 to 6
- keys: bfloat16 [65536, 768], P(('grp', 'seq')), parts along dimension 0, may hold values from -6 to 6
- values: bfloat16 [65536, 768], P(('grp', 'seq')), parts along dimension 0, may hold values from -6.5 to 6.5
- out_grad: bfloat16 [65536, 768], P(('grp', 'seq')), parts along dimension 0, may hold values from -6 to 6
- random_blocks: int32 [1024, 12, 3], P(('grp', 'seq')), parts along dimension 0, may hold values from 0 to 255, as said below
- global_blocks: int32 [8], P('grp'), parts along dimension 0, may hold values from 0 to 255, as said below
Outputs:
- attended: bfloat16 [65536, 768], P(('grp', 'seq')), parts along dimension 0
- query_grad: bfloat16 [65536, 768], P(('grp', 'seq')), parts along dimension 0
- key_grad: bfloat16 [65536, 768], P(('grp', 'seq')), parts along dimension 0
- value_grad: bfloat16 [65536, 768], P(('grp', 'seq')), parts along dimension 0
There are 4 independent parts, one for each index of `grp`. A program takes and returns all parts, laid end to end along the dimension named above; each array names one. Nothing has to cross between parts.
Inputs may be any that keep to these rules, and one draw needn't show every extreme that they name: `random_blocks`: each entry lies on a device other than that of the query block; the 3 entries of one query block and head are distinct; of all entries of the blocks of one device, at most 14 lie on any one device, and exactly 14 on some device, for every device. `global_blocks`: two distinct block numbers, one of which is the last block 255.
All inputs are finite; a program needn't handle non-finite values.
Results may differ from a plain program's by a relative error of at most 0.03.
Values may be sent and summed in bfloat16 or wider, within the bound.
No kernel may reach another device: no remote copies, remote signals or barrier semaphores. Data moves between devices by JAX's collectives and lax.ppermute only.
A program may use at most 384 MiB of HBM per device.

v0:
```python
import math

import jax
import jax.numpy as jnp
from jax import lax
from jax.sharding import PartitionSpec as P

H = 12
HD = 64
BLK = 64
R = 3
NG = 2
QGROUP = 8
SLOTS = 8


def padded_2(block, sides, width):
    for axis, dim in sides:
        count = lax.axis_size(axis)
        forward = [(i, i + 1) for i in range(count - 1)]
        forward.append((count - 1, 0))
        backward = [(target, source) for source, target in forward]
        low = lax.ppermute(
            lax.slice_in_dim(block, block.shape[dim] - width, None, axis=dim), axis, forward
        )
        high = lax.ppermute(lax.slice_in_dim(block, 0, width, axis=dim), axis, backward)
        block = jnp.concatenate([low, block, high], axis=dim)
    return block


def from_root(value, axis, source):
    kept = jnp.where(lax.axis_index(axis) == source, value, 0).astype(value.dtype)
    return lax.psum(kept, axis)


def head_blocks(matrix, blocks):
    return matrix.reshape(blocks, BLK, H, HD).transpose(0, 2, 1, 3)


def token_rows(blocked):
    blocks = blocked.shape[0]
    return blocked.transpose(0, 2, 1, 3).reshape(blocks * BLK, H * HD)


def pair_heads(rows, blocks):
    return (
        rows.reshape(blocks, BLK, 2, H, HD).transpose(0, 3, 1, 2, 4).reshape(blocks, H, BLK, 2 * HD)
    )


def slot_plan(block_lists, per_dev, devices, head_ids):
    owners = (block_lists // per_dev).reshape(-1)
    req_codes = (block_lists % per_dev * H + head_ids[None, :, None]).reshape(-1)
    onehot = (owners[:, None] == jnp.arange(devices, dtype=jnp.int32)[None, :]).astype(jnp.int32)
    before = jnp.cumsum(onehot, axis=0) - onehot
    return (owners, jnp.sum(before * onehot, axis=1), req_codes)


def sparse_group(query_g, grad_g, keyvals, allowed, factor):
    key_part = keyvals[..., :HD]
    value_part = keyvals[..., HD:]
    scores = (
        jnp.einsum("ghqd,ghkd->ghqk", query_g, key_part, preferred_element_type=jnp.float32)
        * factor
    )
    mask = allowed[:, :, None, :]
    row_max = jnp.max(jnp.where(mask, scores, -1e30), axis=-1, keepdims=True)
    expo = jnp.where(mask, jnp.exp(scores - row_max), 0.0)
    totals = jnp.sum(expo, axis=-1, keepdims=True)
    result = (
        jnp.einsum(
            "ghqk,ghkd->ghqd",
            expo.astype(jnp.bfloat16),
            value_part,
            preferred_element_type=jnp.float32,
        )
        / totals
    )
    probs = expo / totals
    dprobs = jnp.einsum("ghqd,ghkd->ghqk", grad_g, value_part, preferred_element_type=jnp.float32)
    dotted = jnp.sum(grad_g.astype(jnp.float32) * result, axis=-1, keepdims=True)
    dscore = (probs * (dprobs - dotted)).astype(jnp.bfloat16)
    dquery = factor * jnp.einsum(
        "ghqk,ghkd->ghqd", dscore, key_part, preferred_element_type=jnp.float32
    )
    dkey = factor * jnp.einsum(
        "ghqk,ghqd->ghkd", dscore, query_g, preferred_element_type=jnp.float32
    )
    dvalue = jnp.einsum(
        "ghqk,ghqd->ghkd", probs.astype(jnp.bfloat16), grad_g, preferred_element_type=jnp.float32
    )
    stats = jnp.stack([row_max[..., 0], totals[..., 0], dotted[..., 0]], axis=1)
    return (result, dquery, jnp.concatenate([dkey, dvalue], axis=-1), stats)


def per_device(queries, keys, values, out_grad, random_blocks, global_blocks):
    tokens = queries.shape[0]
    width = queries.shape[1]
    per_dev = tokens // BLK
    devices = lax.axis_size("seq")
    me_index = lax.axis_index("seq")
    blocks_all = per_dev * devices
    factor = 1.0 / math.sqrt(HD)
    entry_count = per_dev * H * R
    capacity = (entry_count + devices - 2) // (devices - 1) + 4
    head_ids = jnp.arange(H, dtype=jnp.int32)
    block_ids = me_index * per_dev + jnp.arange(per_dev, dtype=jnp.int32)
    is_global = jnp.any(block_ids[:, None] == global_blocks[None, :], axis=1)
    row_global = jnp.repeat(is_global, BLK)
    masked = jnp.where(row_global[:, None], jnp.zeros_like(out_grad), out_grad)
    kv_rows = jnp.concatenate([keys, values], axis=1)
    edge_rows = jnp.concatenate([kv_rows[:BLK], kv_rows[-BLK:]], axis=0)
    padded = padded_2(edge_rows, (("seq", 0),), BLK)
    left_rows = padded[:BLK]
    right_rows = padded[3 * BLK :]
    extended = jnp.concatenate(
        [
            left_rows[None, :, : 2 * width],
            kv_rows.reshape(per_dev, BLK, 2 * width),
            right_rows[None, :, : 2 * width],
        ],
        axis=0,
    )
    kv_heads = pair_heads(extended, per_dev + 2)
    kv_local = kv_heads[1 : per_dev + 1]
    global_rows = []
    for number in range(NG):
        global_id = global_blocks[number]
        row_start = global_id % per_dev * BLK
        picked = jnp.concatenate(
            [
                lax.dynamic_slice_in_dim(source, row_start, BLK, 0)
                for source in (queries, keys, values, out_grad)
            ],
            axis=1,
        )
        global_rows.append(from_root(picked, "seq", global_id // per_dev))
    grows = jnp.stack(global_rows)
    g_query = grows[:, :, :width].reshape(NG, BLK, H, HD)
    g_grad = grows[:, :, 3 * width :].reshape(NG, BLK, H, HD)
    g_kv = pair_heads(grows[:, :, width : 3 * width], NG)
    owners, slot_ids, req_codes = slot_plan(random_blocks, per_dev, devices, head_ids)
    outgoing = jnp.zeros((devices, capacity), jnp.int32).at[owners, slot_ids].set(req_codes)
    wanted = lax.all_to_all(outgoing, "seq", split_axis=0, concat_axis=0, tiled=True)
    sending = kv_local.reshape(per_dev * H, BLK, 2 * HD)[wanted]
    fetched = lax.all_to_all(sending, "seq", split_axis=0, concat_axis=0, tiled=True)
    rand_kv = fetched[owners, slot_ids].reshape(per_dev, H, R, BLK, 2 * HD)
    shifts = jnp.arange(-1, 2, dtype=jnp.int32)
    window_ids = (block_ids[:, None] + shifts[None, :]) % blocks_all
    other_ids = jnp.concatenate(
        [jnp.broadcast_to(window_ids[:, None, :], (per_dev, H, 3)), random_blocks], axis=2
    )
    global_kept = jnp.all(global_blocks[None, None, :, None] != other_ids[:, :, None, :], axis=3)
    allowed = jnp.concatenate(
        [jnp.ones((per_dev, H, 3), jnp.bool_), global_kept, jnp.ones((per_dev, H, R), jnp.bool_)],
        axis=2,
    )
    allowed = jnp.repeat(allowed, BLK, axis=2)
    query_heads = head_blocks(queries, per_dev)
    grad_heads = head_blocks(masked, per_dev)
    group = QGROUP
    groups = per_dev // group
    glob_slots = jnp.broadcast_to(g_kv.transpose(1, 0, 2, 3)[None], (group, H, NG, BLK, 2 * HD))

    def run_group(number):
        win_slots = jnp.stack(
            [kv_heads[0:group], kv_heads[1 : group + 1], kv_heads[2 : group + 2]], axis=2
        )
        keyvals = jnp.concatenate([win_slots, glob_slots, rand_kv], axis=2).reshape(
            group, H, SLOTS * BLK, 2 * HD
        )
        result, dquery, terms, stats = sparse_group(
            query_heads, grad_heads, keyvals, allowed, factor
        )
        terms = terms.reshape(group, H, SLOTS, BLK, 2 * HD)
        spacing = ((0, 0), (0, 0), (0, 0), (0, 0))
        window_sum = (
            jnp.pad(terms[:, :, 0], ((0, 2),) + spacing[1:])
            + jnp.pad(terms[:, :, 1], ((1, 1),) + spacing[1:])
            + jnp.pad(terms[:, :, 2], ((2, 0),) + spacing[1:])
        )
        global_sum = jnp.sum(terms[:, :, 3 : 3 + NG], axis=0)
        random_out = terms[:, :, 3 + NG :].astype(jnp.bfloat16)
        return (result, dquery, window_sum, global_sum, random_out, stats)

    mapped = lax.map(run_group, jnp.arange(groups, dtype=jnp.int32))
    result = mapped[0].reshape(per_dev, H, BLK, HD)
    dquery = mapped[1].reshape(per_dev, H, BLK, HD)
    place = (
        jnp.arange(groups, dtype=jnp.int32)[:, None] * group
        + jnp.arange(group + 2, dtype=jnp.int32)[None, :]
    ).reshape(-1)
    padded_grads = (
        jnp.zeros((per_dev + 2, H, BLK, 2 * HD), jnp.float32)
        .at[place]
        .add(mapped[2].reshape(-1, H, BLK, 2 * HD))
    )
    global_part = jnp.sum(mapped[3], axis=0).transpose(1, 0, 2, 3)
    random_out = mapped[4].reshape(-1, BLK, 2 * HD)
    stats = mapped[5].reshape(per_dev, 3, H, BLK)
    own_grads = padded_grads[1 : per_dev + 1]
    edge_pair = jnp.stack([padded_grads[0], padded_grads[per_dev + 1]])
    near_grads = padded_2(edge_pair.astype(jnp.bfloat16), (("seq", 0),), 1).astype(edge_pair.dtype)
    own_grads = own_grads.at[0].add(near_grads[0]).at[per_dev - 1].add(near_grads[3])
    back_buffer = (
        jnp.zeros((devices, capacity, BLK, 2 * HD), jnp.bfloat16)
        .at[owners, slot_ids]
        .set(random_out)
    )
    returned = lax.all_to_all(back_buffer, "seq", split_axis=0, concat_axis=0, tiled=True)
    table_grads = (
        jnp.zeros((per_dev * H, BLK, 2 * HD), jnp.float32)
        .at[wanted.reshape(-1)]
        .add(returned.reshape(-1, BLK, 2 * HD).astype(jnp.float32))
    )
    own_grads = own_grads + table_grads.reshape(per_dev, H, BLK, 2 * HD)
    key_tok = keys.reshape(tokens, H, HD)
    value_tok = values.reshape(tokens, H, HD)
    scores = (
        jnp.einsum("gqhd,khd->ghqk", g_query, key_tok, preferred_element_type=jnp.float32) * factor
    )
    local_max = jnp.max(scores, axis=-1)
    row_top = lax.pmax(local_max, "seq")
    expo = jnp.exp(scores - row_top[..., None])
    part_acc = jnp.einsum(
        "ghqk,khd->ghqd", expo.astype(jnp.bfloat16), value_tok, preferred_element_type=jnp.float32
    )
    row_tot, row_acc = (
        lax.psum(jnp.sum(expo, axis=-1).astype(jnp.bfloat16), "seq").astype(jnp.float32),
        lax.psum(part_acc.astype(jnp.bfloat16), "seq").astype(jnp.float32),
    )
    global_out = row_acc / row_tot[..., None]
    probs = jnp.exp(scores - row_top[..., None]) / row_tot[..., None]
    dprobs = jnp.einsum("gqhd,khd->ghqk", g_grad, value_tok, preferred_element_type=jnp.float32)
    dotted = jnp.sum(g_grad.transpose(0, 2, 1, 3).astype(jnp.float32) * global_out, axis=-1)
    dscore = (probs * (dprobs - dotted[..., None])).astype(jnp.bfloat16)
    g_dquery = factor * jnp.einsum(
        "ghqk,khd->ghqd", dscore, key_tok, preferred_element_type=jnp.float32
    )
    tok_dkey = factor * jnp.einsum(
        "ghqk,gqhd->khd", dscore, g_query, preferred_element_type=jnp.float32
    )
    tok_dvalue = jnp.einsum(
        "ghqk,gqhd->khd", probs.astype(jnp.bfloat16), g_grad, preferred_element_type=jnp.float32
    )
    dquery_sum, global_sum = (
        lax.psum(g_dquery.astype(jnp.bfloat16), "seq").astype(jnp.float32),
        lax.psum(global_part.astype(jnp.bfloat16), "seq").astype(jnp.float32),
    )
    for number in range(NG):
        owned = global_blocks[number] // per_dev == me_index
        local_block = global_blocks[number] % per_dev
        result = result.at[local_block].set(
            jnp.where(owned, global_out[number], result[local_block])
        )
        dquery = dquery.at[local_block].add(jnp.where(owned, dquery_sum[number], 0.0))
        own_grads = own_grads.at[local_block].add(jnp.where(owned, global_sum[number], 0.0))
    attended = token_rows(result).astype(jnp.bfloat16)
    query_grad = token_rows(dquery).astype(jnp.bfloat16)
    key_grad = (token_rows(own_grads[..., :HD]) + tok_dkey.reshape(tokens, width)).astype(
        jnp.bfloat16
    )
    value_grad = (token_rows(own_grads[..., HD:]) + tok_dvalue.reshape(tokens, width)).astype(
        jnp.bfloat16
    )
    return (attended, query_grad, key_grad, value_grad)


def solution(mesh):
    return jax.shard_map(
        per_device,
        mesh=mesh,
        in_specs=(
            P(("grp", "seq"), None),
            P(("grp", "seq"), None),
            P(("grp", "seq"), None),
            P(("grp", "seq"), None),
            P(("grp", "seq"), None, None),
            P("grp"),
        ),
        out_specs=(
            P(("grp", "seq"), None),
            P(("grp", "seq"), None),
            P(("grp", "seq"), None),
            P(("grp", "seq"), None),
        ),
        check_vma=False,
    )
```

profile of v0, /device:TPU:19, one launch (start us, length us, event | category | flops | bytes accessed | tf_op | source)
XLA Modules:
  0.0 1084.8 jit_solution(1959205801526926620)
XLA Ops:
  10.1 15.5 %scatter_fusion = s32[32,14]{0,1:T(8,128)S(1)} fusion(s32[32,14]{0,1:T(8,128)S(1)} %broadcast.325, s32[288]{0:T(512)S(1)} %get-tuple-element.149, s32[288]{0:T(512)S(1)} %reshape.576), kind=kCustom, calls=%fused_computation.2 | custom fusion | bytes 5760 | tf_op jit(solution)/shard_map/scatter | solution.py:143
  26.3 8.8 all-to-all-start
  57.8 5.2 maximum_bitcast_fusion
  66.5 5.9 copy.142
  72.4 5.3 reshape.537
  77.8 13.3 %gather_fusion = bf16[448,64,128]{2,1,0:T(8,128)(2,1)} fusion(bf16[96,64,128]{2,1,0:T(8,128)(2,1)S(1)} %reshape.537, s32[1024]{0:T(1024)S(1)} %pad_clamp_fusion), kind=kCustom, calls=%fused_computation | custom fusion | bytes 14681856 | tf_op jit(solution)/shard_map/gather | solution.py:145
  91.1 10.2 all-to-all-start.1
  130.4 7.9 copy.141
  146.8 5.9 copy.143
  152.7 5.3 stack.25
  159.7 108.0 %all-reduce.14.cloned.1.call-done = (bf16[1,64,3072]{2,1,0:T(8,128)(2,1)}, bf16[1,64,3072]{2,1,0:T(8,128)(2,1)}) async-done(((bf16[1,64,3072]{2,1,0:T(8,128)(2,1)}, bf16[1,64,3072]{2,1,0:T(8,128)(2,1)}), (bf16[1,64,3072]{2,1,0:T(8,128)(2,1)}, bf16[1,64,3072]{2,1,0:T(8,128)(2,1)})) %all-reduce.14.cloned.1.call-update) | async-done | bytes 786448 | tf_op jit(solution)/shard_map/psum | solution.py:33
  276.5 104.9 %pmax.7 = f32[2,12,64]{2,0,1:T(2,128)} all-reduce(f32[2,12,64]{2,0,1:T(2,128)} %get-tuple-element.188), channel_id=1, replica_groups=mesh['seq'=32,'grp'=4] {'seq'}, use_global_device_ids=true, to_apply=%region_11.12 | all-reduce | flops 1536 | bytes 12288 | tf_op jit(solution)/shard_map/pmax | solution.py:223
  383.5 68.8 %psum.45 = bf16[2,12,64]{2,0,1:T(2,128)(2,1)S(1)} all-reduce(bf16[2,12,64]{2,0,1:T(2,128)(2,1)} %fusion.22), channel_id=1, replica_groups=mesh['seq'=32,'grp'=4] {'seq'}, use_global_device_ids=true, to_apply=%region_14.15 | all-reduce | flops 1536 | bytes 6144 | tf_op jit(solution)/shard_map/psum | solution.py:229
  456.5 8.0 gather_fusion.1
  464.6 6.0 constant_dynamic-update-slice_fusion.4
  470.5 14.1 %fusion.6 = f32[8,12,512,64]{2,3,1,0:T(8,128)} fusion(bf16[8,12,512,128]{3,2,1,0:T(8,128)(2,1)} %bitcast.15, bf16[8,12,64,64]{2,0,3,1:T(8,128)(2,1)} %bitcast.186), kind=kOutput, calls=%fused_computation.19 | convolution fusion | flops 402653184 | bytes 25952256 | tf_op jit(solution)/shard_map/while/body/eval_jaxpr/ghqd,ghkd->ghqk/dot_general | solution.py:63
  484.6 15.5 %bitcast_reduce_fusion = (f32[8,12,64]{2,1,0:T(8,128)S(1)}, f32[8,12,512,64]{2,3,1,0:T(8,128)}) fusion(f32[8,12,512,64]{2,3,1,0:T(8,128)} %fusion.6, pred[8,12,512]{2,1,0:T(8,128)(4,1)} %copy.137), kind=kOutput, calls=%fused_computation.9 | output fusion | flops 18874880 | bytes 25239552 | tf_op jit(solution)/shard_map/while/body/eval_jaxpr/sub | solution.py:68
  500.1 16.3 %multiply_reduce_fusion = (f32[8,12,64]{2,1,0:T(8,128)}, bf16[8,12,64,64]{2,3,1,0:T(8,128)(2,1)}) fusion(bf16[8,64,12,64]{1,3,2,0:T(8,128)(2,1)S(1)} %copy-done.11, f32[8,12,64]{2,1,0:T(8,128)S(1)} %get-tuple-element.186, bf16[8,12,512,128]{3,2,1,0:T(8,128)(2,1)} %bitcast.15, f32[8,12,512,64]{2,3,1,0:T(8,128)} %get-tuple-element.187), kind=kOutput, calls=%fused_computation.46 | convolution fusion | flops 404613120 | bytes 26787840 | tf_op jit(solution)/shard_map/while/body/eval_jaxpr/ghqk,ghkd->ghqd/dot_general | solution.py:71
  516.4 8.3 fusion.13
  524.7 13.5 %multiply_convert_fusion = bf16[8,12,64,512]{3,2,1,0:T(8,128)(2,1)} fusion(f32[8,12,64]{2,1,0:T(8,128)} %get-tuple-element.190, f32[8,12,64]{2,1,0:T(8,128)} %copy-done.20, f32[8,12,512,64]{2,3,1,0:T(8,128)} %get-tuple-element.187, bf16[8,12,512,128]{3,2,1,0:T(8,128)(2,1)} %bitcast.15, bf16[8,12,64,64]{3,1,2,0:T(8,128)(2,1)} %bitcast.190), kind=kOutput, calls=%fused_computation.11 | convolution fusion | flops 415236096 | bytes 32292864 | tf_op jit(solution)/shard_map/while/body/eval_jaxpr/ghqd,ghkd->ghqk/dot_general | solution.py:80
  538.3 5.2 broadcast_multiply_fusion
  545.1 8.7 pad_maximum_fusion
  553.8 24.6 %copy.176 = f32[8,12,512,128]{3,2,1,0:T(8,128)} copy(f32[8,12,512,128]{2,3,1,0:T(8,128)} %pad_maximum_fusion) | data formatting | bytes 50331648 | tf_op jit(solution)/shard_map/while/body/eval_jaxpr/concatenate | solution.py:93
  578.5 7.1 slice.439
  590.4 42.2 %scatter_fusion.2 = bf16[32,14,64,128]{3,2,1,0:T(8,128)(2,1)} fusion(bf16[32,14,64,128]{3,2,1,0:T(8,128)(2,1)} %broadcast_in_dim.148, s32[288]{0:T(512)S(1)} %copy-done.2, bf16[288,64,128]{2,1,0:T(8,128)(2,1)} %bitcast.189), kind=kCustom, calls=%fused_computation.4 | custom fusion | bytes 14158080 | tf_op jit(solution)/shard_map/scatter | solution.py:208
  632.6 23.2 %all-to-all-start.2 = ((bf16[32,14,64,128]{3,2,1,0:T(8,128)(2,1)}), bf16[32,14,64,128]{3,2,1,0:T(8,128)(2,1)}, u32[]{:S(2)}, u32[]{:S(2)}) async-start(bf16[32,14,64,128]{3,2,1,0:T(8,128)(2,1)} %scatter_fusion.2), calls=%async_computation.2 | async-start | bytes 14680064 | tf_op jit(solution)/shard_map/all_to_all | solution.py:210
  667.6 152.0 %all-reduce.10.cloned.1.call-done = bf16[2,12,64,64]{2,3,1,0:T(8,128)(2,1)} async-done(((bf16[2,12,64,64]{2,3,1,0:T(8,128)(2,1)}), bf16[2,12,64,64]{2,3,1,0:T(8,128)(2,1)}) %all-reduce.10.cloned.1.call-update) | async-done | bytes 196624 | tf_op jit(solution)/shard_map/psum | solution.py:230
  837.7 11.3 %scatter_fusion.1 = f32[10,12,64,128]{3,2,1,0:T(8,128)} fusion(f32[10,12,64,128]{3,2,1,0:T(8,128)} %broadcast_in_dim.146, s32[10]{0:T(128)S(1)} %iota.26, f32[10,12,64,128]{3,2,1,0:T(8,128)} %pad_add_fusion), kind=kCustom, calls=%fused_computation.3 | custom fusion | flops 983040 | bytes 11796520 | tf_op jit(solution)/shard_map/scatter-add | solution.py:196
  867.9 8.4 fusion.24
  884.4 103.4 %all-reduce.12.cloned.1.call-done = (bf16[2,12,64,64]{2,3,1,0:T(8,128)(2,1)}, bf16[2,12,64,128]{3,2,1,0:T(8,128)(2,1)}) async-done(((bf16[2,12,64,64]{2,3,1,0:T(8,128)(2,1)}, bf16[2,12,64,128]{3,2,1,0:T(8,128)(2,1)}), (bf16[2,12,64,64]{2,3,1,0:T(8,128)(2,1)}, bf16[2,12,64,128]{3,2,1,0:T(8,128)(2,1)})) %all-reduce.12.cloned.1.call-update) | async-done | bytes 589840 | tf_op jit(solution)/shard_map/psum | solution.py:247
  998.2 10.2 bitcast_convert_fusion.1
  1009.1 46.1 %scatter_fusion.3 = f32[96,64,128]{2,1,0:T(8,128)S(1)} fusion(f32[96,64,128]{2,1,0:T(8,128)S(1)} %broadcast_in_dim.147, s32[448]{0:T(512)S(1)} %bitcast.201, f32[448,64,128]{2,1,0:T(8,128)} %bitcast_convert_fusion.1), kind=kCustom, calls=%fused_computation.5 | custom fusion | flops 3670016 | bytes 44041984 | tf_op jit(solution)/shard_map/scatter-add | solution.py:214
  (185 shorter events, 175.6 us)
Async XLA Ops:
  7.2 27.9 %copy-start.6 = (bf16[512,768]{1,0:T(8,128)(2,1)S(1)}, bf16[512,768]{1,0:T(8,128)(2,1)}, u32[]{:S(2)}) copy-start(bf16[512,768]{1,0:T(8,128)(2,1)} %param.23) | copy-start | bytes 2359300
  10.1 26.3 %copy-start.1 = (s32[288]{0:T(512)}, s32[288]{0:T(512)S(1)}, u32[]{:S(2)}) copy-start(s32[288]{0:T(512)S(1)} %get-tuple-element.149) | copy-start | bytes 3460
  26.3 18.5 %all-to-all-start = ((s32[32,1,14]{2,1,0:T(1,128)}), s32[32,1,14]{2,1,0:T(1,128)}, u32[]{:S(2)}, u32[]{:S(2)}) async-start(s32[32,1,14]{2,1,0:T(1,128)} %copy.152), calls=%async_computation | async-start | bytes 32768 | tf_op jit(solution)/shard_map/all_to_all | solution.py:144
  37.1 9.9 collective-permute-start.1
  37.5 15.4 %collective-permute-start = (bf16[64,1536]{1,0:T(8,128)(2,1)S(1)}, bf16[64,1536]{1,0:T(8,128)(2,1)S(1)}, u32[]{:S(2)}, u32[]{:S(2)}) collective-permute-start(bf16[64,1536]{1,0:T(8,128)(2,1)S(1)} %get-tuple-element.168), channel_id=1, source_target_pairs={{0,4},{4,8},{8,12},{12,16},{16,20},{20,24},{24,28},{28,32},{32,36}... | collective-permute-start | bytes 589832 | tf_op jit(solution)/shard_map/ppermute | solution.py:23
  91.1 10.5 copy-start.18
  91.1 16.4 %copy-start.8 = (bf16[512,768]{1,0:T(8,128)(2,1)S(1)}, bf16[512,768]{1,0:T(8,128)(2,1)}, u32[]{:S(2)}) copy-start(bf16[512,768]{1,0:T(8,128)(2,1)} %param.24) | copy-start | bytes 2359300
  91.1 16.4 %copy-start.13 = (bf16[512,768]{1,0:T(8,128)(2,1)S(1)}, bf16[512,768]{1,0:T(8,128)(2,1)}, u32[]{:S(2)}) copy-start(bf16[512,768]{1,0:T(8,128)(2,1)} %param.22) | copy-start | bytes 2359300
  91.1 16.4 %copy-start.7 = (bf16[512,768]{1,0:T(8,128)(2,1)S(1)}, bf16[512,768]{1,0:T(8,128)(2,1)}, u32[]{:S(2)}) copy-start(bf16[512,768]{1,0:T(8,128)(2,1)} %param.23) | copy-start | bytes 2359300
  91.1 16.4 %copy-start.14 = (bf16[512,768]{1,0:T(8,128)(2,1)S(1)}, bf16[512,768]{1,0:T(8,128)(2,1)}, u32[]{:S(2)}) copy-start(bf16[512,768]{1,0:T(8,128)(2,1)} %param.25) | copy-start | bytes 2359300
  91.1 365.4 %all-to-all-start.1 = ((bf16[32,14,64,128]{3,2,1,0:T(8,128)(2,1)}), bf16[32,14,64,128]{3,2,1,0:T(8,128)(2,1)}, u32[]{:S(2)}, u32[]{:S(2)}) async-start(bf16[32,14,64,128]{3,2,1,0:T(8,128)(2,1)} %bitcast.185), calls=%async_computation.1 | async-start | bytes 14680064 | tf_op jit(solution)/shard_map/all_to_all | solution.py:146
  101.4 166.3 %all-reduce.14.cloned.1.call-start = ((), (), s32[]{:S(2)}) async-start(), calls=%async_computation.5 | async-start | bytes 1572864 | tf_op jit(solution)/shard_map/psum | solution.py:33
  115.4 7.6 copy-start.16
  115.4 9.0 copy-start.19
  115.4 12.4 %copy-start.3 = (bf16[8,12,64,2,64]{4,3,2,1,0:T(2,128)(2,1)S(1)}, bf16[8,12,64,2,64]{4,3,2,1,0:T(2,128)(2,1)}, u32[]{:S(2)}) copy-start(bf16[8,12,64,2,64]{4,3,2,1,0:T(2,128)(2,1)} %copy.142) | copy-start | bytes 4718596
  140.9 6.0 copy-start.4
  484.6 15.5 %copy-start.11 = (bf16[8,64,12,64]{1,3,2,0:T(8,128)(2,1)S(1)}, bf16[8,64,12,64]{1,3,2,0:T(8,128)(2,1)}, u32[]{:S(2)}) copy-start(bf16[8,64,12,64]{1,3,2,0:T(8,128)(2,1)} %copy.167) | copy-start | bytes 2359300
  500.1 16.3 %copy-start.20 = (f32[8,12,64]{2,1,0:T(8,128)}, f32[8,12,64]{2,1,0:T(8,128)S(1)}, u32[]{:S(2)}) copy-start(f32[8,12,64]{2,1,0:T(8,128)S(1)} %get-tuple-element.186) | copy-start | bytes 73732
  538.3 6.8 copy-start.5
  585.6 4.8 copy-start.2
  632.6 365.6 %all-to-all-start.2 = ((bf16[32,14,64,128]{3,2,1,0:T(8,128)(2,1)}), bf16[32,14,64,128]{3,2,1,0:T(8,128)(2,1)}, u32[]{:S(2)}, u32[]{:S(2)}) async-start(bf16[32,14,64,128]{3,2,1,0:T(8,128)(2,1)} %scatter_fusion.2), calls=%async_computation.2 | async-start | bytes 14680064 | tf_op jit(solution)/shard_map/all_to_all | solution.py:210
  655.8 163.7 %all-reduce.10.cloned.1.call-start = ((), (), s32[]{:S(2)}) async-start(), calls=%async_computation.3 | async-start | bytes 786432 | tf_op jit(solution)/shard_map/psum | solution.py:230
  663.8 323.9 %all-reduce.12.cloned.1.call-start = ((), (), s32[]{:S(2)}) async-start(), calls=%async_computation.4 | async-start | bytes 1572864 | tf_op jit(solution)/shard_map/psum | solution.py:247
  821.7 2.5 copy-start.9
  849.0 4.1 copy-start
  853.1 1.8 copy-start.12
  866.0 14.6 %collective-permute-start.3 = (bf16[1,12,64,128]{3,2,1,0:T(8,128)(2,1)S(1)}, bf16[1,12,64,128]{3,2,1,0:T(8,128)(2,1)}, u32[]{:S(2)}, u32[]{:S(2)}) collective-permute-start(bf16[1,12,64,128]{3,2,1,0:T(8,128)(2,1)S(1)} %get-tuple-element.167), channel_id=1, source_target_pairs={{4,0},{8,4},{12,8},{16,12},{20,16},{24,20},{28,24},{32,28},{36,32}... | collective-permute-start | bytes 589832 | tf_op jit(solution)/shard_map/ppermute | solution.py:26
  866.5 14.2 %collective-permute-start.2 = (bf16[1,12,64,128]{3,2,1,0:T(8,128)(2,1)S(1)}, bf16[1,12,64,128]{3,2,1,0:T(8,128)(2,1)}, u32[]{:S(2)}, u32[]{:S(2)}) collective-permute-start(bf16[1,12,64,128]{3,2,1,0:T(8,128)(2,1)S(1)} %get-tuple-element.166), channel_id=1, source_target_pairs={{0,4},{4,8},{8,12},{12,16},{16,20},{20,24},{24,28},{28,32},{32,36}... | collective-permute-start | bytes 589832 | tf_op jit(solution)/shard_map/ppermute | solution.py:23
  991.7 5.6 copy-start.15
  1008.4 0.7 copy-start.17
  1055.2 2.6 copy-start.10
Sparse Core Ops, SparseCore 0:
  109.4 158.2 all-reduce.13
  663.9 155.6 all-reduce.9
  880.8 106.8 all-reduce.11
where the time goes:
time: 1090 us; the launch traced here: 1080 us
  waiting for transfers between devices  363 us (33%)
  local copies, waits for them, and re-layouts  258 us (24%)
  blocking collectives  174 us (16%)
  other arithmetic  142 us (13%)
  matrix products  80.3 us (7%)
  starting transfers between devices  46.6 us (4%)
  between operations  19.8 us (2%)
    psum x1, waiting for transfers between devices, per_device(): lax.psum(part_acc.astype(jnp.bfloat16), 'seq').astype(jnp.float32)  152 us
    psum x1, waiting for transfers between devices, from_root(): return lax.psum(kept, axis)  108 us
    pmax x1, blocking collectives, per_device(): row_top = lax.pmax(local_max, 'seq')  105 us
    psum x1, waiting for transfers between devices, per_device(): lax.psum(g_dquery.astype(jnp.bfloat16), 'seq').astype(jnp.float32)  103 us
    psum x1, blocking collectives, per_device(): lax.psum(jnp.sum(expo, axis=-1).astype(jnp.bfloat16), 'seq')  68.8 us
    scatter-add x1, other arithmetic, per_device(): table_grads = jnp.zeros((per_dev * H, BLK, 2 * HD), jnp.float32).at[wante...  46.1 us
    scatter x1, local copies, waits for them, and re-layouts, per_device(): back_buffer = jnp.zeros((devices, capacity, BLK, 2 * HD), jnp.bfloat16).a...  42.2 us
    unnamed x57, local copies, waits for them, and re-layouts  31.2 us
  transfers between devices with their start and end apart: 10, of which 3 were waited for; matrix products, arithmetic and copies ran while one was open for 16% of the time, Pallas kernels for 0%

commit v1 on v0

--- a/solution.py
+++ b/solution.py
@@ -28,9 +28,23 @@
     return block
 
 
-def from_root(value, axis, source):
-    kept = jnp.where(lax.axis_index(axis) == source, value, 0).astype(value.dtype)
-    return lax.psum(kept, axis)
+def from_owners(value, owners):
+    devices = lax.axis_size("seq")
+    count = value.shape[0]
+    chunks = value.reshape(count, devices, -1).transpose(1, 0, 2)
+    got = lax.all_to_all(chunks, "seq", 0, 0, tiled=True)
+    mine = jnp.stack([got[owners[i], i] for i in range(count)])
+    full = lax.all_gather(mine, "seq", axis=0, tiled=False)
+    return full.transpose(1, 0, 2).reshape(value.shape)
+
+
+def summed_to_all(value):
+    devices = lax.axis_size("seq")
+    chunks = value.astype(jnp.bfloat16).reshape(devices, -1)
+    got = lax.all_to_all(chunks, "seq", 0, 0, tiled=True)
+    total = jnp.sum(got.astype(jnp.float32), axis=0).astype(jnp.bfloat16)
+    full = lax.all_gather(total, "seq", axis=0, tiled=True)
+    return full.reshape(value.shape).astype(jnp.float32)
 
 
 def head_blocks(matrix, blocks):
@@ -125,24 +139,28 @@
     kv_local = kv_heads[1 : per_dev + 1]
     global_rows = []
     for number in range(NG):
-        global_id = global_blocks[number]
-        row_start = global_id % per_dev * BLK
-        picked = jnp.concatenate(
-            [
-                lax.dynamic_slice_in_dim(source, row_start, BLK, 0)
-                for source in (queries, keys, values, out_grad)
-            ],
-            axis=1,
-        )
-        global_rows.append(from_root(picked, "seq", global_id // per_dev))
-    grows = jnp.stack(global_rows)
+        row_start = global_blocks[number] % per_dev * BLK
+        global_rows.append(
+            jnp.concatenate(
+                [
+                    lax.dynamic_slice_in_dim(source, row_start, BLK, 0)
+                    for source in (queries, keys, values, out_grad)
+                ],
+                axis=1,
+            )
+        )
+    grows = from_owners(jnp.stack(global_rows), global_blocks // per_dev)
     g_query = grows[:, :, :width].reshape(NG, BLK, H, HD)
     g_grad = grows[:, :, 3 * width :].reshape(NG, BLK, H, HD)
     g_kv = pair_heads(grows[:, :, width : 3 * width], NG)
     owners, slot_ids, req_codes = slot_plan(random_blocks, per_dev, devices, head_ids)
-    outgoing = jnp.zeros((devices, capacity), jnp.int32).at[owners, slot_ids].set(req_codes)
+    slot_key = owners * capacity + slot_ids
+    slot_hit = jnp.arange(devices * capacity, dtype=jnp.int32)[:, None] == slot_key[None, :]
+    outgoing = jnp.where(
+        jnp.any(slot_hit, axis=1), jnp.sum(jnp.where(slot_hit, req_codes[None, :], 0), axis=1), -1
+    ).reshape(devices, capacity)
     wanted = lax.all_to_all(outgoing, "seq", split_axis=0, concat_axis=0, tiled=True)
-    sending = kv_local.reshape(per_dev * H, BLK, 2 * HD)[wanted]
+    sending = kv_local.reshape(per_dev * H, BLK, 2 * HD)[jnp.maximum(wanted, 0)]
     fetched = lax.all_to_all(sending, "seq", split_axis=0, concat_axis=0, tiled=True)
     rand_kv = fetched[owners, slot_ids].reshape(per_dev, H, R, BLK, 2 * HD)
     shifts = jnp.arange(-1, 2, dtype=jnp.int32)
@@ -190,11 +208,14 @@
         jnp.arange(groups, dtype=jnp.int32)[:, None] * group
         + jnp.arange(group + 2, dtype=jnp.int32)[None, :]
     ).reshape(-1)
-    padded_grads = (
-        jnp.zeros((per_dev + 2, H, BLK, 2 * HD), jnp.float32)
-        .at[place]
-        .add(mapped[2].reshape(-1, H, BLK, 2 * HD))
-    )
+    if groups == 1:
+        padded_grads = mapped[2].reshape(per_dev + 2, H, BLK, 2 * HD)
+    else:
+        padded_grads = (
+            jnp.zeros((per_dev + 2, H, BLK, 2 * HD), jnp.float32)
+            .at[place]
+            .add(mapped[2].reshape(-1, H, BLK, 2 * HD))
+        )
     global_part = jnp.sum(mapped[3], axis=0).transpose(1, 0, 2, 3)
     random_out = mapped[4].reshape(-1, BLK, 2 * HD)
     stats = mapped[5].reshape(per_dev, 3, H, BLK)
@@ -202,17 +223,22 @@
     edge_pair = jnp.stack([padded_grads[0], padded_grads[per_dev + 1]])
     near_grads = padded_2(edge_pair.astype(jnp.bfloat16), (("seq", 0),), 1).astype(edge_pair.dtype)
     own_grads = own_grads.at[0].add(near_grads[0]).at[per_dev - 1].add(near_grads[3])
-    back_buffer = (
-        jnp.zeros((devices, capacity, BLK, 2 * HD), jnp.bfloat16)
-        .at[owners, slot_ids]
-        .set(random_out)
-    )
+    back_buffer = jnp.einsum(
+        "se,ef->sf",
+        slot_hit.astype(jnp.bfloat16),
+        random_out.reshape(-1, BLK * 2 * HD),
+        preferred_element_type=jnp.bfloat16,
+    ).reshape(devices, capacity, BLK, 2 * HD)
     returned = lax.all_to_all(back_buffer, "seq", split_axis=0, concat_axis=0, tiled=True)
-    table_grads = (
-        jnp.zeros((per_dev * H, BLK, 2 * HD), jnp.float32)
-        .at[wanted.reshape(-1)]
-        .add(returned.reshape(-1, BLK, 2 * HD).astype(jnp.float32))
-    )
+    code_hit = (
+        wanted.reshape(-1)[:, None] == jnp.arange(per_dev * H, dtype=jnp.int32)[None, :]
+    ).astype(jnp.bfloat16)
+    table_grads = jnp.einsum(
+        "sc,sf->cf",
+        code_hit,
+        returned.reshape(-1, BLK * 2 * HD),
+        preferred_element_type=jnp.float32,
+    ).reshape(per_dev * H, BLK, 2 * HD)
     own_grads = own_grads + table_grads.reshape(per_dev, H, BLK, 2 * HD)
     key_tok = keys.reshape(tokens, H, HD)
     value_tok = values.reshape(tokens, H, HD)
@@ -220,16 +246,28 @@
         jnp.einsum("gqhd,khd->ghqk", g_query, key_tok, preferred_element_type=jnp.float32) * factor
     )
     local_max = jnp.max(scores, axis=-1)
-    row_top = lax.pmax(local_max, "seq")
-    expo = jnp.exp(scores - row_top[..., None])
+    local_expo = jnp.exp(scores - local_max[..., None])
     part_acc = jnp.einsum(
-        "ghqk,khd->ghqd", expo.astype(jnp.bfloat16), value_tok, preferred_element_type=jnp.float32
-    )
-    row_tot, row_acc = (
-        lax.psum(jnp.sum(expo, axis=-1).astype(jnp.bfloat16), "seq").astype(jnp.float32),
-        lax.psum(part_acc.astype(jnp.bfloat16), "seq").astype(jnp.float32),
-    )
-    global_out = row_acc / row_tot[..., None]
+        "ghqk,khd->ghqd",
+        local_expo.astype(jnp.bfloat16),
+        value_tok,
+        preferred_element_type=jnp.float32,
+    )
+    row_shape = local_max.shape
+    packed = jnp.concatenate(
+        [local_max[..., None], jnp.sum(local_expo, axis=-1)[..., None], part_acc], axis=-1
+    ).reshape(devices, -1, HD + 2)
+    got = lax.all_to_all(packed, "seq", 0, 0, tiled=True)
+    top = jnp.max(got[..., 0], axis=0)
+    scale = jnp.exp(got[..., 0] - top[None])
+    tot = jnp.sum(scale * got[..., 1], axis=0)
+    acc = jnp.sum(scale[..., None] * got[..., 2:], axis=0) / tot[:, None]
+    merged = lax.all_gather(
+        jnp.concatenate([top[:, None], tot[:, None], acc], axis=-1), "seq", axis=0, tiled=True
+    )
+    row_top = merged[:, 0].reshape(row_shape)
+    row_tot = merged[:, 1].reshape(row_shape)
+    global_out = merged[:, 2:].reshape(row_shape + (HD,))
     probs = jnp.exp(scores - row_top[..., None]) / row_tot[..., None]
     dprobs = jnp.einsum("gqhd,khd->ghqk", g_grad, value_tok, preferred_element_type=jnp.float32)
     dotted = jnp.sum(g_grad.transpose(0, 2, 1, 3).astype(jnp.float32) * global_out, axis=-1)
@@ -243,10 +281,9 @@
     tok_dvalue = jnp.einsum(
         "ghqk,gqhd->khd", probs.astype(jnp.bfloat16), g_grad, preferred_element_type=jnp.float32
     )
-    dquery_sum, global_sum = (
-        lax.psum(g_dquery.astype(jnp.bfloat16), "seq").astype(jnp.float32),
-        lax.psum(global_part.astype(jnp.bfloat16), "seq").astype(jnp.float32),
-    )
+    both_sum = summed_to_all(jnp.concatenate([g_dquery, global_part], axis=-1))
+    dquery_sum = both_sum[..., :HD]
+    global_sum = both_sum[..., HD:]
     for number in range(NG):
         owned = global_blocks[number] // per_dev == me_index
         local_block = global_blocks[number] % per_dev

time: 1090 us -> 672 us (0.62)
  waiting for transfers between devices: 363 us -> 17.6 us
  blocking collectives: 174 us -> 120 us
  other arithmetic: 142 us -> 88.3 us
  local copies, waits for them, and re-layouts: 258 us -> 281 us
  matrix products: 80.3 us -> 95.6 us
    psum x3 -> x0, waiting for transfers between devices: 363 us -> none  [the longest x1 152 us: per_device(): lax.psum(part_acc.astype(jnp.bfloat16), 'seq').astype(jnp.float32)]
    all_gather x0 -> x3, blocking collectives: none -> 120 us  [the longest x1 59.4 us: per_device(): lax.all_gather(jnp.concatenate([top[:, None], tot[:, None], acc], axis=-1...]
    pmax x1 -> x0, blocking collectives: 105 us -> none  [per_device(): row_top = lax.pmax(local_max, 'seq')]
    psum x1 -> x0, blocking collectives: 68.8 us -> none  [per_device(): lax.psum(jnp.sum(expo, axis=-1).astype(jnp.bfloat16), 'seq')]
    scatter x2 -> x0, local copies, waits for them, and re-layouts: 57.7 us -> none  [the longest x1 42.2 us: per_device(): back_buffer = jnp.zeros((devices, capacity, BLK, 2 * HD), jnp.bfloat16).a...]
    scatter-add x2 -> x0, other arithmetic: 57.4 us -> none  [the longest x1 46.1 us: per_device(): table_grads = jnp.zeros((per_dev * H, BLK, 2 * HD), jnp.float32).at[wante...]
    unnamed x57 -> x111, local copies, waits for them, and re-layouts: 31.2 us -> 53.9 us
    all_to_all x0 -> x3, starting transfers between devices: none -> 18.8 us  [the longest x1 8.09 us: from_owners(): got = lax.all_to_all(chunks, 'seq', 0, 0, tiled=True)]
  transfers between devices with their start and end apart: 10 -> 10, of which waited for: 3 -> 1; matrix products, arithmetic and copies ran while one was open for 16% -> 40% of each run, Pallas kernels for 0% -> 0%
where the time goes in v1:
time: 672 us; the launch traced here: 660 us
  local copies, waits for them, and re-layouts  281 us (42%)
  blocking collectives  120 us (18%)
  matrix products  95.6 us (14%)
  other arithmetic  88.3 us (13%)
  starting transfers between devices  46.4 us (7%)
  waiting for transfers between devices  17.6 us (3%)
  between operations  11 us (2%)
    all_gather x1, blocking collectives, per_device(): lax.all_gather(jnp.concatenate([top[:, None], tot[:, None], acc], axis=-1...  59.4 us
    unnamed x111, local copies, waits for them, and re-layouts  53.9 us
    all_gather x1, blocking collectives, summed_to_all(): full = lax.all_gather(total, 'seq', axis=0, tiled=True)  35.3 us
    all_gather x1, blocking collectives, from_owners(): full = lax.all_gather(mine, 'seq', axis=0, tiled=False)  25.4 us
    concatenate x1, local copies, waits for them, and re-layouts, sparse_group(): return (result, dquery, jnp.concatenate([dkey, dvalue], axis=-1), stats)  24.8 us
    slice x2, local copies, waits for them, and re-layouts, run_group(): kv_heads[2:group + 2]  18.3 us
    ppermute x2, waiting for transfers between devices, padded_2(): lax.ppermute(lax.slice_in_dim(block, block.shape[dim] - width, None, axis...  17.6 us
    dot_general x1, matrix products, sparse_group(): jnp.einsum('ghqk,ghkd->ghqd', expo.astype(jnp.bfloat16), value_part, pref...  16.4 us
  transfers between devices with their start and end apart: 10, of which 1 were waited for; matrix products, arithmetic and copies ran while one was open for 40% of the time, Pallas kernels for 0%

profile of v1, /device:TPU:19, one launch (start us, length us, event | category | flops | bytes accessed | tf_op | source)
XLA Modules:
  0.0 660.3 jit_solution(17812615895938730329)
XLA Ops:
  4.5 8.8 %all-to-all-start.1 = ((s32[32,1,14]{2,1,0:T(1,128)}), s32[32,1,14]{2,1,0:T(1,128)S(1)}, u32[]{:S(2)}, u32[]{:S(2)}) async-start(s32[32,1,14]{2,1,0:T(1,128)} %bitcast.16), calls=%async_computation.1 | async-start | bytes 32768 | tf_op jit(solution)/shard_map/all_to_all | solution.py:162
  32.2 8.1 %all-to-all-start = ((bf16[32,2,6144]{2,1,0:T(2,128)(2,1)}), bf16[32,2,6144]{2,1,0:T(2,128)(2,1)}, u32[]{:S(2)}, u32[]{:S(2)}) async-start(bf16[32,2,6144]{2,1,0:T(2,128)(2,1)} %copy.314), calls=%async_computation | async-start | bytes 1572864 | tf_op jit(solution)/shard_map/all_to_all | solution.py:35
  66.4 6.5 maximum_bitcast_fusion
  73.7 25.4 %all-gather.1 = bf16[32,2,6144]{2,1,0:T(2,128)(2,1)S(1)} all-gather(bf16[1,2,6144]{2,1,0:T(2,128)(2,1)S(1)} %maximum_bitcast_fusion.2), channel_id=2, replica_groups=mesh['seq'=32,'grp'=4] {'seq'}, dimensions={0}, use_global_device_ids=true | all-gather | bytes 811008 | tf_op jit(solution)/shard_map/all_gather | solution.py:37
  113.5 5.8 all-to-all-start.3
  119.3 8.7 %fusion.97 = (bf16[8,12,64,2,64]{2,0,4,1,3:T(8,128)(2,1)}, bf16[8,12,64,2,64]{2,0,4,1,3:T(8,128)(2,1)}, bf16[8,12,64,2,64]{2,0,4,1,3:T(8,128)(2,1)}) fusion(bf16[10,12,64,2,64]{2,0,4,1,3:T(8,128)(2,1)} %maximum_bitcast_fusion), kind=kLoop, calls=%fused_computation.213 | loop fusion | bytes 9437184 | tf_op jit(solution)/shard_map/while/body/eval_jaxpr/slice | solution.py:185
  128.0 9.4 %copy.312 = bf16[8,12,64,2,64]{4,3,2,1,0:T(2,128)(2,1)} copy(bf16[8,12,64,2,64]{2,0,4,1,3:T(8,128)(2,1)} %get-tuple-element.171) | data formatting | bytes 3145728 | tf_op jit(solution)/shard_map/while/body/eval_jaxpr/slice | solution.py:185
  142.8 13.3 %gather_fusion = bf16[448,64,128]{2,1,0:T(8,128)(2,1)} fusion(bf16[96,64,128]{2,1,0:T(8,128)(2,1)S(1)} %reshape.604, s32[1024]{0:T(1024)S(1)} %pad_clamp_fusion), kind=kCustom, calls=%fused_computation | custom fusion | bytes 14681856 | tf_op jit(solution)/shard_map/gather | solution.py:163
  157.0 7.8 %all-to-all-start.2 = ((bf16[32,14,64,128]{3,2,1,0:T(8,128)(2,1)}), bf16[32,14,64,128]{3,2,1,0:T(8,128)(2,1)}, u32[]{:S(2)}, u32[]{:S(2)}) async-start(bf16[32,14,64,128]{3,2,1,0:T(8,128)(2,1)} %bitcast.237), calls=%async_computation.2 | async-start | bytes 14680064 | tf_op jit(solution)/shard_map/all_to_all | solution.py:164
  182.3 9.6 %copy.313 = bf16[8,12,64,2,64]{4,3,2,1,0:T(2,128)(2,1)} copy(bf16[8,12,64,2,64]{2,0,4,1,3:T(8,128)(2,1)} %get-tuple-element.170) | data formatting | bytes 3145728 | tf_op jit(solution)/shard_map/while/body/eval_jaxpr/slice | solution.py:185
  191.8 6.3 stack.28
  198.1 5.9 copy.311
  204.0 6.4 stack.26
  232.0 59.4 %all_gather.14 = f32[1536,66]{1,0:T(8,128)S(1)} all-gather(f32[48,66]{1,0:T(8,128)S(1)} %pad_maximum_fusion.8), channel_id=1, replica_groups=mesh['seq'=32,'grp'=4] {'seq'}, dimensions={0}, use_global_device_ids=true | all-gather | bytes 418176 | tf_op jit(solution)/shard_map/all_gather | solution.py:265
  306.1 8.0 %gather_fusion.1 = bf16[288,64,128]{2,1,0:T(8,128)(2,1)} fusion(bf16[32,14,64,128]{3,2,1,0:T(8,128)(2,1)} %all-to-all-done.2, s32[288]{0:T(512)S(1)} %fusion.88), kind=kCustom, calls=%fused_computation.1 | custom fusion | bytes 9439488 | tf_op jit(solution)/shard_map/gather | solution.py:165
  314.1 6.0 constant_dynamic-update-slice_fusion.2
  320.1 14.1 %fusion.6 = f32[8,12,512,64]{2,3,1,0:T(8,128)} fusion(bf16[8,12,512,128]{3,2,1,0:T(8,128)(2,1)} %bitcast.19, bf16[8,12,64,64]{2,0,3,1:T(8,128)(2,1)} %bitcast.238), kind=kOutput, calls=%fused_computation.15 | convolution fusion | flops 402653184 | bytes 25952256 | tf_op jit(solution)/shard_map/while/body/eval_jaxpr/ghqd,ghkd->ghqk/dot_general | solution.py:77
  334.2 15.1 %bitcast_reduce_fusion = (f32[8,12,64]{2,1,0:T(8,128)S(1)}, f32[8,12,512,64]{2,3,1,0:T(8,128)}) fusion(f32[8,12,512,64]{2,3,1,0:T(8,128)} %fusion.6, pred[8,12,512]{2,1,0:T(8,128)(4,1)} %copy.307), kind=kOutput, calls=%fused_computation.5 | output fusion | flops 18874880 | bytes 25239552 | tf_op jit(solution)/shard_map/while/body/eval_jaxpr/sub | solution.py:82
  349.3 16.4 %multiply_reduce_fusion = (f32[8,12,64]{2,1,0:T(8,128)}, bf16[8,12,64,64]{2,3,1,0:T(8,128)(2,1)}) fusion(bf16[8,64,12,64]{1,3,2,0:T(8,128)(2,1)S(1)} %copy-done.21, f32[8,12,64]{2,1,0:T(8,128)S(1)} %get-tuple-element.203, bf16[8,12,512,128]{3,2,1,0:T(8,128)(2,1)} %bitcast.19, f32[8,12,512,64]{2,3,1,0:T(8,128)} %get-tuple-element.204), kind=kOutput, calls=%fused_computation.52 | convolution fusion | flops 404613120 | bytes 26787840 | tf_op jit(solution)/shard_map/while/body/eval_jaxpr/ghqk,ghkd->ghqd/dot_general | solution.py:85
  365.7 8.3 %fusion.15 = f32[8,12,512,64]{2,3,1,0:T(8,128)} fusion(f32[8,12,512,64]{2,3,1,0:T(8,128)} %get-tuple-element.204, f32[8,12,64]{2,1,0:T(8,128)S(1)} %get-tuple-element.203, bf16[8,64,12,64]{1,3,2,0:T(8,128)(2,1)S(1)} %copy-done.21), kind=kOutput, calls=%fused_computation.27 | convolution fusion | flops 408944640 | bytes 25976832 | tf_op jit(solution)/shard_map/while/body/eval_jaxpr/ghqk,ghqd->ghkd/dot_general | solution.py:103
  374.0 13.4 %multiply_convert_fusion = bf16[8,12,64,512]{3,2,1,0:T(8,128)(2,1)} fusion(f32[8,12,64]{2,1,0:T(8,128)} %get-tuple-element.207, f32[8,12,64]{2,1,0:T(8,128)} %copy-done.42, f32[8,12,512,64]{2,3,1,0:T(8,128)} %get-tuple-element.204, bf16[8,12,512,128]{3,2,1,0:T(8,128)(2,1)} %bitcast.19, bf16[8,12,64,64]{3,1,2,0:T(8,128)(2,1)} %bitcast.244), kind=kOutput, calls=%fused_computation.7 | convolution fusion | flops 415236096 | bytes 32292864 | tf_op jit(solution)/shard_map/while/body/eval_jaxpr/ghqd,ghkd->ghqk/dot_general | solution.py:94
  394.3 8.7 %pad_maximum_fusion = f32[8,12,512,128]{2,3,1,0:T(8,128)} fusion(f32[8,12,512,64]{2,3,1,0:T(8,128)S(1)} %copy-done.7, f32[8,12,512,64]{2,3,1,0:T(8,128)S(1)} %broadcast_multiply_fusion), kind=kLoop, calls=%fused_computation.3 | loop fusion | flops 6291456 | bytes 50331648 | tf_op jit(solution)/shard_map/while/body/eval_jaxpr/concatenate | solution.py:107
  403.0 24.8 %copy.358 = f32[8,12,512,128]{3,2,1,0:T(8,128)} copy(f32[8,12,512,128]{2,3,1,0:T(8,128)} %pad_maximum_fusion) | data formatting | bytes 50331648 | tf_op jit(solution)/shard_map/while/body/eval_jaxpr/concatenate | solution.py:107
  431.4 7.1 %slice.477 = bf16[8,12,3,64,128]{4,3,2,1,0:T(8,128)(2,1)} slice(f32[8,12,8,64,128]{4,3,2,1,0:T(8,128)} %bitcast.233), slice={[0:8], [0:12], [5:8], [0:64], [0:128]} | slice | bytes 9437184 | tf_op jit(solution)/shard_map/while/body/eval_jaxpr/slice | solution.py:201
  444.9 6.0 reduce.55
  458.1 9.4 %fusion.20 = bf16[32,14,64,128]{3,0,2,1:T(8,128)(2,1)S(1)} fusion(s32[288]{0:T(512)S(1)} %copy-done.31, s32[32,14]{0,1:T(8,128)S(1)} %copy-done.38, bf16[36,8,64,128]{3,2,1,0:T(8,128)(2,1)} %bitcast.245), kind=kOutput, calls=%fused_computation.36 | convolution fusion | flops 2114058240 | bytes 12061568 | tf_op jit(solution)/shard_map/se,ef->sf/dot_general | solution.py:226
  473.3 8.1 %all-to-all-start.5 = ((bf16[32,14,64,128]{3,2,1,0:T(8,128)(2,1)}), bf16[32,14,64,128]{3,2,1,0:T(8,128)(2,1)}, u32[]{:S(2)}, u32[]{:S(2)}) async-start(bf16[32,14,64,128]{3,2,1,0:T(8,128)(2,1)} %copy.368), calls=%async_computation.5 | async-start | bytes 14680064 | tf_op jit(solution)/shard_map/all_to_all | solution.py:232
  511.3 7.8 %fusion.95 = (bf16[10,12,64,128]{3,1,2,0:T(8,128)(2,1)}, f32[10,12,64,128]{3,1,2,0:T(8,128)}) fusion(f32[8,12,64,128]{3,1,2,0:T(8,128)} %bitcast.243, f32[8,12,64,128]{3,1,2,0:T(8,128)} %bitcast.242, f32[8,12,64,128]{3,1,2,0:T(8,128)S(1)} %bitcast.241), kind=kLoop, calls=%fused_computation.211 | loop fusion | flops 2949120 | bytes 15335424 | tf_op jit(solution)/shard_map/convert.9
  524.6 6.6 fusion.30
  546.1 17.6 %collective-permute-done.2 = bf16[1,12,64,128]{3,1,2,0:T(8,128)(2,1)} collective-permute-done((bf16[1,12,64,128]{3,1,2,0:T(8,128)(2,1)S(1)}, bf16[1,12,64,128]{3,1,2,0:T(8,128)(2,1)}, u32[]{:S(2)}, u32[]{:S(2)}) %collective-permute-start.2) | collective-permute-done | bytes 196640 | tf_op jit(solution)/shard_map/ppermute | solution.py:23
  574.5 35.3 %all_gather.15 = bf16[294912]{0:T(1024)(128)(2,1)} all-gather(bf16[9216]{0:T(1024)(128)(2,1)S(1)} %reduce_sum.112), channel_id=1, replica_groups=mesh['seq'=32,'grp'=4] {'seq'}, dimensions={0}, use_global_device_ids=true | all-gather | bytes 608256 | tf_op jit(solution)/shard_map/all_gather | solution.py:46
  627.9 9.1 %fusion.29 = f32[8,12,64,128]{3,1,2,0:T(8,128)S(1)} fusion(f32[8,12,64,128]{3,1,2,0:T(8,128)} %fusion.64, s32[8,12]{1,0:T(8,128)S(1)} %copy-done.34, s32[448]{0:T(512)S(1)} %copy-done.37, bf16[56,8,64,128]{3,2,1,0:T(8,128)(2,1)} %bitcast.94), kind=kOutput, calls=%fused_computation.55 | convolution fusion | flops 705472512 | bytes 13633664 | tf_op jit(solution)/shard_map/sc,sf->cf/dot_general | solution.py:236
  (270 shorter events, 246.1 us)
Async XLA Ops:
  0.6 24.1 %copy-start.12 = (bf16[512,768]{1,0:T(8,128)(2,1)S(1)}, bf16[512,768]{1,0:T(8,128)(2,1)}, u32[]{:S(2)}) copy-start(bf16[512,768]{1,0:T(8,128)(2,1)} %param.23) | copy-start | bytes 2359300
  0.6 21.8 %copy-start.13 = (bf16[512,768]{1,0:T(8,128)(2,1)S(1)}, bf16[512,768]{1,0:T(8,128)(2,1)}, u32[]{:S(2)}) copy-start(bf16[512,768]{1,0:T(8,128)(2,1)} %param.24) | copy-start | bytes 2359300
  0.7 17.2 %copy-start.39 = (s32[2]{0:T(128)S(1)}, s32[2]{0:T(128)}, u32[]{:S(2)}) copy-start(s32[2]{0:T(128)} %param.27) | copy-start | bytes 28
  4.5 27.7 %all-to-all-start.1 = ((s32[32,1,14]{2,1,0:T(1,128)}), s32[32,1,14]{2,1,0:T(1,128)S(1)}, u32[]{:S(2)}, u32[]{:S(2)}) async-start(s32[32,1,14]{2,1,0:T(1,128)} %bitcast.16), calls=%async_computation.1 | async-start | bytes 32768 | tf_op jit(solution)/shard_map/all_to_all | solution.py:162
  16.4 44.1 %collective-permute-start = (bf16[64,1536]{1,0:T(8,128)(2,1)}, bf16[64,1536]{1,0:T(8,128)(2,1)}, u32[]{:S(2)}, u32[]{:S(2)}) collective-permute-start(bf16[64,1536]{1,0:T(8,128)(2,1)} %get-tuple-element.181), channel_id=1, source_target_pairs={{0,4},{4,8},{8,12},{12,16},{16,20},{20,24},{24,28},{28,32},{32,36}... | collective-permute-start | bytes 589832 | tf_op jit(solution)/shard_map/ppermute | solution.py:23
  17.9 36.7 %collective-permute-start.1 = (bf16[64,1536]{1,0:T(8,128)(2,1)}, bf16[64,1536]{1,0:T(8,128)(2,1)}, u32[]{:S(2)}, u32[]{:S(2)}) collective-permute-start(bf16[64,1536]{1,0:T(8,128)(2,1)} %get-tuple-element.182), channel_id=1, source_target_pairs={{4,0},{8,4},{12,8},{16,12},{20,16},{24,20},{28,24},{32,28},{36,32}... | collective-permute-start | bytes 589832 | tf_op jit(solution)/shard_map/ppermute | solution.py:26
  29.3 11.0 %copy-start.40 = (s32[2]{0:T(128)S(1)}, s32[2]{0:T(128)}, u32[]{:S(2)}) copy-start(s32[2]{0:T(128)} %param.27) | copy-start | bytes 28
  32.2 40.7 %all-to-all-start = ((bf16[32,2,6144]{2,1,0:T(2,128)(2,1)}), bf16[32,2,6144]{2,1,0:T(2,128)(2,1)}, u32[]{:S(2)}, u32[]{:S(2)}) async-start(bf16[32,2,6144]{2,1,0:T(2,128)(2,1)} %copy.314), calls=%async_computation | async-start | bytes 1572864 | tf_op jit(solution)/shard_map/all_to_all | solution.py:35
  101.2 8.9 %copy-start.14 = (bf16[2,64,12,64]{1,3,0,2:T(8,128)(2,1)}, bf16[2,64,12,64]{1,3,0,2:T(8,128)(2,1)S(1)}, u32[]{:S(2)}) copy-start(bf16[2,64,12,64]{1,3,0,2:T(8,128)(2,1)S(1)} %copy.373) | copy-start | bytes 589828
  113.5 42.6 %all-to-all-start.3 = ((f32[32,48,66]{2,1,0:T(8,128)}), f32[32,48,66]{2,1,0:T(8,128)S(1)}, u32[]{:S(2)}, u32[]{:S(2)}) async-start(f32[32,48,66]{2,1,0:T(8,128)} %pad_maximum_fusion.1), calls=%async_computation.3 | async-start | bytes 1572864 | tf_op jit(solution)/shard_map/all_to_all | solution.py:260
  156.2 9.2 %copy-start.41 = (s32[2]{0:T(128)S(1)}, s32[2]{0:T(128)}, u32[]{:S(2)}) copy-start(s32[2]{0:T(128)} %param.27) | copy-start | bytes 28
  156.2 9.6 %copy-start.29 = (s32[8,12,3]{1,0,2:T(8,128)S(1)}, s32[8,12,3]{1,0,2:T(8,128)}, u32[]{:S(2)}) copy-start(s32[8,12,3]{1,0,2:T(8,128)} %param.26) | copy-start | bytes 3460
  157.0 149.1 %all-to-all-start.2 = ((bf16[32,14,64,128]{3,2,1,0:T(8,128)(2,1)}), bf16[32,14,64,128]{3,2,1,0:T(8,128)(2,1)}, u32[]{:S(2)}, u32[]{:S(2)}) async-start(bf16[32,14,64,128]{3,2,1,0:T(8,128)(2,1)} %bitcast.237), calls=%async_computation.2 | async-start | bytes 14680064 | tf_op jit(solution)/shard_map/all_to_all | solution.py:164
  168.8 10.8 %copy-start.33 = (s32[288]{0:T(512)S(1)}, s32[288]{0:T(512)}, u32[]{:S(2)}) copy-start(s32[288]{0:T(512)} %copy-done.32) | copy-start | bytes 3460
  168.8 10.8 %copy-start = (bf16[8,12,64,2,64]{4,3,2,1,0:T(2,128)(2,1)S(1)}, bf16[8,12,64,2,64]{4,3,2,1,0:T(2,128)(2,1)}, u32[]{:S(2)}) copy-start(bf16[8,12,64,2,64]{4,3,2,1,0:T(2,128)(2,1)} %copy.312) | copy-start | bytes 4718596
  182.3 15.8 %copy-start.6 = (bf16[8,12,64,2,64]{2,0,4,1,3:T(8,128)(2,1)S(1)}, bf16[8,12,64,2,64]{2,0,4,1,3:T(8,128)(2,1)}, u32[]{:S(2)}) copy-start(bf16[8,12,64,2,64]{2,0,4,1,3:T(8,128)(2,1)} %get-tuple-element.172) | copy-start | bytes 4718596
  204.0 9.4 %copy-start.9 = (bf16[8,12,1,64,128]{4,3,1,0,2:T(8,128)(2,1)S(1)}, bf16[8,12,1,64,128]{4,3,1,0,2:T(8,128)(2,1)}, u32[]{:S(2)}) copy-start(bf16[8,12,1,64,128]{4,3,1,0,2:T(8,128)(2,1)} %stack.27) | copy-start | bytes 4718596
  224.7 77.0 %copy-start.2 = (f32[12,2,64,512]{3,2,1,0:T(8,128)S(1)}, f32[12,2,64,512]{3,2,1,0:T(8,128)}, u32[]{:S(2)}) copy-start(f32[12,2,64,512]{3,2,1,0:T(8,128)} %copy-done.1) | copy-start | bytes 9437188
  224.7 77.0 %copy-start.27 = (bf16[2,64,12,64]{1,3,0,2:T(8,128)(2,1)S(1)}, bf16[2,64,12,64]{1,3,0,2:T(8,128)(2,1)}, u32[]{:S(2)}) copy-start(bf16[2,64,12,64]{1,3,0,2:T(8,128)(2,1)} %copy.375) | copy-start | bytes 589828
  334.2 15.1 %copy-start.21 = (bf16[8,64,12,64]{1,3,2,0:T(8,128)(2,1)S(1)}, bf16[8,64,12,64]{1,3,2,0:T(8,128)(2,1)}, u32[]{:S(2)}) copy-start(bf16[8,64,12,64]{1,3,2,0:T(8,128)(2,1)} %copy.348) | copy-start | bytes 2359300
  349.2 16.4 %copy-start.42 = (f32[8,12,64]{2,1,0:T(8,128)}, f32[8,12,64]{2,1,0:T(8,128)S(1)}, u32[]{:S(2)}) copy-start(f32[8,12,64]{2,1,0:T(8,128)S(1)} %get-tuple-element.203) | copy-start | bytes 73732
  438.9 19.2 %copy-start.31 = (s32[288]{0:T(512)S(1)}, s32[288]{0:T(512)}, u32[]{:S(2)}) copy-start(s32[288]{0:T(512)} %copy-done.30) | copy-start | bytes 3460
  438.9 19.2 %copy-start.38 = (s32[32,14]{0,1:T(8,128)S(1)}, s32[32,14]{0,1:T(8,128)}, u32[]{:S(2)}) copy-start(s32[32,14]{0,1:T(8,128)} %multiply_add_fusion) | copy-start | bytes 5380
  453.2 20.1 %all-to-all-start.4 = ((bf16[32,2,4608]{2,1,0:T(2,128)(2,1)}), bf16[32,2,4608]{2,1,0:T(2,128)(2,1)}, u32[]{:S(2)}, u32[]{:S(2)}) async-start(bf16[32,2,4608]{2,1,0:T(2,128)(2,1)} %reshape.680), calls=%async_computation.4 | async-start | bytes 1179648 | tf_op jit(solution)/shard_map/all_to_all | solution.py:44
  473.3 11.6 %copy-start.28 = (s32[32,14]{1,0:T(8,128)S(1)}, s32[32,14]{1,0:T(8,128)}, u32[]{:S(2)}) copy-start(s32[32,14]{1,0:T(8,128)} %get-tuple-element.161) | copy-start | bytes 5380
  473.3 17.8 %copy-start.15 = (bf16[2,64,12,64]{1,3,0,2:T(8,128)(2,1)S(1)}, bf16[2,64,12,64]{1,3,0,2:T(8,128)(2,1)}, u32[]{:S(2)}) copy-start(bf16[2,64,12,64]{1,3,0,2:T(8,128)(2,1)} %copy-done.14) | copy-start | bytes 589828
  473.3 154.5 %all-to-all-start.5 = ((bf16[32,14,64,128]{3,2,1,0:T(8,128)(2,1)}), bf16[32,14,64,128]{3,2,1,0:T(8,128)(2,1)}, u32[]{:S(2)}, u32[]{:S(2)}) async-start(bf16[32,14,64,128]{3,2,1,0:T(8,128)(2,1)} %copy.368), calls=%async_computation.5 | async-start | bytes 14680064 | tf_op jit(solution)/shard_map/all_to_all | solution.py:232
  507.4 17.2 %slice-start = ((s8[6291456]{0:T(1024)(128)(4,1)}), s8[4194304]{0:T(1024)(128)(4,1)S(1)}, s32[]{:S(2)}) async-start(s8[6291456]{0:T(1024)(128)(4,1)} %bitcast.235), calls=%async_computation.6 | async-start | bytes 8388608
  511.3 11.0 %copy-start.24 = (bf16[1,12,64,64]{2,3,1,0:T(8,128)(2,1)S(1)}, bf16[1,12,64,64]{2,3,1,0:T(8,128)(2,1)}, u32[]{:S(2)}) copy-start(bf16[1,12,64,64]{2,3,1,0:T(8,128)(2,1)} %copy.343) | copy-start | bytes 294916
  511.3 13.4 %slice-start.1 = ((s8[6291456]{0:T(1024)(128)(4,1)}), s8[2097152]{0:T(1024)(128)(4,1)S(1)}, s32[]{:S(2)}) async-start(s8[6291456]{0:T(1024)(128)(4,1)} %bitcast.235), calls=%async_computation.7 | async-start | bytes 4194304
  520.8 42.9 %collective-permute-start.2 = (bf16[1,12,64,128]{3,1,2,0:T(8,128)(2,1)S(1)}, bf16[1,12,64,128]{3,1,2,0:T(8,128)(2,1)}, u32[]{:S(2)}, u32[]{:S(2)}) collective-permute-start(bf16[1,12,64,128]{3,1,2,0:T(8,128)(2,1)S(1)} %get-tuple-element.175), channel_id=1, source_target_pairs={{0,4},{4,8},{8,12},{12,16},{16,20},{20,24},{24,28},{28,32},{32,36}... | collective-permute-start | bytes 589832 | tf_op jit(solution)/shard_map/ppermute | solution.py:23
  522.3 41.4 %collective-permute-start.3 = (bf16[1,12,64,128]{3,1,2,0:T(8,128)(2,1)}, bf16[1,12,64,128]{3,1,2,0:T(8,128)(2,1)}, u32[]{:S(2)}, u32[]{:S(2)}) collective-permute-start(bf16[1,12,64,128]{3,1,2,0:T(8,128)(2,1)} %get-tuple-element.176), channel_id=1, source_target_pairs={{4,0},{8,4},{12,8},{16,12},{20,16},{24,20},{28,24},{32,28},{36,32}... | collective-permute-start | bytes 589832 | tf_op jit(solution)/shard_map/ppermute | solution.py:26
  (24 other events, 109.7 us)

commit v2 on v1

--- a/solution.py
+++ b/solution.py
@@ -3,6 +3,7 @@
 import jax
 import jax.numpy as jnp
 from jax import lax
+from jax.experimental import pallas as pl
 from jax.sharding import PartitionSpec as P
 
 H = 12
@@ -105,6 +106,59 @@
     )
     stats = jnp.stack([row_max[..., 0], totals[..., 0], dotted[..., 0]], axis=1)
     return (result, dquery, jnp.concatenate([dkey, dvalue], axis=-1), stats)
+
+
+def sparse_kernel(q_ref, g_ref, kv_ref, allow_ref, out_ref, dq_ref, terms_ref, *, factor):
+    query = q_ref[0, 0]
+    grad = g_ref[0, 0]
+    keyval = kv_ref[0, 0]
+    key = keyval[:, :HD]
+    value = keyval[:, HD:]
+    nt = (((1,), (1,)), ((), ()))
+    scores = lax.dot_general(query, key, nt, preferred_element_type=jnp.float32) * factor
+    mask = allow_ref[0, 0] > 0.5
+    row_max = jnp.max(jnp.where(mask, scores, -1e30), axis=-1, keepdims=True)
+    expo = jnp.where(mask, jnp.exp(scores - row_max), 0.0)
+    totals = jnp.sum(expo, axis=-1, keepdims=True)
+    result = jnp.dot(expo.astype(jnp.bfloat16), value, preferred_element_type=jnp.float32) / totals
+    probs = expo / totals
+    dprobs = lax.dot_general(grad, value, nt, preferred_element_type=jnp.float32)
+    dotted = jnp.sum(grad.astype(jnp.float32) * result, axis=-1, keepdims=True)
+    dscore = probs * (dprobs - dotted)
+    dq = factor * jnp.dot(dscore.astype(jnp.bfloat16), key, preferred_element_type=jnp.float32)
+    dkey = factor * jnp.dot(dscore.T.astype(jnp.bfloat16), query, preferred_element_type=jnp.float32)
+    dvalue = jnp.dot(probs.T.astype(jnp.bfloat16), grad, preferred_element_type=jnp.float32)
+    out_ref[0, 0] = result
+    dq_ref[0, 0] = dq
+    terms_ref[0, 0, :, :HD] = dkey
+    terms_ref[0, 0, :, HD:] = dvalue
+
+
+def sparse_call(query_h, grad_h, keyvals, allowed_f, factor, interpret=False):
+    blocks, heads, rows, _ = query_h.shape
+    keys_n = keyvals.shape[2]
+    small = pl.BlockSpec((1, 1, rows, HD), lambda i, h: (i, h, 0, 0))
+    return pl.pallas_call(
+        lambda *refs: sparse_kernel(*refs, factor=factor),
+        grid=(blocks, heads),
+        in_specs=[
+            small,
+            small,
+            pl.BlockSpec((1, 1, keys_n, 2 * HD), lambda i, h: (i, h, 0, 0)),
+            pl.BlockSpec((1, 1, 1, keys_n), lambda i, h: (i, h, 0, 0)),
+        ],
+        out_specs=[
+            small,
+            small,
+            pl.BlockSpec((1, 1, keys_n, 2 * HD), lambda i, h: (i, h, 0, 0)),
+        ],
+        out_shape=[
+            jax.ShapeDtypeStruct((blocks, heads, rows, HD), jnp.float32),
+            jax.ShapeDtypeStruct((blocks, heads, rows, HD), jnp.float32),
+            jax.ShapeDtypeStruct((blocks, heads, keys_n, 2 * HD), jnp.float32),
+        ],
+        interpret=interpret,
+    )(query_h, grad_h, keyvals, allowed_f)
 
 
 def per_device(queries, keys, values, out_grad, random_blocks, global_blocks):
@@ -149,10 +203,7 @@
                 axis=1,
             )
         )
-    grows = from_owners(jnp.stack(global_rows), global_blocks // per_dev)
-    g_query = grows[:, :, :width].reshape(NG, BLK, H, HD)
-    g_grad = grows[:, :, 3 * width :].reshape(NG, BLK, H, HD)
-    g_kv = pair_heads(grows[:, :, width : 3 * width], NG)
+    stacked_rows = jnp.stack(global_rows)
     owners, slot_ids, req_codes = slot_plan(random_blocks, per_dev, devices, head_ids)
     slot_key = owners * capacity + slot_ids
     slot_hit = jnp.arange(devices * capacity, dtype=jnp.int32)[:, None] == slot_key[None, :]
@@ -161,6 +212,11 @@
     ).reshape(devices, capacity)
     wanted = lax.all_to_all(outgoing, "seq", split_axis=0, concat_axis=0, tiled=True)
     sending = kv_local.reshape(per_dev * H, BLK, 2 * HD)[jnp.maximum(wanted, 0)]
+    sending, stacked_rows = lax.optimization_barrier((sending, stacked_rows))
+    grows = from_owners(stacked_rows, global_blocks // per_dev)
+    g_query = grows[:, :, :width].reshape(NG, BLK, H, HD)
+    g_grad = grows[:, :, 3 * width :].reshape(NG, BLK, H, HD)
+    g_kv = pair_heads(grows[:, :, width : 3 * width], NG)
     fetched = lax.all_to_all(sending, "seq", split_axis=0, concat_axis=0, tiled=True)
     rand_kv = fetched[owners, slot_ids].reshape(per_dev, H, R, BLK, 2 * HD)
     shifts = jnp.arange(-1, 2, dtype=jnp.int32)
@@ -187,8 +243,8 @@
         keyvals = jnp.concatenate([win_slots, glob_slots, rand_kv], axis=2).reshape(
             group, H, SLOTS * BLK, 2 * HD
         )
-        result, dquery, terms, stats = sparse_group(
-            query_heads, grad_heads, keyvals, allowed, factor
+        result, dquery, terms = sparse_call(
+            query_heads, grad_heads, keyvals, allowed.astype(jnp.float32)[:, :, None, :], factor
         )
         terms = terms.reshape(group, H, SLOTS, BLK, 2 * HD)
         spacing = ((0, 0), (0, 0), (0, 0), (0, 0))
@@ -199,9 +255,12 @@
         )
         global_sum = jnp.sum(terms[:, :, 3 : 3 + NG], axis=0)
         random_out = terms[:, :, 3 + NG :].astype(jnp.bfloat16)
-        return (result, dquery, window_sum, global_sum, random_out, stats)
-
-    mapped = lax.map(run_group, jnp.arange(groups, dtype=jnp.int32))
+        return (result, dquery, window_sum, global_sum, random_out)
+
+    if groups == 1:
+        mapped = tuple(part[None] for part in run_group(0))
+    else:
+        mapped = lax.map(run_group, jnp.arange(groups, dtype=jnp.int32))
     result = mapped[0].reshape(per_dev, H, BLK, HD)
     dquery = mapped[1].reshape(per_dev, H, BLK, HD)
     place = (
@@ -218,7 +277,6 @@
         )
     global_part = jnp.sum(mapped[3], axis=0).transpose(1, 0, 2, 3)
     random_out = mapped[4].reshape(-1, BLK, 2 * HD)
-    stats = mapped[5].reshape(per_dev, 3, H, BLK)
     own_grads = padded_grads[1 : per_dev + 1]
     edge_pair = jnp.stack([padded_grads[0], padded_grads[per_dev + 1]])
     near_grads = padded_2(edge_pair.astype(jnp.bfloat16), (("seq", 0),), 1).astype(edge_pair.dtype)

time: 672 us -> 643 us (0.957)
  Pallas kernels: 0 us -> 91.7 us
  local copies, waits for them, and re-layouts: 281 us -> 204 us
  matrix products: 95.6 us -> 26.4 us
  other arithmetic: 88.3 us -> 52 us
  waiting for transfers between devices: 17.6 us -> 49.5 us
  blocking collectives: 120 us -> 147 us
  starting transfers between devices: 46.4 us -> 53.7 us
    pallas_call x0 -> x1, Pallas kernels: none -> 91.7 us  [sparse_call(): pl.pallas_call(lambda *refs: sparse_kernel(*refs, factor=factor), grid=(b...]
    dot_general x6 -> x0, matrix products: 64 us -> none  [the longest x1 16.4 us: sparse_group(): jnp.einsum('ghqk,ghkd->ghqd', expo.astype(jnp.bfloat16), value_part, pref...]
    ppermute x2, waiting for transfers between devices: 0.01 us -> 37.9 us  [padded_2(): lax.ppermute(lax.slice_in_dim(block, 0, width, axis=dim), axis, backward)]
    concatenate x1 -> x0, local copies, waits for them, and re-layouts: 24.8 us -> none  [sparse_group(): return (result, dquery, jnp.concatenate([dkey, dvalue], axis=-1), stats)]
    unnamed x111 -> x101, local copies, waits for them, and re-layouts: 53.9 us -> 30.5 us
    all_to_all x0 -> x1, blocking collectives: none -> 18.2 us  [per_device(): got = lax.all_to_all(packed, 'seq', 0, 0, tiled=True)]
    sub x1 -> x0, other arithmetic: 15.1 us -> none  [sparse_group(): expo = jnp.where(mask, jnp.exp(scores - row_max), 0.0)]
    ppermute x2, waiting for transfers between devices: 17.6 us -> 4.02 us  [padded_2(): lax.ppermute(lax.slice_in_dim(block, block.shape[dim] - width, None, axis...]
  transfers between devices with their start and end apart: 10 -> 9, of which waited for: 1 -> 3; matrix products, arithmetic and copies ran while one was open for 40% -> 25% of each run, Pallas kernels for 0% -> 0%
where the time goes in v2:
time: 643 us; the launch traced here: 635 us
  local copies, waits for them, and re-layouts  204 us (32%)
  blocking collectives  147 us (23%)
  Pallas kernels  91.7 us (14%)
  starting transfers between devices  53.7 us (8%)
  other arithmetic  52 us (8%)
  waiting for transfers between devices  49.5 us (8%)
  matrix products  26.4 us (4%)
  between operations  10.9 us (2%)
    pallas_call x1, Pallas kernels, sparse_call(): pl.pallas_call(lambda *refs: sparse_kernel(*refs, factor=factor), grid=(b...  91.7 us
    all_gather x1, blocking collectives, per_device(): lax.all_gather(jnp.concatenate([top[:, None], tot[:, None], acc], axis=-1...  66.6 us
    all_gather x1, blocking collectives, summed_to_all(): full = lax.all_gather(total, 'seq', axis=0, tiled=True)  38.2 us
    ppermute x2, waiting for transfers between devices, padded_2(): lax.ppermute(lax.slice_in_dim(block, 0, width, axis=dim), axis, backward)  37.9 us
    unnamed x101, local copies, waits for them, and re-layouts  30.5 us
    all_gather x1, blocking collectives, from_owners(): full = lax.all_gather(mine, 'seq', axis=0, tiled=False)  23.6 us
    all_to_all x1, blocking collectives, per_device(): got = lax.all_to_all(packed, 'seq', 0, 0, tiled=True)  18.2 us
    another operation x3, local copies, waits for them, and re-layouts, run_group(): jnp.stack([kv_heads[0:group], kv_heads[1:group + 1], kv_heads[2:group + 2...  15.4 us
  transfers between devices with their start and end apart: 9, of which 3 were waited for; matrix products, arithmetic and copies ran while one was open for 25% of the time, Pallas kernels for 0%

profile of v2, /device:TPU:19, one launch (start us, length us, event | category | flops | bytes accessed | tf_op | source)
XLA Modules:
  0.0 634.9 jit_solution(10108557204409639296)
XLA Ops:
  9.0 11.1 %all-to-all-start = ((s32[32,1,14]{2,1,0:T(1,128)}), s32[32,1,14]{2,1,0:T(1,128)S(1)}, u32[]{:S(2)}, u32[]{:S(2)}) async-start(s32[32,1,14]{2,1,0:T(1,128)} %bitcast.7), calls=%async_computation | async-start | bytes 32768 | tf_op jit(solution)/shard_map/all_to_all | solution.py:213
  47.8 5.2 maximum_bitcast_fusion
  56.4 6.1 copy.258
  62.5 5.3 reshape.599
  67.9 13.6 %gather_fusion = bf16[448,64,128]{2,1,0:T(8,128)(2,1)} fusion(bf16[96,64,128]{2,1,0:T(8,128)(2,1)S(1)} %reshape.599, s32[1024]{0:T(1024)S(1)} %pad_clamp_fusion), kind=kCustom, calls=%fused_computation | custom fusion | bytes 14681856 | tf_op jit(solution)/shard_map/gather | solution.py:214
  83.4 7.4 %all-to-all-start.1 = ((bf16[32,2,6144]{2,1,0:T(2,128)(2,1)}), bf16[32,2,6144]{2,1,0:T(2,128)(2,1)S(1)}, u32[]{:S(2)}, u32[]{:S(2)}) async-start(bf16[32,2,6144]{2,1,0:T(2,128)(2,1)} %copy.266), calls=%async_computation.1 | async-start | bytes 1572864 | tf_op jit(solution)/shard_map/all_to_all | solution.py:36
  96.0 7.6 %all-to-all-done.1 = bf16[32,2,6144]{2,1,0:T(2,128)(2,1)S(1)} async-done(((bf16[32,2,6144]{2,1,0:T(2,128)(2,1)}), bf16[32,2,6144]{2,1,0:T(2,128)(2,1)S(1)}, u32[]{:S(2)}, u32[]{:S(2)}) %all-to-all-start.1) | async-done | bytes 786464 | tf_op jit(solution)/shard_map/all_to_all | solution.py:36
  103.7 23.6 %all-gather.1 = bf16[32,2,6144]{2,1,0:T(2,128)(2,1)S(1)} all-gather(bf16[1,2,6144]{2,1,0:T(2,128)(2,1)S(1)} %maximum_bitcast_fusion.3), channel_id=2, replica_groups=mesh['seq'=32,'grp'=4] {'seq'}, dimensions={0}, use_global_device_ids=true | all-gather | bytes 811008 | tf_op jit(solution)/shard_map/all_gather | solution.py:38
  135.2 18.2 %all_to_all.32 = f32[32,48,66]{2,1,0:T(8,128)} all-to-all(f32[32,48,66]{2,1,0:T(8,128)S(1)} %pad_maximum_fusion.1), channel_id=1, replica_groups=mesh['seq'=32,'grp'=4] {'seq'}, dimensions={0} | all-to-all | bytes 811008 | tf_op jit(solution)/shard_map/all_to_all | solution.py:318
  153.4 6.8 %all-to-all-start.2 = ((bf16[32,14,64,128]{3,2,1,0:T(8,128)(2,1)}), bf16[32,14,64,128]{3,2,1,0:T(8,128)(2,1)}, u32[]{:S(2)}, u32[]{:S(2)}) async-start(bf16[32,14,64,128]{3,2,1,0:T(8,128)(2,1)} %bitcast.212), calls=%async_computation.2 | async-start | bytes 14680064 | tf_op jit(solution)/shard_map/all_to_all | solution.py:220
  167.6 4.9 copy_bitcast_fusion
  175.0 9.5 %copy.257 = bf16[8,12,64,2,64]{4,3,2,1,0:T(2,128)(2,1)} copy(bf16[8,12,64,2,64]{2,0,4,1,3:T(8,128)(2,1)} %get-tuple-element.146) | data formatting | bytes 3145728 | tf_op jit(solution)/shard_map/slice | solution.py:241
  184.5 6.4 %stack.23 = bf16[8,12,1,64,128]{4,3,1,0,2:T(8,128)(2,1)} reshape(bf16[8,12,64,2,64]{4,3,2,1,0:T(2,128)(2,1)} %copy.257) | data formatting | bytes 3145728 | tf_op jit(solution)/shard_map/stack | solution.py:240
  190.9 6.0 copy.259
  197.0 6.4 %stack.25 = bf16[8,12,1,64,128]{4,3,1,0,2:T(8,128)(2,1)} reshape(bf16[8,12,64,2,64]{4,3,2,1,0:T(2,128)(2,1)} %copy.259) | data formatting | bytes 3145728 | tf_op jit(solution)/shard_map/stack | solution.py:240
  220.1 66.6 %all_gather.14 = f32[1536,66]{1,0:T(8,128)S(1)} all-gather(f32[48,66]{1,0:T(8,128)S(1)} %pad_maximum_fusion.6), channel_id=1, replica_groups=mesh['seq'=32,'grp'=4] {'seq'}, dimensions={0}, use_global_device_ids=true | all-gather | bytes 418176 | tf_op jit(solution)/shard_map/all_gather | solution.py:323
  302.4 8.0 %gather_fusion.1 = bf16[288,64,128]{2,1,0:T(8,128)(2,1)} fusion(bf16[32,14,64,128]{3,2,1,0:T(8,128)(2,1)} %all-to-all-done.2, s32[288]{0:T(512)S(1)} %fusion.56), kind=kCustom, calls=%fused_computation.1 | custom fusion | bytes 9439488 | tf_op jit(solution)/shard_map/gather | solution.py:221
  310.3 6.0 constant_dynamic-update-slice_fusion.2
  316.4 91.7 %shard_map.93 = (f32[8,12,64,64]{3,2,1,0:T(8,128)}, f32[8,12,64,64]{3,2,1,0:T(8,128)}, f32[8,12,512,128]{3,2,1,0:T(8,128)}) custom-call(bf16[8,12,64,64]{3,2,1,0:T(8,128)(2,1)} %get-tuple-element.178.refs_0_, bf16[8,12,64,64]{3,2,1,0:T(8,128)(2,1)} %get-tuple-element.177.refs_1_, bf16[8,12,512,128]{3,2,1,0:T(8,128)(2,1)} %bitcast.23.refs_2_, ...), custom_call_target="tpu_custom_call" | custom-call | tf_op jit(solution)/shard_map/pallas_call | solution.py:141
  411.6 7.2 %slice.457 = bf16[8,12,3,64,128]{4,3,2,1,0:T(8,128)(2,1)} slice(f32[8,12,8,64,128]{4,3,2,1,0:T(8,128)} %bitcast.215), slice={[0:8], [0:12], [5:8], [0:64], [0:128]} | slice | bytes 9437184 | tf_op jit(solution)/shard_map/slice | solution.py:257
  420.1 4.6 convert_element_type.112
  425.2 6.0 reduce.54
  433.6 5.3 all-to-all-start.4
  438.9 9.4 %fusion.2 = bf16[32,14,64,128]{3,0,2,1:T(8,128)(2,1)S(1)} fusion(s32[288]{0:T(512)S(1)} %copy-done.31, s32[32,14]{0,1:T(8,128)S(1)} %copy-done.37, bf16[36,8,64,128]{3,2,1,0:T(8,128)(2,1)} %bitcast.217), kind=kOutput, calls=%fused_computation.11 | convolution fusion | flops 2114058240 | bytes 12061568 | tf_op jit(solution)/shard_map/se,ef->sf/dot_general | solution.py:284
  448.3 5.8 copy.299
  454.1 7.6 %all-to-all-start.5 = ((bf16[32,14,64,128]{3,2,1,0:T(8,128)(2,1)}), bf16[32,14,64,128]{3,2,1,0:T(8,128)(2,1)}, u32[]{:S(2)}, u32[]{:S(2)}) async-start(bf16[32,14,64,128]{3,2,1,0:T(8,128)(2,1)} %copy.299), calls=%async_computation.5 | async-start | bytes 14680064 | tf_op jit(solution)/shard_map/all_to_all | solution.py:290
  472.3 4.8 slice_bitcast_fusion.4
  480.7 12.9 %collective-permute-start.2 = (bf16[1,12,64,128]{3,2,1,0:T(8,128)(2,1)S(1)}, bf16[1,12,64,128]{3,2,1,0:T(8,128)(2,1)}, u32[]{:S(2)}, u32[]{:S(2)}) collective-permute-start(bf16[1,12,64,128]{3,2,1,0:T(8,128)(2,1)S(1)} %get-tuple-element.149), channel_id=1, source_target_pairs={{0,4},{4,8},{8,12},{12,16},{16,20},{20,24},{24,28},{28,32},{32,36}... | collective-permute-start | bytes 589832 | tf_op jit(solution)/shard_map/ppermute | solution.py:24
  500.6 37.9 %collective-permute-done.3 = bf16[1,12,64,128]{3,2,1,0:T(8,128)(2,1)} collective-permute-done((bf16[1,12,64,128]{3,2,1,0:T(8,128)(2,1)S(1)}, bf16[1,12,64,128]{3,2,1,0:T(8,128)(2,1)}, u32[]{:S(2)}, u32[]{:S(2)}) %collective-permute-start.3) | collective-permute-done | bytes 196640 | tf_op jit(solution)/shard_map/ppermute | solution.py:27
  544.7 4.7 reshape.677
  551.6 38.2 %all_gather.15 = bf16[294912]{0:T(1024)(128)(2,1)} all-gather(bf16[9216]{0:T(1024)(128)(2,1)S(1)} %reduce_sum.89), channel_id=1, replica_groups=mesh['seq'=32,'grp'=4] {'seq'}, dimensions={0}, use_global_device_ids=true | all-gather | bytes 608256 | tf_op jit(solution)/shard_map/all_gather | solution.py:47
  606.2 6.7 %fusion = f32[8,12,64,128]{3,1,2,0:T(8,128)S(1)} fusion(s32[8,12]{1,0:T(8,128)S(1)} %copy-done.40, s32[448]{0:T(512)S(1)} %copy-done.41, bf16[56,8,64,128]{3,2,1,0:T(8,128)(2,1)} %bitcast.98), kind=kOutput, calls=%fused_computation.5 | convolution fusion | flops 704686080 | bytes 10487936 | tf_op jit(solution)/shard_map/sc,sf->cf/dot_general | solution.py:294
  (246 shorter events, 162.7 us)
Async XLA Ops:
  0.6 19.4 %copy-start.38 = (s32[2]{0:T(128)S(1)}, s32[2]{0:T(128)}, u32[]{:S(2)}) copy-start(s32[2]{0:T(128)} %param.27) | copy-start | bytes 28
  3.8 33.2 %collective-permute-start.1 = (bf16[64,1536]{1,0:T(8,128)(2,1)}, bf16[64,1536]{1,0:T(8,128)(2,1)}, u32[]{:S(2)}, u32[]{:S(2)}) collective-permute-start(bf16[64,1536]{1,0:T(8,128)(2,1)} %get-tuple-element.152), channel_id=1, source_target_pairs={{4,0},{8,4},{12,8},{16,12},{20,16},{24,20},{28,24},{32,28},{36,32}... | collective-permute-start | bytes 589832 | tf_op jit(solution)/shard_map/ppermute | solution.py:27
  4.4 38.4 %collective-permute-start = (bf16[64,1536]{1,0:T(8,128)(2,1)S(1)}, bf16[64,1536]{1,0:T(8,128)(2,1)S(1)}, u32[]{:S(2)}, u32[]{:S(2)}) collective-permute-start(bf16[64,1536]{1,0:T(8,128)(2,1)S(1)} %get-tuple-element.151), channel_id=1, source_target_pairs={{0,4},{4,8},{8,12},{12,16},{16,20},{20,24},{24,28},{28,32},{32,36}... | collective-permute-start | bytes 589832 | tf_op jit(solution)/shard_map/ppermute | solution.py:24
  6.1 22.6 %copy-start.24 = (s32[8,12,3]{2,1,0:T(8,128)}, s32[8,12,3]{2,1,0:T(8,128)S(1)}, u32[]{:S(2)}) copy-start(s32[8,12,3]{2,1,0:T(8,128)S(1)} %copy.261) | copy-start | bytes 3460
  7.6 21.1 %copy-start.32 = (s32[288]{0:T(512)}, s32[288]{0:T(512)S(1)}, u32[]{:S(2)}) copy-start(s32[288]{0:T(512)S(1)} %fusion.45) | copy-start | bytes 3460
  7.6 21.1 %copy-start.30 = (s32[288]{0:T(512)}, s32[288]{0:T(512)S(1)}, u32[]{:S(2)}) copy-start(s32[288]{0:T(512)S(1)} %multiply_add_fusion.2) | copy-start | bytes 3460
  9.0 25.3 %all-to-all-start = ((s32[32,1,14]{2,1,0:T(1,128)}), s32[32,1,14]{2,1,0:T(1,128)S(1)}, u32[]{:S(2)}, u32[]{:S(2)}) async-start(s32[32,1,14]{2,1,0:T(1,128)} %bitcast.7), calls=%async_computation | async-start | bytes 32768 | tf_op jit(solution)/shard_map/all_to_all | solution.py:213
  67.8 13.6 %copy-start.18 = (bf16[2,64,3072]{2,1,0:T(8,128)(2,1)S(1)}, bf16[2,64,3072]{2,1,0:T(8,128)(2,1)}, u32[]{:S(2)}) copy-start(bf16[2,64,3072]{2,1,0:T(8,128)(2,1)} %pad_maximum_fusion) | copy-start | bytes 2359300
  81.4 9.4 %copy-start.39 = (s32[2]{0:T(128)S(1)}, s32[2]{0:T(128)}, u32[]{:S(2)}) copy-start(s32[2]{0:T(128)} %param.27) | copy-start | bytes 28
  81.4 12.6 %copy-start.13 = (bf16[512,768]{1,0:T(8,128)(2,1)S(1)}, bf16[512,768]{1,0:T(8,128)(2,1)}, u32[]{:S(2)}) copy-start(bf16[512,768]{1,0:T(8,128)(2,1)} %param.24) | copy-start | bytes 2359300
  81.5 12.9 %copy-start.14 = (bf16[512,768]{1,0:T(8,128)(2,1)S(1)}, bf16[512,768]{1,0:T(8,128)(2,1)}, u32[]{:S(2)}) copy-start(bf16[512,768]{1,0:T(8,128)(2,1)} %param.23) | copy-start | bytes 2359300
  83.4 20.1 %all-to-all-start.1 = ((bf16[32,2,6144]{2,1,0:T(2,128)(2,1)}), bf16[32,2,6144]{2,1,0:T(2,128)(2,1)S(1)}, u32[]{:S(2)}, u32[]{:S(2)}) async-start(bf16[32,2,6144]{2,1,0:T(2,128)(2,1)} %copy.266), calls=%async_computation.1 | async-start | bytes 1572864 | tf_op jit(solution)/shard_map/all_to_all | solution.py:36
  94.4 37.3 %copy-start.19 = (bf16[512,768]{0,1:T(8,128)(2,1)}, bf16[512,768]{0,1:T(8,128)(2,1)S(1)}, u32[]{:S(2)}) copy-start(bf16[512,768]{0,1:T(8,128)(2,1)S(1)} %copy.279) | copy-start | bytes 2359300
  94.7 34.6 %copy-start.15 = (bf16[512,768]{0,1:T(8,128)(2,1)}, bf16[512,768]{0,1:T(8,128)(2,1)S(1)}, u32[]{:S(2)}) copy-start(bf16[512,768]{0,1:T(8,128)(2,1)S(1)} %copy.275) | copy-start | bytes 2359300
  153.4 6.8 %copy-start.22 = (bf16[512,768]{1,0:T(8,128)(2,1)S(1)}, bf16[512,768]{1,0:T(8,128)(2,1)}, u32[]{:S(2)}) copy-start(bf16[512,768]{1,0:T(8,128)(2,1)} %param.22) | copy-start | bytes 2359300
  153.4 9.1 %copy-start.25 = (s32[8,12,3]{2,1,0:T(8,128)S(1)}, s32[8,12,3]{2,1,0:T(8,128)}, u32[]{:S(2)}) copy-start(s32[8,12,3]{2,1,0:T(8,128)} %copy-done.24) | copy-start | bytes 3460
  153.4 148.9 %all-to-all-start.2 = ((bf16[32,14,64,128]{3,2,1,0:T(8,128)(2,1)}), bf16[32,14,64,128]{3,2,1,0:T(8,128)(2,1)}, u32[]{:S(2)}, u32[]{:S(2)}) async-start(bf16[32,14,64,128]{3,2,1,0:T(8,128)(2,1)} %bitcast.212), calls=%async_computation.2 | async-start | bytes 14680064 | tf_op jit(solution)/shard_map/all_to_all | solution.py:220
  184.5 6.4 %copy-start.5 = (bf16[8,12,64,2,64]{2,0,4,1,3:T(8,128)(2,1)S(1)}, bf16[8,12,64,2,64]{2,0,4,1,3:T(8,128)(2,1)}, u32[]{:S(2)}) copy-start(bf16[8,12,64,2,64]{2,0,4,1,3:T(8,128)(2,1)} %get-tuple-element.144) | copy-start | bytes 4718596
  197.0 6.4 %copy-start.8 = (bf16[8,12,1,64,128]{4,3,1,0,2:T(8,128)(2,1)S(1)}, bf16[8,12,1,64,128]{4,3,1,0,2:T(8,128)(2,1)}, u32[]{:S(2)}) copy-start(bf16[8,12,1,64,128]{4,3,1,0,2:T(8,128)(2,1)} %stack.23) | copy-start | bytes 4718596
  197.0 8.2 %copy-start.7 = (bf16[8,12,1,64,128]{4,3,1,0,2:T(8,128)(2,1)S(1)}, bf16[8,12,1,64,128]{4,3,1,0,2:T(8,128)(2,1)}, u32[]{:S(2)}) copy-start(bf16[8,12,1,64,128]{4,3,1,0,2:T(8,128)(2,1)} %stack.24) | copy-start | bytes 4718596
  217.4 70.5 %copy-start.12 = (bf16[2,64,12,64]{3,2,1,0:T(8,128)(2,1)S(1)}, bf16[2,64,12,64]{3,2,1,0:T(8,128)(2,1)}, u32[]{:S(2)}) copy-start(bf16[2,64,12,64]{3,2,1,0:T(8,128)(2,1)} %copy-done.11) | copy-start | bytes 589828
  217.4 80.1 %copy-start.2 = (f32[12,2,64,512]{3,2,1,0:T(8,128)S(1)}, f32[12,2,64,512]{3,2,1,0:T(8,128)}, u32[]{:S(2)}) copy-start(f32[12,2,64,512]{3,2,1,0:T(8,128)} %copy-done.1) | copy-start | bytes 9437188
  411.6 7.2 %copy-start.27 = (bf16[2,12,64,64]{3,2,0,1:T(8,128)(2,1)S(1)}, bf16[2,12,64,64]{3,2,0,1:T(8,128)(2,1)}, u32[]{:S(2)}) copy-start(bf16[2,12,64,64]{3,2,0,1:T(8,128)(2,1)} %fusion.23) | copy-start | bytes 589828
  420.1 18.7 %copy-start.31 = (s32[288]{0:T(512)S(1)}, s32[288]{0:T(512)}, u32[]{:S(2)}) copy-start(s32[288]{0:T(512)} %copy-done.30) | copy-start | bytes 3460
  420.1 18.7 %copy-start.37 = (s32[32,14]{0,1:T(8,128)S(1)}, s32[32,14]{0,1:T(8,128)}, u32[]{:S(2)}) copy-start(s32[32,14]{0,1:T(8,128)} %multiply_add_fusion) | copy-start | bytes 5380
  433.6 20.6 %all-to-all-start.4 = ((bf16[32,2,4608]{2,1,0:T(2,128)(2,1)}), bf16[32,2,4608]{2,1,0:T(2,128)(2,1)}, u32[]{:S(2)}, u32[]{:S(2)}) async-start(bf16[32,2,4608]{2,1,0:T(2,128)(2,1)} %reshape.676), calls=%async_computation.4 | async-start | bytes 1179648 | tf_op jit(solution)/shard_map/all_to_all | solution.py:45
  454.1 9.6 %copy-start.42 = (s32[4]{0:T(128)S(1)}, s32[4]{0:T(128)}, u32[]{:S(2)}) copy-start(s32[4]{0:T(128)} %constant.301.clone.1) | copy-start | bytes 52
  454.1 152.1 %all-to-all-start.5 = ((bf16[32,14,64,128]{3,2,1,0:T(8,128)(2,1)}), bf16[32,14,64,128]{3,2,1,0:T(8,128)(2,1)}, u32[]{:S(2)}, u32[]{:S(2)}) async-start(bf16[32,14,64,128]{3,2,1,0:T(8,128)(2,1)} %copy.299), calls=%async_computation.5 | async-start | bytes 14680064 | tf_op jit(solution)/shard_map/all_to_all | solution.py:290
  461.7 8.6 %copy-start.34 = (f32[2,12,64]{2,0,1:T(2,128)S(1)}, f32[2,12,64]{2,0,1:T(2,128)}, u32[]{:S(2)}) copy-start(f32[2,12,64]{2,0,1:T(2,128)} %copy.287) | copy-start | bytes 18436
  477.1 16.5 %copy-start.10 = (f32[8,12,64,64]{3,2,1,0:T(8,128)S(1)}, f32[8,12,64,64]{3,2,1,0:T(8,128)}, u32[]{:S(2)}) copy-start(f32[8,12,64,64]{3,2,1,0:T(8,128)} %get-tuple-element.107) | copy-start | bytes 4718596
  480.2 58.3 %collective-permute-start.3 = (bf16[1,12,64,128]{3,2,1,0:T(8,128)(2,1)S(1)}, bf16[1,12,64,128]{3,2,1,0:T(8,128)(2,1)}, u32[]{:S(2)}, u32[]{:S(2)}) collective-permute-start(bf16[1,12,64,128]{3,2,1,0:T(8,128)(2,1)S(1)} %get-tuple-element.150), channel_id=1, source_target_pairs={{4,0},{8,4},{12,8},{16,12},{20,16},{24,20},{28,24},{32,28},{36,32}... | collective-permute-start | bytes 589832 | tf_op jit(solution)/shard_map/ppermute | solution.py:27
  480.7 61.9 %collective-permute-start.2 = (bf16[1,12,64,128]{3,2,1,0:T(8,128)(2,1)S(1)}, bf16[1,12,64,128]{3,2,1,0:T(8,128)(2,1)}, u32[]{:S(2)}, u32[]{:S(2)}) collective-permute-start(bf16[1,12,64,128]{3,2,1,0:T(8,128)(2,1)S(1)} %get-tuple-element.149), channel_id=1, source_target_pairs={{0,4},{4,8},{8,12},{12,16},{16,20},{20,24},{24,28},{28,32},{32,36}... | collective-permute-start | bytes 589832 | tf_op jit(solution)/shard_map/ppermute | solution.py:24
  (21 other events, 77.3 us)

commit v3 on v2

--- a/solution.py
+++ b/solution.py
@@ -29,14 +29,17 @@
     return block
 
 
-def from_owners(value, owners):
+def from_owners(value, owners, extra):
     devices = lax.axis_size("seq")
     count = value.shape[0]
-    chunks = value.reshape(count, devices, -1).transpose(1, 0, 2)
-    got = lax.all_to_all(chunks, "seq", 0, 0, tiled=True)
-    mine = jnp.stack([got[owners[i], i] for i in range(count)])
+    chunks = value.reshape(count, devices, -1).transpose(1, 0, 2).reshape(devices, -1)
+    width = chunks.shape[1]
+    packed = jnp.concatenate([chunks, extra.astype(value.dtype)], axis=1)
+    got = lax.all_to_all(packed, "seq", 0, 0, tiled=True)
+    rows = got[:, :width].reshape(devices, count, -1)
+    mine = jnp.stack([rows[owners[i], i] for i in range(count)])
     full = lax.all_gather(mine, "seq", axis=0, tiled=False)
-    return full.transpose(1, 0, 2).reshape(value.shape)
+    return full.transpose(1, 0, 2).reshape(value.shape), got[:, width:].astype(extra.dtype)
 
 
 def summed_to_all(value):
@@ -109,48 +112,54 @@
 
 
 def sparse_kernel(q_ref, g_ref, kv_ref, allow_ref, out_ref, dq_ref, terms_ref, *, factor):
-    query = q_ref[0, 0]
-    grad = g_ref[0, 0]
-    keyval = kv_ref[0, 0]
-    key = keyval[:, :HD]
-    value = keyval[:, HD:]
     nt = (((1,), (1,)), ((), ()))
-    scores = lax.dot_general(query, key, nt, preferred_element_type=jnp.float32) * factor
-    mask = allow_ref[0, 0] > 0.5
-    row_max = jnp.max(jnp.where(mask, scores, -1e30), axis=-1, keepdims=True)
-    expo = jnp.where(mask, jnp.exp(scores - row_max), 0.0)
-    totals = jnp.sum(expo, axis=-1, keepdims=True)
-    result = jnp.dot(expo.astype(jnp.bfloat16), value, preferred_element_type=jnp.float32) / totals
-    probs = expo / totals
-    dprobs = lax.dot_general(grad, value, nt, preferred_element_type=jnp.float32)
-    dotted = jnp.sum(grad.astype(jnp.float32) * result, axis=-1, keepdims=True)
-    dscore = probs * (dprobs - dotted)
-    dq = factor * jnp.dot(dscore.astype(jnp.bfloat16), key, preferred_element_type=jnp.float32)
-    dkey = factor * jnp.dot(dscore.T.astype(jnp.bfloat16), query, preferred_element_type=jnp.float32)
-    dvalue = jnp.dot(probs.T.astype(jnp.bfloat16), grad, preferred_element_type=jnp.float32)
-    out_ref[0, 0] = result
-    dq_ref[0, 0] = dq
-    terms_ref[0, 0, :, :HD] = dkey
-    terms_ref[0, 0, :, HD:] = dvalue
-
-
-def sparse_call(query_h, grad_h, keyvals, allowed_f, factor, interpret=False):
+    for head in range(q_ref.shape[1]):
+        query = q_ref[0, head]
+        grad = g_ref[0, head]
+        keyval = kv_ref[0, head]
+        key = keyval[:, :HD]
+        value = keyval[:, HD:]
+        scores = lax.dot_general(query, key, nt, preferred_element_type=jnp.float32) * factor
+        mask = allow_ref[0, head] > 0.5
+        row_max = jnp.max(jnp.where(mask, scores, -1e30), axis=-1, keepdims=True)
+        expo = jnp.where(mask, jnp.exp(scores - row_max), 0.0)
+        totals = jnp.sum(expo, axis=-1, keepdims=True)
+        result = (
+            jnp.dot(expo.astype(jnp.bfloat16), value, preferred_element_type=jnp.float32)
+            / totals
+        )
+        probs = expo / totals
+        dprobs = lax.dot_general(grad, value, nt, preferred_element_type=jnp.float32)
+        dotted = jnp.sum(grad.astype(jnp.float32) * result, axis=-1, keepdims=True)
+        dscore = probs * (dprobs - dotted)
+        dq = factor * jnp.dot(dscore.astype(jnp.bfloat16), key, preferred_element_type=jnp.float32)
+        dkey = factor * jnp.dot(
+            dscore.T.astype(jnp.bfloat16), query, preferred_element_type=jnp.float32
+        )
+        dvalue = jnp.dot(probs.T.astype(jnp.bfloat16), grad, preferred_element_type=jnp.float32)
+        out_ref[0, head] = result
+        dq_ref[0, head] = dq
+        terms_ref[0, head, :, :HD] = dkey
+        terms_ref[0, head, :, HD:] = dvalue
+
+
+def sparse_call(query_h, grad_h, keyvals, allowed_f, factor, interpret=False, per_step=4):
     blocks, heads, rows, _ = query_h.shape
     keys_n = keyvals.shape[2]
-    small = pl.BlockSpec((1, 1, rows, HD), lambda i, h: (i, h, 0, 0))
+    small = pl.BlockSpec((1, per_step, rows, HD), lambda i, h: (i, h, 0, 0))
     return pl.pallas_call(
         lambda *refs: sparse_kernel(*refs, factor=factor),
-        grid=(blocks, heads),
+        grid=(blocks, heads // per_step),
         in_specs=[
             small,
             small,
-            pl.BlockSpec((1, 1, keys_n, 2 * HD), lambda i, h: (i, h, 0, 0)),
-            pl.BlockSpec((1, 1, 1, keys_n), lambda i, h: (i, h, 0, 0)),
+            pl.BlockSpec((1, per_step, keys_n, 2 * HD), lambda i, h: (i, h, 0, 0)),
+            pl.BlockSpec((1, per_step, 1, keys_n), lambda i, h: (i, h, 0, 0)),
         ],
         out_specs=[
             small,
             small,
-            pl.BlockSpec((1, 1, keys_n, 2 * HD), lambda i, h: (i, h, 0, 0)),
+            pl.BlockSpec((1, per_step, keys_n, 2 * HD), lambda i, h: (i, h, 0, 0)),
         ],
         out_shape=[
             jax.ShapeDtypeStruct((blocks, heads, rows, HD), jnp.float32),
@@ -210,10 +219,8 @@
     outgoing = jnp.where(
         jnp.any(slot_hit, axis=1), jnp.sum(jnp.where(slot_hit, req_codes[None, :], 0), axis=1), -1
     ).reshape(devices, capacity)
-    wanted = lax.all_to_all(outgoing, "seq", split_axis=0, concat_axis=0, tiled=True)
+    grows, wanted = from_owners(stacked_rows, global_blocks // per_dev, outgoing)
     sending = kv_local.reshape(per_dev * H, BLK, 2 * HD)[jnp.maximum(wanted, 0)]
-    sending, stacked_rows = lax.optimization_barrier((sending, stacked_rows))
-    grows = from_owners(stacked_rows, global_blocks // per_dev)
     g_query = grows[:, :, :width].reshape(NG, BLK, H, HD)
     g_grad = grows[:, :, 3 * width :].reshape(NG, BLK, H, HD)
     g_kv = pair_heads(grows[:, :, width : 3 * width], NG)

time: 643 us -> 616 us (0.958)
  Pallas kernels: 91.7 us -> 69.3 us
  blocking collectives: 147 us -> 131 us
  local copies, waits for them, and re-layouts: 204 us -> 219 us
  starting transfers between devices: 53.7 us -> 40.8 us
  other arithmetic: 52 us -> 58.5 us
    pallas_call x1, Pallas kernels: 91.7 us -> 69.3 us  [sparse_call(): pl.pallas_call(lambda *refs: sparse_kernel(*refs, factor=factor), grid=(b...]
    all_to_all x1 -> x0, blocking collectives: 18.2 us -> none  [per_device(): got = lax.all_to_all(packed, 'seq', 0, 0, tiled=True)]
    unnamed x101 -> x97, local copies, waits for them, and re-layouts: 30.5 us -> 41.9 us
    ppermute x2, starting transfers between devices: 14.4 us -> 3.29 us  [padded_2(): lax.ppermute(lax.slice_in_dim(block, block.shape[dim] - width, None, axis...]
    ppermute x2, waiting for transfers between devices: 37.9 us -> 47.9 us  [padded_2(): lax.ppermute(lax.slice_in_dim(block, 0, width, axis=dim), axis, backward)]
    all_to_all x2, waiting for transfers between devices: 7.59 us -> 0.01 us  [the longest x1 0.01 us: from_owners(): got = lax.all_to_all(packed, 'seq', 0, 0, tiled=True)]
  transfers between devices with their start and end apart: 9 -> 9, of which waited for: 3 -> 2; matrix products, arithmetic and copies ran while one was open for 25% -> 33% of each run, Pallas kernels for 0% -> 0%
where the time goes in v3:
time: 616 us; the launch traced here: 608 us
  local copies, waits for them, and re-layouts  219 us (36%)
  blocking collectives  131 us (21%)
  Pallas kernels  69.3 us (11%)
  other arithmetic  58.5 us (9%)
  waiting for transfers between devices  52 us (8%)
  starting transfers between devices  40.8 us (7%)
  matrix products  26.4 us (4%)
  between operations  11 us (2%)
    pallas_call x1, Pallas kernels, sparse_call(): pl.pallas_call(lambda *refs: sparse_kernel(*refs, factor=factor), grid=(b...  69.3 us
    all_gather x1, blocking collectives, per_device(): lax.all_gather(jnp.concatenate([top[:, None], tot[:, None], acc], axis=-1...  66.5 us
    ppermute x2, waiting for transfers between devices, padded_2(): lax.ppermute(lax.slice_in_dim(block, 0, width, axis=dim), axis, backward)  47.9 us
    unnamed x97, local copies, waits for them, and re-layouts  41.9 us
    all_gather x1, blocking collectives, summed_to_all(): full = lax.all_gather(total, 'seq', axis=0, tiled=True)  38.2 us
    all_gather x1, blocking collectives, from_owners(): full = lax.all_gather(mine, 'seq', axis=0, tiled=False)  25.8 us
    another operation x3, local copies, waits for them, and re-layouts, run_group(): jnp.stack([kv_heads[0:group], kv_heads[1:group + 1], kv_heads[2:group + 2...  15.4 us
    concatenate x5, local copies, waits for them, and re-layouts, per_device(): jnp.concatenate([left_rows[None, :, :2 * width], kv_rows.reshape(per_dev,...  14.7 us
  transfers between devices with their start and end apart: 9, of which 2 were waited for; matrix products, arithmetic and copies ran while one was open for 33% of the time, Pallas kernels for 0%

profile of v3, /device:TPU:19, one launch (start us, length us, event | category | flops | bytes accessed | tf_op | source)
XLA Modules:
  0.0 607.9 jit_solution(12328863626892962089)
XLA Ops:
  20.6 8.9 %all-to-all-start = ((bf16[32,2,6151]{2,1,0:T(2,128)(2,1)}), bf16[32,2,6151]{2,1,0:T(2,128)(2,1)}, u32[]{:S(2)}, u32[]{:S(2)}) async-start(bf16[32,2,6151]{2,1,0:T(2,128)(2,1)} %reshape.642), calls=%async_computation | async-start | bytes 1605632 | tf_op jit(solution)/shard_map/all_to_all | solution.py:38
  55.9 6.5 %maximum_bitcast_fusion = bf16[10,12,64,2,64]{2,0,4,1,3:T(8,128)(2,1)} fusion(bf16[1,64,2,12,64]{1,0,4,3,2:T(2,128)(2,1)} %copy.263, bf16[8,64,2,12,64]{1,0,4,3,2:T(8,128)(2,1)S(1)} %concatenate.78, bf16[1,64,2,12,64]{1,0,4,3,2:T(2,128)(2,1)} %copy.262), kind=kLoop, calls=%fused_computation.8 | loop fusion | flops 5898240 | bytes 3932160 | tf_op jit(solution)/shard_map/transpose | solution.py:65
  62.4 5.2 reshape.643
  69.4 25.8 %all-gather.1 = bf16[32,2,6144]{2,1,0:T(2,128)(2,1)S(1)} all-gather(bf16[1,2,6144]{2,1,0:T(2,128)(2,1)S(1)} %maximum_bitcast_fusion.2), channel_id=2, replica_groups=mesh['seq'=32,'grp'=4] {'seq'}, dimensions={0}, use_global_device_ids=true | all-gather | bytes 811008 | tf_op jit(solution)/shard_map/all_gather | solution.py:41
  102.7 6.9 %all-to-all-start.2 = ((f32[32,48,66]{2,1,0:T(8,128)}), f32[32,48,66]{2,1,0:T(8,128)S(1)}, u32[]{:S(2)}, u32[]{:S(2)}) async-start(f32[32,48,66]{2,1,0:T(8,128)} %pad_maximum_fusion.1), calls=%async_computation.2 | async-start | bytes 1572864 | tf_op jit(solution)/shard_map/all_to_all | solution.py:325
  109.7 8.7 %fusion.60 = (bf16[8,12,64,2,64]{2,0,4,1,3:T(8,128)(2,1)}, bf16[8,12,64,2,64]{2,0,4,1,3:T(8,128)(2,1)}, bf16[8,12,64,2,64]{2,0,4,1,3:T(8,128)(2,1)}) fusion(bf16[10,12,64,2,64]{2,0,4,1,3:T(8,128)(2,1)} %maximum_bitcast_fusion), kind=kLoop, calls=%fused_computation.185 | loop fusion | bytes 9437184 | tf_op jit(solution)/shard_map/slice | solution.py:248
  118.3 9.4 %copy.265 = bf16[8,12,64,2,64]{4,3,2,1,0:T(2,128)(2,1)} copy(bf16[8,12,64,2,64]{2,0,4,1,3:T(8,128)(2,1)} %get-tuple-element.139) | data formatting | bytes 3145728 | tf_op jit(solution)/shard_map/slice | solution.py:248
  127.7 5.3 reshape.586
  133.9 13.3 %gather_fusion = bf16[448,64,128]{2,1,0:T(8,128)(2,1)} fusion(bf16[96,64,128]{2,1,0:T(8,128)(2,1)S(1)} %reshape.586, s32[1024]{0:T(1024)S(1)} %pad_clamp_fusion), kind=kCustom, calls=%fused_computation | custom fusion | bytes 14681856 | tf_op jit(solution)/shard_map/gather | solution.py:223
  148.1 7.9 %all-to-all-start.1 = ((bf16[32,14,64,128]{3,2,1,0:T(8,128)(2,1)}), bf16[32,14,64,128]{3,2,1,0:T(8,128)(2,1)}, u32[]{:S(2)}, u32[]{:S(2)}) async-start(bf16[32,14,64,128]{3,2,1,0:T(8,128)(2,1)} %bitcast.214), calls=%async_computation.1 | async-start | bytes 14680064 | tf_op jit(solution)/shard_map/all_to_all | solution.py:227
  163.3 4.9 copy_bitcast_fusion
  170.8 9.4 %copy.264 = bf16[8,12,64,2,64]{4,3,2,1,0:T(2,128)(2,1)} copy(bf16[8,12,64,2,64]{2,0,4,1,3:T(8,128)(2,1)} %get-tuple-element.140) | data formatting | bytes 3145728 | tf_op jit(solution)/shard_map/slice | solution.py:248
  180.2 6.4 %stack.23 = bf16[8,12,1,64,128]{4,3,1,0,2:T(8,128)(2,1)} reshape(bf16[8,12,64,2,64]{4,3,2,1,0:T(2,128)(2,1)} %copy.264) | data formatting | bytes 3145728 | tf_op jit(solution)/shard_map/stack | solution.py:247
  186.6 5.9 copy.266
  192.5 6.4 %stack.25 = bf16[8,12,1,64,128]{4,3,1,0,2:T(8,128)(2,1)} reshape(bf16[8,12,64,2,64]{4,3,2,1,0:T(2,128)(2,1)} %copy.266) | data formatting | bytes 3145728 | tf_op jit(solution)/shard_map/stack | solution.py:247
  215.9 66.5 %all_gather.14 = f32[1536,66]{1,0:T(8,128)S(1)} all-gather(f32[48,66]{1,0:T(8,128)S(1)} %pad_maximum_fusion.8), channel_id=1, replica_groups=mesh['seq'=32,'grp'=4] {'seq'}, dimensions={0}, use_global_device_ids=true | all-gather | bytes 418176 | tf_op jit(solution)/shard_map/all_gather | solution.py:330
  298.1 8.0 %gather_fusion.1 = bf16[288,64,128]{2,1,0:T(8,128)(2,1)} fusion(bf16[32,14,64,128]{3,2,1,0:T(8,128)(2,1)} %all-to-all-done.1, s32[288]{0:T(512)S(1)} %fusion.56), kind=kCustom, calls=%fused_computation.1 | custom fusion | bytes 9439488 | tf_op jit(solution)/shard_map/gather | solution.py:228
  306.2 6.0 constant_dynamic-update-slice_fusion.2
  312.1 69.3 %shard_map.93 = (f32[8,12,64,64]{3,2,1,0:T(8,128)}, f32[8,12,64,64]{3,2,1,0:T(8,128)}, f32[8,12,512,128]{3,2,1,0:T(8,128)}) custom-call(bf16[8,12,64,64]{3,2,1,0:T(8,128)(2,1)} %get-tuple-element.172.refs_0_, bf16[8,12,64,64]{3,2,1,0:T(8,128)(2,1)} %get-tuple-element.171.refs_1_, bf16[8,12,512,128]{3,2,1,0:T(8,128)(2,1)} %bitcast.21.refs_2_, ...), custom_call_target="tpu_custom_call" | custom-call | tf_op jit(solution)/shard_map/pallas_call | solution.py:150
  385.0 7.2 %slice.470 = bf16[8,12,3,64,128]{4,3,2,1,0:T(8,128)(2,1)} slice(f32[8,12,8,64,128]{4,3,2,1,0:T(8,128)} %bitcast.217), slice={[0:8], [0:12], [5:8], [0:64], [0:128]} | slice | bytes 9437184 | tf_op jit(solution)/shard_map/slice | solution.py:264
  393.6 4.6 convert_element_type.124
  398.1 6.0 reduce.46
  406.4 5.4 all-to-all-start.3
  411.8 9.5 %fusion.2 = bf16[32,14,64,128]{3,0,2,1:T(8,128)(2,1)S(1)} fusion(s32[288]{0:T(512)S(1)} %multiply_add_fusion.2, s32[32,14]{0,1:T(8,128)S(1)} %copy-done.33, bf16[36,8,64,128]{3,2,1,0:T(8,128)(2,1)} %bitcast.219), kind=kOutput, calls=%fused_computation.11 | convolution fusion | flops 2114058240 | bytes 12061568 | tf_op jit(solution)/shard_map/se,ef->sf/dot_general | solution.py:291
  421.3 5.8 copy.307
  427.1 7.5 %all-to-all-start.4 = ((bf16[32,14,64,128]{3,2,1,0:T(8,128)(2,1)}), bf16[32,14,64,128]{3,2,1,0:T(8,128)(2,1)}, u32[]{:S(2)}, u32[]{:S(2)}) async-start(bf16[32,14,64,128]{3,2,1,0:T(8,128)(2,1)} %copy.307), calls=%async_computation.4 | async-start | bytes 14680064 | tf_op jit(solution)/shard_map/all_to_all | solution.py:297
  446.6 4.8 slice_bitcast_fusion.4
  463.6 47.9 %collective-permute-done.3 = bf16[1,12,64,128]{3,2,1,0:T(8,128)(2,1)} collective-permute-done((bf16[1,12,64,128]{3,2,1,0:T(8,128)(2,1)S(1)}, bf16[1,12,64,128]{3,2,1,0:T(8,128)(2,1)}, u32[]{:S(2)}, u32[]{:S(2)}) %collective-permute-start.3) | collective-permute-done | bytes 196640 | tf_op jit(solution)/shard_map/ppermute | solution.py:27
  511.5 4.0 collective-permute-done.2
  517.6 4.7 reshape.645
  524.5 38.2 %all_gather.15 = bf16[294912]{0:T(1024)(128)(2,1)} all-gather(bf16[9216]{0:T(1024)(128)(2,1)S(1)} %reduce_sum.89), channel_id=1, replica_groups=mesh['seq'=32,'grp'=4] {'seq'}, dimensions={0}, use_global_device_ids=true | all-gather | bytes 608256 | tf_op jit(solution)/shard_map/all_gather | solution.py:50
  579.1 6.7 %fusion = f32[8,12,64,128]{3,1,2,0:T(8,128)S(1)} fusion(s32[8,12]{1,0:T(8,128)S(1)} %copy-done.36, s32[448]{0:T(512)S(1)} %copy-done.37, bf16[56,8,64,128]{3,2,1,0:T(8,128)(2,1)} %bitcast.99), kind=kOutput, calls=%fused_computation.5 | convolution fusion | flops 704686080 | bytes 10487936 | tf_op jit(solution)/shard_map/sc,sf->cf/dot_general | solution.py:301
  (245 shorter events, 164.0 us)
Async XLA Ops:
  6.8 5.3 copy-start.25
  14.9 14.7 %copy-start.15 = (bf16[512,768]{1,0:T(8,128)(2,1)S(1)}, bf16[512,768]{1,0:T(8,128)(2,1)}, u32[]{:S(2)}) copy-start(bf16[512,768]{1,0:T(8,128)(2,1)} %param.23) | copy-start | bytes 2359300
  15.5 14.1 %copy-start.14 = (bf16[512,768]{1,0:T(8,128)(2,1)S(1)}, bf16[512,768]{1,0:T(8,128)(2,1)}, u32[]{:S(2)}) copy-start(bf16[512,768]{1,0:T(8,128)(2,1)} %param.24) | copy-start | bytes 2359300
  20.6 12.0 %copy-start.34 = (s32[2]{0:T(128)S(1)}, s32[2]{0:T(128)}, u32[]{:S(2)}) copy-start(s32[2]{0:T(128)} %param.27) | copy-start | bytes 28
  20.6 41.8 %all-to-all-start = ((bf16[32,2,6151]{2,1,0:T(2,128)(2,1)}), bf16[32,2,6151]{2,1,0:T(2,128)(2,1)}, u32[]{:S(2)}, u32[]{:S(2)}) async-start(bf16[32,2,6151]{2,1,0:T(2,128)(2,1)} %reshape.642), calls=%async_computation | async-start | bytes 1605632 | tf_op jit(solution)/shard_map/all_to_all | solution.py:38
  30.4 14.7 %collective-permute-start.1 = (bf16[64,1536]{1,0:T(8,128)(2,1)}, bf16[64,1536]{1,0:T(8,128)(2,1)}, u32[]{:S(2)}, u32[]{:S(2)}) collective-permute-start(bf16[64,1536]{1,0:T(8,128)(2,1)} %get-tuple-element.146), channel_id=1, source_target_pairs={{4,0},{8,4},{12,8},{16,12},{20,16},{24,20},{28,24},{32,28},{36,32}... | collective-permute-start | bytes 589832 | tf_op jit(solution)/shard_map/ppermute | solution.py:27
  30.8 20.2 %collective-permute-start = (bf16[64,1536]{1,0:T(8,128)(2,1)S(1)}, bf16[64,1536]{1,0:T(8,128)(2,1)S(1)}, u32[]{:S(2)}, u32[]{:S(2)}) collective-permute-start(bf16[64,1536]{1,0:T(8,128)(2,1)S(1)} %get-tuple-element.145), channel_id=1, source_target_pairs={{0,4},{4,8},{8,12},{12,16},{16,20},{20,24},{24,28},{28,32},{32,36}... | collective-permute-start | bytes 589832 | tf_op jit(solution)/shard_map/ppermute | solution.py:24
  69.4 27.9 %copy-start.17 = (bf16[512,768]{0,1:T(8,128)(2,1)S(1)}, bf16[512,768]{0,1:T(8,128)(2,1)}, u32[]{:S(2)}) copy-start(bf16[512,768]{0,1:T(8,128)(2,1)} %copy.283) | copy-start | bytes 2359300
  102.7 44.5 %all-to-all-start.2 = ((f32[32,48,66]{2,1,0:T(8,128)}), f32[32,48,66]{2,1,0:T(8,128)S(1)}, u32[]{:S(2)}, u32[]{:S(2)}) async-start(f32[32,48,66]{2,1,0:T(8,128)} %pad_maximum_fusion.1), calls=%async_computation.2 | async-start | bytes 1572864 | tf_op jit(solution)/shard_map/all_to_all | solution.py:325
  147.2 8.8 %copy-start.23 = (bf16[512,768]{1,0:T(8,128)(2,1)S(1)}, bf16[512,768]{1,0:T(8,128)(2,1)}, u32[]{:S(2)}) copy-start(bf16[512,768]{1,0:T(8,128)(2,1)} %param.22) | copy-start | bytes 2359300
  147.3 11.0 %copy-start.26 = (s32[8,12,3]{2,1,0:T(8,128)S(1)}, s32[8,12,3]{2,1,0:T(8,128)}, u32[]{:S(2)}) copy-start(s32[8,12,3]{2,1,0:T(8,128)} %copy-done.25) | copy-start | bytes 3460
  147.3 11.2 %copy-start.35 = (s32[2]{0:T(128)S(1)}, s32[2]{0:T(128)}, u32[]{:S(2)}) copy-start(s32[2]{0:T(128)} %param.27) | copy-start | bytes 28
  148.1 150.0 %all-to-all-start.1 = ((bf16[32,14,64,128]{3,2,1,0:T(8,128)(2,1)}), bf16[32,14,64,128]{3,2,1,0:T(8,128)(2,1)}, u32[]{:S(2)}, u32[]{:S(2)}) async-start(bf16[32,14,64,128]{3,2,1,0:T(8,128)(2,1)} %bitcast.214), calls=%async_computation.1 | async-start | bytes 14680064 | tf_op jit(solution)/shard_map/all_to_all | solution.py:227
  156.0 5.2 copy-start.29
  163.3 4.9 copy-start
  180.2 6.4 %copy-start.6 = (bf16[8,12,64,2,64]{2,0,4,1,3:T(8,128)(2,1)S(1)}, bf16[8,12,64,2,64]{2,0,4,1,3:T(8,128)(2,1)}, u32[]{:S(2)}) copy-start(bf16[8,12,64,2,64]{2,0,4,1,3:T(8,128)(2,1)} %get-tuple-element.138) | copy-start | bytes 4718596
  192.5 6.4 %copy-start.9 = (bf16[8,12,1,64,128]{4,3,1,0,2:T(8,128)(2,1)S(1)}, bf16[8,12,1,64,128]{4,3,1,0,2:T(8,128)(2,1)}, u32[]{:S(2)}) copy-start(bf16[8,12,1,64,128]{4,3,1,0,2:T(8,128)(2,1)} %stack.23) | copy-start | bytes 4718596
  192.5 8.2 %copy-start.8 = (bf16[8,12,1,64,128]{4,3,1,0,2:T(8,128)(2,1)S(1)}, bf16[8,12,1,64,128]{4,3,1,0,2:T(8,128)(2,1)}, u32[]{:S(2)}) copy-start(bf16[8,12,1,64,128]{4,3,1,0,2:T(8,128)(2,1)} %stack.24) | copy-start | bytes 4718596
  206.5 5.3 copy-start.12
  213.2 70.4 %copy-start.13 = (bf16[2,64,12,64]{3,2,1,0:T(8,128)(2,1)S(1)}, bf16[2,64,12,64]{3,2,1,0:T(8,128)(2,1)}, u32[]{:S(2)}) copy-start(bf16[2,64,12,64]{3,2,1,0:T(8,128)(2,1)} %copy-done.12) | copy-start | bytes 589828
  213.3 79.9 %copy-start.2 = (f32[12,2,64,512]{3,2,1,0:T(8,128)S(1)}, f32[12,2,64,512]{3,2,1,0:T(8,128)}, u32[]{:S(2)}) copy-start(f32[12,2,64,512]{3,2,1,0:T(8,128)} %copy-done.1) | copy-start | bytes 9437188
  385.0 7.2 %copy-start.28 = (bf16[2,12,64,64]{3,2,0,1:T(8,128)(2,1)S(1)}, bf16[2,12,64,64]{3,2,0,1:T(8,128)(2,1)}, u32[]{:S(2)}) copy-start(bf16[2,12,64,64]{3,2,0,1:T(8,128)(2,1)} %fusion.23) | copy-start | bytes 589828
  393.6 18.3 %copy-start.33 = (s32[32,14]{0,1:T(8,128)S(1)}, s32[32,14]{0,1:T(8,128)}, u32[]{:S(2)}) copy-start(s32[32,14]{0,1:T(8,128)} %multiply_add_fusion) | copy-start | bytes 5380
  406.4 20.7 %all-to-all-start.3 = ((bf16[32,2,4608]{2,1,0:T(2,128)(2,1)}), bf16[32,2,4608]{2,1,0:T(2,128)(2,1)}, u32[]{:S(2)}, u32[]{:S(2)}) async-start(bf16[32,2,4608]{2,1,0:T(2,128)(2,1)} %reshape.644), calls=%async_computation.3 | async-start | bytes 1179648 | tf_op jit(solution)/shard_map/all_to_all | solution.py:48
  427.1 9.5 %copy-start.38 = (s32[4]{0:T(128)S(1)}, s32[4]{0:T(128)}, u32[]{:S(2)}) copy-start(s32[4]{0:T(128)} %constant.301.clone.1) | copy-start | bytes 52
  427.1 152.1 %all-to-all-start.4 = ((bf16[32,14,64,128]{3,2,1,0:T(8,128)(2,1)}), bf16[32,14,64,128]{3,2,1,0:T(8,128)(2,1)}, u32[]{:S(2)}, u32[]{:S(2)}) async-start(bf16[32,14,64,128]{3,2,1,0:T(8,128)(2,1)} %copy.307), calls=%async_computation.4 | async-start | bytes 14680064 | tf_op jit(solution)/shard_map/all_to_all | solution.py:297
  434.6 9.9 %copy-start.30 = (f32[2,12,64]{2,0,1:T(2,128)S(1)}, f32[2,12,64]{2,0,1:T(2,128)}, u32[]{:S(2)}) copy-start(f32[2,12,64]{2,0,1:T(2,128)} %copy.295) | copy-start | bytes 18436
  451.3 5.1 copy-start.11
  454.4 57.0 %collective-permute-start.3 = (bf16[1,12,64,128]{3,2,1,0:T(8,128)(2,1)S(1)}, bf16[1,12,64,128]{3,2,1,0:T(8,128)(2,1)}, u32[]{:S(2)}, u32[]{:S(2)}) collective-permute-start(bf16[1,12,64,128]{3,2,1,0:T(8,128)(2,1)S(1)} %get-tuple-element.144), channel_id=1, source_target_pairs={{4,0},{8,4},{12,8},{16,12},{20,16},{24,20},{28,24},{32,28},{36,32}... | collective-permute-start | bytes 589832 | tf_op jit(solution)/shard_map/ppermute | solution.py:27
  454.9 60.6 %collective-permute-start.2 = (bf16[1,12,64,128]{3,2,1,0:T(8,128)(2,1)S(1)}, bf16[1,12,64,128]{3,2,1,0:T(8,128)(2,1)}, u32[]{:S(2)}, u32[]{:S(2)}) collective-permute-start(bf16[1,12,64,128]{3,2,1,0:T(8,128)(2,1)S(1)} %get-tuple-element.143), channel_id=1, source_target_pairs={{0,4},{4,8},{8,12},{12,16},{16,20},{20,24},{24,28},{28,32},{32,36}... | collective-permute-start | bytes 589832 | tf_op jit(solution)/shard_map/ppermute | solution.py:24
  572.7 6.4 %copy-start.36 = (s32[8,12]{1,0:T(8,128)S(1)}, s32[8,12]{1,0:T(8,128)}, u32[]{:S(2)}) copy-start(s32[8,12]{1,0:T(8,128)} %multiply_add_fusion.1) | copy-start | bytes 1156
  572.8 6.4 %copy-start.37 = (s32[448]{0:T(512)S(1)}, s32[448]{0:T(512)}, u32[]{:S(2)}) copy-start(s32[448]{0:T(512)} %eq.123) | copy-start | bytes 5380
  (17 other events, 42.3 us)

commit v4 on v3

--- a/solution.py
+++ b/solution.py
@@ -346,7 +346,9 @@
     tok_dvalue = jnp.einsum(
         "ghqk,gqhd->khd", probs.astype(jnp.bfloat16), g_grad, preferred_element_type=jnp.float32
     )
-    both_sum = summed_to_all(jnp.concatenate([g_dquery, global_part], axis=-1))
+    both_sum = lax.psum(
+        jnp.concatenate([g_dquery, global_part], axis=-1).astype(jnp.bfloat16), "seq"
+    ).astype(jnp.float32)
     dquery_sum = both_sum[..., :HD]
     global_sum = both_sum[..., HD:]
     for number in range(NG):

time: 616 us -> 703 us (1.14)
  blocking collectives: 131 us -> 180 us
  waiting for transfers between devices: 52 us -> 100 us
  local copies, waits for them, and re-layouts: 219 us -> 201 us
  between operations: 11 us -> 23.8 us
    psum x0 -> x1, waiting for transfers between devices: none -> 100 us  [per_device(): lax.psum(jnp.concatenate([g_dquery, global_part], axis=-1).astype(jnp.bfl...]
    ppermute x2, waiting for transfers between devices: 47.9 us -> 0.01 us  [padded_2(): lax.ppermute(lax.slice_in_dim(block, 0, width, axis=dim), axis, backward)]
    all_gather x1, blocking collectives: 66.5 us -> 112 us  [per_device(): lax.all_gather(jnp.concatenate([top[:, None], tot[:, None], acc], axis=-1...]
    all_gather x1, blocking collectives: 25.8 us -> 68.6 us  [from_owners(): full = lax.all_gather(mine, 'seq', axis=0, tiled=False)]
    all_gather x1 -> x0, blocking collectives: 38.2 us -> none  [summed_to_all(): full = lax.all_gather(total, 'seq', axis=0, tiled=True)]
    unnamed x97 -> x77, local copies, waits for them, and re-layouts: 41.9 us -> 32.8 us
    convert_element_type x2 -> x0, local copies, waits for them, and re-layouts: 7.14 us -> none  [the longest x1 4.59 us: summed_to_all(): chunks = value.astype(jnp.bfloat16).reshape(devices, -1)]
  transfers between devices with their start and end apart: 9 -> 9, of which waited for: 2 -> 1; matrix products, arithmetic and copies ran while one was open for 33% -> 33% of each run, Pallas kernels for 0% -> 10%
where the time goes in v4:
time: 703 us; the launch traced here: 694 us
  local copies, waits for them, and re-layouts  201 us (29%)
  blocking collectives  180 us (26%)
  waiting for transfers between devices  100 us (14%)
  Pallas kernels  69.2 us (10%)
  other arithmetic  53.3 us (8%)
  starting transfers between devices  36.4 us (5%)
  matrix products  29 us (4%)
  between operations  23.8 us (3%)
    all_gather x1, blocking collectives, per_device(): lax.all_gather(jnp.concatenate([top[:, None], tot[:, None], acc], axis=-1...  112 us
    psum x1, waiting for transfers between devices, per_device(): lax.psum(jnp.concatenate([g_dquery, global_part], axis=-1).astype(jnp.bfl...  100 us
    pallas_call x1, Pallas kernels, sparse_call(): pl.pallas_call(lambda *refs: sparse_kernel(*refs, factor=factor), grid=(b...  69.2 us
    all_gather x1, blocking collectives, from_owners(): full = lax.all_gather(mine, 'seq', axis=0, tiled=False)  68.6 us
    unnamed x77, local copies, waits for them, and re-layouts  32.8 us
    concatenate x5, local copies, waits for them, and re-layouts, per_device(): jnp.concatenate([left_rows[None, :, :2 * width], kv_rows.reshape(per_dev,...  15.7 us
    another operation x3, local copies, waits for them, and re-layouts, run_group(): jnp.stack([kv_heads[0:group], kv_heads[1:group + 1], kv_heads[2:group + 2...  15.4 us
  transfers between devices with their start and end apart: 9, of which 1 were waited for; matrix products, arithmetic and copies ran while one was open for 33% of the time, Pallas kernels for 10%

profile of v4, /device:TPU:19, one launch (start us, length us, event | category | flops | bytes accessed | tf_op | source)
XLA Modules:
  0.0 693.7 jit_solution(2390956600174821338)
XLA Ops:
  29.1 11.5 %all-to-all-start = ((bf16[32,2,6151]{2,1,0:T(2,128)(2,1)}), bf16[32,2,6151]{2,1,0:T(2,128)(2,1)}, u32[]{:S(2)}, u32[]{:S(2)}) async-start(bf16[32,2,6151]{2,1,0:T(2,128)(2,1)} %reshape.623), calls=%async_computation | async-start | bytes 1605632 | tf_op jit(solution)/shard_map/all_to_all | solution.py:38
  42.2 3.9 concatenate.78
  48.3 3.7 copy.264
  54.2 3.7 copy.263
  57.9 5.2 maximum_bitcast_fusion
  63.0 3.6 fusion.70
  66.6 5.9 copy.266
  72.5 5.3 reshape.568
  77.9 5.2 reshape.624
  84.2 13.3 %gather_fusion = bf16[448,64,128]{2,1,0:T(8,128)(2,1)} fusion(bf16[96,64,128]{2,1,0:T(8,128)(2,1)S(1)} %reshape.568, s32[1024]{0:T(1024)S(1)} %pad_clamp_fusion), kind=kCustom, calls=%fused_computation | custom fusion | bytes 14681856 | tf_op jit(solution)/shard_map/gather | solution.py:223
  97.5 7.9 %all-to-all-start.1 = ((bf16[32,14,64,128]{3,2,1,0:T(8,128)(2,1)}), bf16[32,14,64,128]{3,2,1,0:T(8,128)(2,1)}, u32[]{:S(2)}, u32[]{:S(2)}) async-start(bf16[32,14,64,128]{3,2,1,0:T(8,128)(2,1)} %bitcast.211), calls=%async_computation.1 | async-start | bytes 14680064 | tf_op jit(solution)/shard_map/all_to_all | solution.py:227
  121.9 4.8 copy_bitcast_fusion
  129.3 9.4 %copy.265 = bf16[8,12,64,2,64]{4,3,2,1,0:T(2,128)(2,1)} copy(bf16[8,12,64,2,64]{2,0,4,1,3:T(8,128)(2,1)} %get-tuple-element.140) | data formatting | bytes 3145728 | tf_op jit(solution)/shard_map/slice | solution.py:248
  138.7 6.4 stack.23
  145.1 5.9 copy.267
  151.0 6.4 stack.25
  163.3 68.6 %all-gather.1 = bf16[32,2,6144]{2,1,0:T(2,128)(2,1)S(1)} all-gather(bf16[1,2,6144]{2,1,0:T(2,128)(2,1)S(1)} %maximum_bitcast_fusion.2), channel_id=2, replica_groups=mesh['seq'=32,'grp'=4] {'seq'}, dimensions={0}, use_global_device_ids=true | all-gather | bytes 811008 | tf_op jit(solution)/shard_map/all_gather | solution.py:41
  254.1 5.5 all-to-all-start.2
  259.5 8.0 %gather_fusion.1 = bf16[288,64,128]{2,1,0:T(8,128)(2,1)} fusion(bf16[32,14,64,128]{3,2,1,0:T(8,128)(2,1)} %all-to-all-done.1, s32[288]{0:T(512)S(1)} %fusion.66), kind=kCustom, calls=%fused_computation.1 | custom fusion | bytes 9439488 | tf_op jit(solution)/shard_map/gather | solution.py:228
  267.6 6.0 constant_dynamic-update-slice_fusion.2
  273.5 69.2 %shard_map.93 = (f32[8,12,64,64]{3,2,1,0:T(8,128)}, f32[8,12,64,64]{3,2,1,0:T(8,128)}, f32[8,12,512,128]{3,2,1,0:T(8,128)}) custom-call(bf16[8,12,64,64]{3,2,1,0:T(8,128)(2,1)} %get-tuple-element.172.refs_0_, bf16[8,12,64,64]{3,2,1,0:T(8,128)(2,1)} %get-tuple-element.171.refs_1_, bf16[8,12,512,128]{3,2,1,0:T(8,128)(2,1)} %bitcast.21.refs_2_, ...), custom_call_target="tpu_custom_call" | custom-call | tf_op jit(solution)/shard_map/pallas_call | solution.py:150
  342.7 4.9 slice.470
  347.7 11.3 %fusion.2 = bf16[32,14,64,128]{3,0,2,1:T(8,128)(2,1)S(1)} fusion(s32[288]{0:T(512)S(1)} %multiply_add_fusion.2, s32[32,14]{0,1:T(8,128)S(1)} %multiply_add_fusion, bf16[36,8,64,128]{3,2,1,0:T(8,128)(2,1)S(1)} %bitcast.216), kind=kOutput, calls=%fused_computation.11 | convolution fusion | flops 2114058240 | bytes 12061568 | tf_op jit(solution)/shard_map/se,ef->sf/dot_general | solution.py:291
  359.0 5.8 copy.308
  364.7 7.4 %all-to-all-start.3 = ((bf16[32,14,64,128]{3,2,1,0:T(8,128)(2,1)}), bf16[32,14,64,128]{3,2,1,0:T(8,128)(2,1)}, u32[]{:S(2)}, u32[]{:S(2)}) async-start(bf16[32,14,64,128]{3,2,1,0:T(8,128)(2,1)} %copy.308), calls=%async_computation.3 | async-start | bytes 14680064 | tf_op jit(solution)/shard_map/all_to_all | solution.py:297
  386.8 111.6 %all_gather.11 = f32[1536,66]{1,0:T(8,128)S(1)} all-gather(f32[48,66]{1,0:T(8,128)S(1)} %pad_maximum_fusion.8), channel_id=1, replica_groups=mesh['seq'=32,'grp'=4] {'seq'}, dimensions={0}, use_global_device_ids=true | all-gather | bytes 418176 | tf_op jit(solution)/shard_map/all_gather | solution.py:330
  517.9 4.8 slice_bitcast_fusion.4
  529.1 3.6 slice_reduce_fusion
  542.9 100.4 %all-reduce.6.cloned.1.call-done = bf16[2,12,64,192]{3,2,1,0:T(8,128)(2,1)} async-done(((bf16[2,12,64,192]{3,2,1,0:T(8,128)(2,1)}), bf16[2,12,64,192]{3,2,1,0:T(8,128)(2,1)}) %all-reduce.6.cloned.1.call-update) | async-done | bytes 589840 | tf_op jit(solution)/shard_map/psum | solution.py:349
  654.2 3.9 reshape.615
  658.1 6.7 fusion
  667.9 3.8 slice_bitcast_fusion
  (221 shorter events, 146.4 us)
Async XLA Ops:
  7.2 5.4 copy-start.26
  7.2 9.5 %copy-start.21 = (s32[8,12,3]{1,0,2:T(8,128)S(1)}, s32[8,12,3]{1,0,2:T(8,128)}, u32[]{:S(2)}) copy-start(s32[8,12,3]{1,0,2:T(8,128)} %param.26) | copy-start | bytes 3460
  10.4 35.8 %collective-permute-start.1 = (bf16[64,1536]{1,0:T(8,128)(2,1)}, bf16[64,1536]{1,0:T(8,128)(2,1)}, u32[]{:S(2)}, u32[]{:S(2)}) collective-permute-start(bf16[64,1536]{1,0:T(8,128)(2,1)} %get-tuple-element.146), channel_id=1, source_target_pairs={{4,0},{8,4},{12,8},{16,12},{20,16},{24,20},{28,24},{32,28},{36,32}... | collective-permute-start | bytes 589832 | tf_op jit(solution)/shard_map/ppermute | solution.py:27
  11.0 41.0 %collective-permute-start = (bf16[64,1536]{1,0:T(8,128)(2,1)}, bf16[64,1536]{1,0:T(8,128)(2,1)}, u32[]{:S(2)}, u32[]{:S(2)}) collective-permute-start(bf16[64,1536]{1,0:T(8,128)(2,1)} %get-tuple-element.145), channel_id=1, source_target_pairs={{0,4},{4,8},{8,12},{12,16},{16,20},{20,24},{24,28},{28,32},{32,36}... | collective-permute-start | bytes 589832 | tf_op jit(solution)/shard_map/ppermute | solution.py:24
  16.9 6.2 copy-start.18
  29.1 48.8 %all-to-all-start = ((bf16[32,2,6151]{2,1,0:T(2,128)(2,1)}), bf16[32,2,6151]{2,1,0:T(2,128)(2,1)}, u32[]{:S(2)}, u32[]{:S(2)}) async-start(bf16[32,2,6151]{2,1,0:T(2,128)(2,1)} %reshape.623), calls=%async_computation | async-start | bytes 1605632 | tf_op jit(solution)/shard_map/all_to_all | solution.py:38
  97.5 8.0 %copy-start.17 = (bf16[512,768]{1,0:T(8,128)(2,1)S(1)}, bf16[512,768]{1,0:T(8,128)(2,1)}, u32[]{:S(2)}) copy-start(bf16[512,768]{1,0:T(8,128)(2,1)} %param.22) | copy-start | bytes 2359300
  97.5 10.3 %copy-start.27 = (s32[2]{0:T(128)S(1)}, s32[2]{0:T(128)}, u32[]{:S(2)}) copy-start(s32[2]{0:T(128)} %param.27) | copy-start | bytes 28
  97.5 13.6 %copy-start.19 = (s32[8,12,3]{2,1,0:T(8,128)S(1)}, s32[8,12,3]{2,1,0:T(8,128)}, u32[]{:S(2)}) copy-start(s32[8,12,3]{2,1,0:T(8,128)} %copy-done.18) | copy-start | bytes 3460
  97.5 156.5 %all-to-all-start.1 = ((bf16[32,14,64,128]{3,2,1,0:T(8,128)(2,1)}), bf16[32,14,64,128]{3,2,1,0:T(8,128)(2,1)}, u32[]{:S(2)}, u32[]{:S(2)}) async-start(bf16[32,14,64,128]{3,2,1,0:T(8,128)(2,1)} %bitcast.211), calls=%async_computation.1 | async-start | bytes 14680064 | tf_op jit(solution)/shard_map/all_to_all | solution.py:227
  105.5 5.9 copy-start.10
  105.5 7.0 %copy-start.11 = (bf16[512,768]{1,0:T(8,128)(2,1)S(1)}, bf16[512,768]{1,0:T(8,128)(2,1)}, u32[]{:S(2)}) copy-start(bf16[512,768]{1,0:T(8,128)(2,1)} %param.23) | copy-start | bytes 2359300
  105.5 9.7 %copy-start.16 = (bf16[512,768]{1,0:T(8,128)(2,1)S(1)}, bf16[512,768]{1,0:T(8,128)(2,1)}, u32[]{:S(2)}) copy-start(bf16[512,768]{1,0:T(8,128)(2,1)} %param.25) | copy-start | bytes 2359300
  113.7 7.4 %copy-start.29 = (s32[4]{0:T(128)S(1)}, s32[4]{0:T(128)}, u32[]{:S(2)}) copy-start(s32[4]{0:T(128)} %constant.300.clone.1) | copy-start | bytes 52
  113.7 8.2 %copy-start.24 = (s32[288]{0:T(512)S(1)}, s32[288]{0:T(512)}, u32[]{:S(2)}) copy-start(s32[288]{0:T(512)} %copy-done.23) | copy-start | bytes 3460
  121.9 4.8 copy-start
  138.7 6.4 copy-start.2
  151.0 6.4 copy-start.6
  151.0 8.2 %copy-start.5 = (bf16[8,12,1,64,128]{4,3,1,0,2:T(8,128)(2,1)S(1)}, bf16[8,12,1,64,128]{4,3,1,0,2:T(8,128)(2,1)}, u32[]{:S(2)}) copy-start(bf16[8,12,1,64,128]{4,3,1,0,2:T(8,128)(2,1)} %stack.24) | copy-start | bytes 4718596
  157.5 3.6 copy-start.7
  159.3 3.3 copy-start.13
  248.3 3.1 copy-start.15
  254.1 110.7 %all-to-all-start.2 = ((f32[32,48,66]{2,1,0:T(8,128)}), f32[32,48,66]{2,1,0:T(8,128)}, u32[]{:S(2)}, u32[]{:S(2)}) async-start(f32[32,48,66]{2,1,0:T(8,128)} %pad_maximum_fusion.1), calls=%async_computation.2 | async-start | bytes 1572864 | tf_op jit(solution)/shard_map/all_to_all | solution.py:325
  364.7 293.3 %all-to-all-start.3 = ((bf16[32,14,64,128]{3,2,1,0:T(8,128)(2,1)}), bf16[32,14,64,128]{3,2,1,0:T(8,128)(2,1)}, u32[]{:S(2)}, u32[]{:S(2)}) async-start(bf16[32,14,64,128]{3,2,1,0:T(8,128)(2,1)} %copy.308), calls=%async_computation.3 | async-start | bytes 14680064 | tf_op jit(solution)/shard_map/all_to_all | solution.py:297
  372.2 271.0 %all-reduce.6.cloned.1.call-start = ((), (), s32[]{:S(2)}) async-start(), calls=%async_computation.4 | async-start | bytes 1572864 | tf_op jit(solution)/shard_map/psum | solution.py:349
  384.2 115.3 %copy-start.9 = (bf16[2,64,12,64]{3,2,1,0:T(8,128)(2,1)S(1)}, bf16[2,64,12,64]{3,2,1,0:T(8,128)(2,1)}, u32[]{:S(2)}) copy-start(bf16[2,64,12,64]{3,2,1,0:T(8,128)(2,1)} %reshape.575) | copy-start | bytes 589828
  513.0 2.9 copy-start.20
  513.0 2.9 copy-start.25
  522.6 5.0 copy-start.8
  525.8 15.0 %collective-permute-start.3 = (bf16[1,12,64,128]{3,2,1,0:T(8,128)(2,1)S(1)}, bf16[1,12,64,128]{3,2,1,0:T(8,128)(2,1)}, u32[]{:S(2)}, u32[]{:S(2)}) collective-permute-start(bf16[1,12,64,128]{3,2,1,0:T(8,128)(2,1)S(1)} %get-tuple-element.144), channel_id=1, source_target_pairs={{4,0},{8,4},{12,8},{16,12},{20,16},{24,20},{28,24},{32,28},{36,32}... | collective-permute-start | bytes 589832 | tf_op jit(solution)/shard_map/ppermute | solution.py:27
  526.0 14.7 %collective-permute-start.2 = (bf16[1,12,64,128]{3,2,1,0:T(8,128)(2,1)S(1)}, bf16[1,12,64,128]{3,2,1,0:T(8,128)(2,1)}, u32[]{:S(2)}, u32[]{:S(2)}) collective-permute-start(bf16[1,12,64,128]{3,2,1,0:T(8,128)(2,1)S(1)} %get-tuple-element.143), channel_id=1, source_target_pairs={{0,4},{4,8},{8,12},{12,16},{16,20},{20,24},{24,28},{28,32},{32,36}... | collective-permute-start | bytes 589832 | tf_op jit(solution)/shard_map/ppermute | solution.py:24
  651.7 6.4 copy-start.28
  (7 other events, 10.7 us)
Sparse Core Ops, SparseCore 0:
  538.7 104.4 all-reduce.5

commit v5 on v3

--- a/solution.py
+++ b/solution.py
@@ -134,16 +134,16 @@
         dscore = probs * (dprobs - dotted)
         dq = factor * jnp.dot(dscore.astype(jnp.bfloat16), key, preferred_element_type=jnp.float32)
         dkey = factor * jnp.dot(
-            dscore.T.astype(jnp.bfloat16), query, preferred_element_type=jnp.float32
-        )
-        dvalue = jnp.dot(probs.T.astype(jnp.bfloat16), grad, preferred_element_type=jnp.float32)
+            dscore.astype(jnp.bfloat16).T, query, preferred_element_type=jnp.float32
+        )
+        dvalue = jnp.dot(probs.astype(jnp.bfloat16).T, grad, preferred_element_type=jnp.float32)
         out_ref[0, head] = result
         dq_ref[0, head] = dq
         terms_ref[0, head, :, :HD] = dkey
         terms_ref[0, head, :, HD:] = dvalue
 
 
-def sparse_call(query_h, grad_h, keyvals, allowed_f, factor, interpret=False, per_step=4):
+def sparse_call(query_h, grad_h, keyvals, allowed_f, factor, interpret=False, per_step=6):
     blocks, heads, rows, _ = query_h.shape
     keys_n = keyvals.shape[2]
     small = pl.BlockSpec((1, per_step, rows, HD), lambda i, h: (i, h, 0, 0))

time: 616 us -> 614 us (level)
  transfers between devices with their start and end apart: 9 -> 9, of which waited for: 2 -> 2; matrix products, arithmetic and copies ran while one was open for 33% -> 34% of each run, Pallas kernels for 0% -> 0%
where the time goes in v5:
time: 614 us; the launch traced here: 606 us
  local copies, waits for them, and re-layouts  219 us (36%)
  blocking collectives  131 us (21%)
  Pallas kernels  67.2 us (11%)
  other arithmetic  58.5 us (10%)
  waiting for transfers between devices  52 us (8%)
  starting transfers between devices  40.8 us (7%)
  matrix products  26.4 us (4%)
  between operations  11 us (2%)
    pallas_call x1, Pallas kernels, sparse_call(): pl.pallas_call(lambda *refs: sparse_kernel(*refs, factor=factor), grid=(b...  67.2 us
    all_gather x1, blocking collectives, per_device(): lax.all_gather(jnp.concatenate([top[:, None], tot[:, None], acc], axis=-1...  66.5 us
    ppermute x2, waiting for transfers between devices, padded_2(): lax.ppermute(lax.slice_in_dim(block, 0, width, axis=dim), axis, backward)  47.9 us
    unnamed x97, local copies, waits for them, and re-layouts  41.9 us
    all_gather x1, blocking collectives, summed_to_all(): full = lax.all_gather(total, 'seq', axis=0, tiled=True)  38.2 us
    all_gather x1, blocking collectives, from_owners(): full = lax.all_gather(mine, 'seq', axis=0, tiled=False)  25.8 us
    another operation x3, local copies, waits for them, and re-layouts, run_group(): jnp.stack([kv_heads[0:group], kv_heads[1:group + 1], kv_heads[2:group + 2...  15.4 us
    concatenate x5, local copies, waits for them, and re-layouts, per_device(): jnp.concatenate([left_rows[None, :, :2 * width], kv_rows.reshape(per_dev,...  14.7 us
  transfers between devices with their start and end apart: 9, of which 2 were waited for; matrix products, arithmetic and copies ran while one was open for 34% of the time, Pallas kernels for 0%

profile of v5, /device:TPU:19, one launch (start us, length us, event | category | flops | bytes accessed | tf_op | source)
XLA Modules:
  0.0 605.8 jit_solution(6699779518414185779)
XLA Ops:
  20.6 8.9 %all-to-all-start = ((bf16[32,2,6151]{2,1,0:T(2,128)(2,1)}), bf16[32,2,6151]{2,1,0:T(2,128)(2,1)}, u32[]{:S(2)}, u32[]{:S(2)}) async-start(bf16[32,2,6151]{2,1,0:T(2,128)(2,1)} %reshape.642), calls=%async_computation | async-start | bytes 1605632 | tf_op jit(solution)/shard_map/all_to_all | solution.py:38
  55.9 6.5 %maximum_bitcast_fusion = bf16[10,12,64,2,64]{2,0,4,1,3:T(8,128)(2,1)} fusion(bf16[1,64,2,12,64]{1,0,4,3,2:T(2,128)(2,1)} %copy.263, bf16[8,64,2,12,64]{1,0,4,3,2:T(8,128)(2,1)S(1)} %concatenate.78, bf16[1,64,2,12,64]{1,0,4,3,2:T(2,128)(2,1)} %copy.262), kind=kLoop, calls=%fused_computation.8 | loop fusion | flops 5898240 | bytes 3932160 | tf_op jit(solution)/shard_map/transpose | solution.py:65
  62.4 5.2 reshape.643
  69.4 25.8 %all-gather.1 = bf16[32,2,6144]{2,1,0:T(2,128)(2,1)S(1)} all-gather(bf16[1,2,6144]{2,1,0:T(2,128)(2,1)S(1)} %maximum_bitcast_fusion.2), channel_id=2, replica_groups=mesh['seq'=32,'grp'=4] {'seq'}, dimensions={0}, use_global_device_ids=true | all-gather | bytes 811008 | tf_op jit(solution)/shard_map/all_gather | solution.py:41
  102.7 6.9 %all-to-all-start.2 = ((f32[32,48,66]{2,1,0:T(8,128)}), f32[32,48,66]{2,1,0:T(8,128)S(1)}, u32[]{:S(2)}, u32[]{:S(2)}) async-start(f32[32,48,66]{2,1,0:T(8,128)} %pad_maximum_fusion.1), calls=%async_computation.2 | async-start | bytes 1572864 | tf_op jit(solution)/shard_map/all_to_all | solution.py:325
  109.7 8.7 %fusion.60 = (bf16[8,12,64,2,64]{2,0,4,1,3:T(8,128)(2,1)}, bf16[8,12,64,2,64]{2,0,4,1,3:T(8,128)(2,1)}, bf16[8,12,64,2,64]{2,0,4,1,3:T(8,128)(2,1)}) fusion(bf16[10,12,64,2,64]{2,0,4,1,3:T(8,128)(2,1)} %maximum_bitcast_fusion), kind=kLoop, calls=%fused_computation.185 | loop fusion | bytes 9437184 | tf_op jit(solution)/shard_map/slice | solution.py:248
  118.3 9.4 %copy.265 = bf16[8,12,64,2,64]{4,3,2,1,0:T(2,128)(2,1)} copy(bf16[8,12,64,2,64]{2,0,4,1,3:T(8,128)(2,1)} %get-tuple-element.139) | data formatting | bytes 3145728 | tf_op jit(solution)/shard_map/slice | solution.py:248
  127.7 5.3 reshape.586
  133.9 13.3 %gather_fusion = bf16[448,64,128]{2,1,0:T(8,128)(2,1)} fusion(bf16[96,64,128]{2,1,0:T(8,128)(2,1)S(1)} %reshape.586, s32[1024]{0:T(1024)S(1)} %pad_clamp_fusion), kind=kCustom, calls=%fused_computation | custom fusion | bytes 14681856 | tf_op jit(solution)/shard_map/gather | solution.py:223
  148.1 7.9 %all-to-all-start.1 = ((bf16[32,14,64,128]{3,2,1,0:T(8,128)(2,1)}), bf16[32,14,64,128]{3,2,1,0:T(8,128)(2,1)}, u32[]{:S(2)}, u32[]{:S(2)}) async-start(bf16[32,14,64,128]{3,2,1,0:T(8,128)(2,1)} %bitcast.214), calls=%async_computation.1 | async-start | bytes 14680064 | tf_op jit(solution)/shard_map/all_to_all | solution.py:227
  163.3 4.9 copy_bitcast_fusion
  170.8 9.4 %copy.264 = bf16[8,12,64,2,64]{4,3,2,1,0:T(2,128)(2,1)} copy(bf16[8,12,64,2,64]{2,0,4,1,3:T(8,128)(2,1)} %get-tuple-element.140) | data formatting | bytes 3145728 | tf_op jit(solution)/shard_map/slice | solution.py:248
  180.2 6.4 %stack.23 = bf16[8,12,1,64,128]{4,3,1,0,2:T(8,128)(2,1)} reshape(bf16[8,12,64,2,64]{4,3,2,1,0:T(2,128)(2,1)} %copy.264) | data formatting | bytes 3145728 | tf_op jit(solution)/shard_map/stack | solution.py:247
  186.6 5.9 copy.266
  192.5 6.4 %stack.25 = bf16[8,12,1,64,128]{4,3,1,0,2:T(8,128)(2,1)} reshape(bf16[8,12,64,2,64]{4,3,2,1,0:T(2,128)(2,1)} %copy.266) | data formatting | bytes 3145728 | tf_op jit(solution)/shard_map/stack | solution.py:247
  215.9 66.5 %all_gather.14 = f32[1536,66]{1,0:T(8,128)S(1)} all-gather(f32[48,66]{1,0:T(8,128)S(1)} %pad_maximum_fusion.8), channel_id=1, replica_groups=mesh['seq'=32,'grp'=4] {'seq'}, dimensions={0}, use_global_device_ids=true | all-gather | bytes 418176 | tf_op jit(solution)/shard_map/all_gather | solution.py:330
  298.1 8.0 %gather_fusion.1 = bf16[288,64,128]{2,1,0:T(8,128)(2,1)} fusion(bf16[32,14,64,128]{3,2,1,0:T(8,128)(2,1)} %all-to-all-done.1, s32[288]{0:T(512)S(1)} %fusion.56), kind=kCustom, calls=%fused_computation.1 | custom fusion | bytes 9439488 | tf_op jit(solution)/shard_map/gather | solution.py:228
  306.2 6.0 constant_dynamic-update-slice_fusion.2
  312.1 67.2 %shard_map.93 = (f32[8,12,64,64]{3,2,1,0:T(8,128)}, f32[8,12,64,64]{3,2,1,0:T(8,128)}, f32[8,12,512,128]{3,2,1,0:T(8,128)}) custom-call(bf16[8,12,64,64]{3,2,1,0:T(8,128)(2,1)} %get-tuple-element.172.refs_0_, bf16[8,12,64,64]{3,2,1,0:T(8,128)(2,1)} %get-tuple-element.171.refs_1_, bf16[8,12,512,128]{3,2,1,0:T(8,128)(2,1)} %bitcast.21.refs_2_, ...), custom_call_target="tpu_custom_call" | custom-call | tf_op jit(solution)/shard_map/pallas_call | solution.py:150
  382.9 7.2 %slice.470 = bf16[8,12,3,64,128]{4,3,2,1,0:T(8,128)(2,1)} slice(f32[8,12,8,64,128]{4,3,2,1,0:T(8,128)} %bitcast.217), slice={[0:8], [0:12], [5:8], [0:64], [0:128]} | slice | bytes 9437184 | tf_op jit(solution)/shard_map/slice | solution.py:264
  391.4 4.6 convert_element_type.124
  396.0 6.0 reduce.46
  404.3 5.4 all-to-all-start.3
  409.7 9.4 %fusion.2 = bf16[32,14,64,128]{3,0,2,1:T(8,128)(2,1)S(1)} fusion(s32[288]{0:T(512)S(1)} %multiply_add_fusion.2, s32[32,14]{0,1:T(8,128)S(1)} %copy-done.33, bf16[36,8,64,128]{3,2,1,0:T(8,128)(2,1)} %bitcast.219), kind=kOutput, calls=%fused_computation.11 | convolution fusion | flops 2114058240 | bytes 12061568 | tf_op jit(solution)/shard_map/se,ef->sf/dot_general | solution.py:291
  419.1 5.8 copy.307
  424.9 7.6 %all-to-all-start.4 = ((bf16[32,14,64,128]{3,2,1,0:T(8,128)(2,1)}), bf16[32,14,64,128]{3,2,1,0:T(8,128)(2,1)}, u32[]{:S(2)}, u32[]{:S(2)}) async-start(bf16[32,14,64,128]{3,2,1,0:T(8,128)(2,1)} %copy.307), calls=%async_computation.4 | async-start | bytes 14680064 | tf_op jit(solution)/shard_map/all_to_all | solution.py:297
  444.4 4.8 slice_bitcast_fusion.4
  461.4 47.9 %collective-permute-done.3 = bf16[1,12,64,128]{3,2,1,0:T(8,128)(2,1)} collective-permute-done((bf16[1,12,64,128]{3,2,1,0:T(8,128)(2,1)S(1)}, bf16[1,12,64,128]{3,2,1,0:T(8,128)(2,1)}, u32[]{:S(2)}, u32[]{:S(2)}) %collective-permute-start.3) | collective-permute-done | bytes 196640 | tf_op jit(solution)/shard_map/ppermute | solution.py:27
  509.3 4.0 collective-permute-done.2
  515.5 4.7 reshape.645
  522.4 38.2 %all_gather.15 = bf16[294912]{0:T(1024)(128)(2,1)} all-gather(bf16[9216]{0:T(1024)(128)(2,1)S(1)} %reduce_sum.89), channel_id=1, replica_groups=mesh['seq'=32,'grp'=4] {'seq'}, dimensions={0}, use_global_device_ids=true | all-gather | bytes 608256 | tf_op jit(solution)/shard_map/all_gather | solution.py:50
  577.0 6.7 %fusion = f32[8,12,64,128]{3,1,2,0:T(8,128)S(1)} fusion(s32[8,12]{1,0:T(8,128)S(1)} %copy-done.36, s32[448]{0:T(512)S(1)} %copy-done.37, bf16[56,8,64,128]{3,2,1,0:T(8,128)(2,1)} %bitcast.99), kind=kOutput, calls=%fused_computation.5 | convolution fusion | flops 704686080 | bytes 10487936 | tf_op jit(solution)/shard_map/sc,sf->cf/dot_general | solution.py:301
  (245 shorter events, 164.0 us)
Async XLA Ops:
  6.8 5.3 copy-start.25
  14.9 14.7 %copy-start.15 = (bf16[512,768]{1,0:T(8,128)(2,1)S(1)}, bf16[512,768]{1,0:T(8,128)(2,1)}, u32[]{:S(2)}) copy-start(bf16[512,768]{1,0:T(8,128)(2,1)} %param.23) | copy-start | bytes 2359300
  15.5 14.1 %copy-start.14 = (bf16[512,768]{1,0:T(8,128)(2,1)S(1)}, bf16[512,768]{1,0:T(8,128)(2,1)}, u32[]{:S(2)}) copy-start(bf16[512,768]{1,0:T(8,128)(2,1)} %param.24) | copy-start | bytes 2359300
  20.6 12.0 %copy-start.34 = (s32[2]{0:T(128)S(1)}, s32[2]{0:T(128)}, u32[]{:S(2)}) copy-start(s32[2]{0:T(128)} %param.27) | copy-start | bytes 28
  20.6 41.8 %all-to-all-start = ((bf16[32,2,6151]{2,1,0:T(2,128)(2,1)}), bf16[32,2,6151]{2,1,0:T(2,128)(2,1)}, u32[]{:S(2)}, u32[]{:S(2)}) async-start(bf16[32,2,6151]{2,1,0:T(2,128)(2,1)} %reshape.642), calls=%async_computation | async-start | bytes 1605632 | tf_op jit(solution)/shard_map/all_to_all | solution.py:38
  30.4 14.7 %collective-permute-start.1 = (bf16[64,1536]{1,0:T(8,128)(2,1)}, bf16[64,1536]{1,0:T(8,128)(2,1)}, u32[]{:S(2)}, u32[]{:S(2)}) collective-permute-start(bf16[64,1536]{1,0:T(8,128)(2,1)} %get-tuple-element.146), channel_id=1, source_target_pairs={{4,0},{8,4},{12,8},{16,12},{20,16},{24,20},{28,24},{32,28},{36,32}... | collective-permute-start | bytes 589832 | tf_op jit(solution)/shard_map/ppermute | solution.py:27
  30.8 20.2 %collective-permute-start = (bf16[64,1536]{1,0:T(8,128)(2,1)S(1)}, bf16[64,1536]{1,0:T(8,128)(2,1)S(1)}, u32[]{:S(2)}, u32[]{:S(2)}) collective-permute-start(bf16[64,1536]{1,0:T(8,128)(2,1)S(1)} %get-tuple-element.145), channel_id=1, source_target_pairs={{0,4},{4,8},{8,12},{12,16},{16,20},{20,24},{24,28},{28,32},{32,36}... | collective-permute-start | bytes 589832 | tf_op jit(solution)/shard_map/ppermute | solution.py:24
  69.4 27.9 %copy-start.17 = (bf16[512,768]{0,1:T(8,128)(2,1)S(1)}, bf16[512,768]{0,1:T(8,128)(2,1)}, u32[]{:S(2)}) copy-start(bf16[512,768]{0,1:T(8,128)(2,1)} %copy.283) | copy-start | bytes 2359300
  102.7 44.5 %all-to-all-start.2 = ((f32[32,48,66]{2,1,0:T(8,128)}), f32[32,48,66]{2,1,0:T(8,128)S(1)}, u32[]{:S(2)}, u32[]{:S(2)}) async-start(f32[32,48,66]{2,1,0:T(8,128)} %pad_maximum_fusion.1), calls=%async_computation.2 | async-start | bytes 1572864 | tf_op jit(solution)/shard_map/all_to_all | solution.py:325
  147.2 8.8 %copy-start.23 = (bf16[512,768]{1,0:T(8,128)(2,1)S(1)}, bf16[512,768]{1,0:T(8,128)(2,1)}, u32[]{:S(2)}) copy-start(bf16[512,768]{1,0:T(8,128)(2,1)} %param.22) | copy-start | bytes 2359300
  147.3 11.0 %copy-start.26 = (s32[8,12,3]{2,1,0:T(8,128)S(1)}, s32[8,12,3]{2,1,0:T(8,128)}, u32[]{:S(2)}) copy-start(s32[8,12,3]{2,1,0:T(8,128)} %copy-done.25) | copy-start | bytes 3460
  147.3 11.2 %copy-start.35 = (s32[2]{0:T(128)S(1)}, s32[2]{0:T(128)}, u32[]{:S(2)}) copy-start(s32[2]{0:T(128)} %param.27) | copy-start | bytes 28
  148.1 150.0 %all-to-all-start.1 = ((bf16[32,14,64,128]{3,2,1,0:T(8,128)(2,1)}), bf16[32,14,64,128]{3,2,1,0:T(8,128)(2,1)}, u32[]{:S(2)}, u32[]{:S(2)}) async-start(bf16[32,14,64,128]{3,2,1,0:T(8,128)(2,1)} %bitcast.214), calls=%async_computation.1 | async-start | bytes 14680064 | tf_op jit(solution)/shard_map/all_to_all | solution.py:227
  156.0 5.2 copy-start.29
  163.3 4.9 copy-start
  180.2 6.4 %copy-start.6 = (bf16[8,12,64,2,64]{2,0,4,1,3:T(8,128)(2,1)S(1)}, bf16[8,12,64,2,64]{2,0,4,1,3:T(8,128)(2,1)}, u32[]{:S(2)}) copy-start(bf16[8,12,64,2,64]{2,0,4,1,3:T(8,128)(2,1)} %get-tuple-element.138) | copy-start | bytes 4718596
  192.5 6.4 %copy-start.9 = (bf16[8,12,1,64,128]{4,3,1,0,2:T(8,128)(2,1)S(1)}, bf16[8,12,1,64,128]{4,3,1,0,2:T(8,128)(2,1)}, u32[]{:S(2)}) copy-start(bf16[8,12,1,64,128]{4,3,1,0,2:T(8,128)(2,1)} %stack.23) | copy-start | bytes 4718596
  192.5 8.2 %copy-start.8 = (bf16[8,12,1,64,128]{4,3,1,0,2:T(8,128)(2,1)S(1)}, bf16[8,12,1,64,128]{4,3,1,0,2:T(8,128)(2,1)}, u32[]{:S(2)}) copy-start(bf16[8,12,1,64,128]{4,3,1,0,2:T(8,128)(2,1)} %stack.24) | copy-start | bytes 4718596
  206.5 5.3 copy-start.12
  213.3 70.4 %copy-start.13 = (bf16[2,64,12,64]{3,2,1,0:T(8,128)(2,1)S(1)}, bf16[2,64,12,64]{3,2,1,0:T(8,128)(2,1)}, u32[]{:S(2)}) copy-start(bf16[2,64,12,64]{3,2,1,0:T(8,128)(2,1)} %copy-done.12) | copy-start | bytes 589828
  213.3 79.9 %copy-start.2 = (f32[12,2,64,512]{3,2,1,0:T(8,128)S(1)}, f32[12,2,64,512]{3,2,1,0:T(8,128)}, u32[]{:S(2)}) copy-start(f32[12,2,64,512]{3,2,1,0:T(8,128)} %copy-done.1) | copy-start | bytes 9437188
  382.9 7.2 %copy-start.28 = (bf16[2,12,64,64]{3,2,0,1:T(8,128)(2,1)S(1)}, bf16[2,12,64,64]{3,2,0,1:T(8,128)(2,1)}, u32[]{:S(2)}) copy-start(bf16[2,12,64,64]{3,2,0,1:T(8,128)(2,1)} %fusion.23) | copy-start | bytes 589828
  391.4 18.3 %copy-start.33 = (s32[32,14]{0,1:T(8,128)S(1)}, s32[32,14]{0,1:T(8,128)}, u32[]{:S(2)}) copy-start(s32[32,14]{0,1:T(8,128)} %multiply_add_fusion) | copy-start | bytes 5380
  404.3 20.6 %all-to-all-start.3 = ((bf16[32,2,4608]{2,1,0:T(2,128)(2,1)}), bf16[32,2,4608]{2,1,0:T(2,128)(2,1)}, u32[]{:S(2)}, u32[]{:S(2)}) async-start(bf16[32,2,4608]{2,1,0:T(2,128)(2,1)} %reshape.644), calls=%async_computation.3 | async-start | bytes 1179648 | tf_op jit(solution)/shard_map/all_to_all | solution.py:48
  424.9 9.5 %copy-start.38 = (s32[4]{0:T(128)S(1)}, s32[4]{0:T(128)}, u32[]{:S(2)}) copy-start(s32[4]{0:T(128)} %constant.301.clone.1) | copy-start | bytes 52
  424.9 152.1 %all-to-all-start.4 = ((bf16[32,14,64,128]{3,2,1,0:T(8,128)(2,1)}), bf16[32,14,64,128]{3,2,1,0:T(8,128)(2,1)}, u32[]{:S(2)}, u32[]{:S(2)}) async-start(bf16[32,14,64,128]{3,2,1,0:T(8,128)(2,1)} %copy.307), calls=%async_computation.4 | async-start | bytes 14680064 | tf_op jit(solution)/shard_map/all_to_all | solution.py:297
  432.5 9.9 %copy-start.30 = (f32[2,12,64]{2,0,1:T(2,128)S(1)}, f32[2,12,64]{2,0,1:T(2,128)}, u32[]{:S(2)}) copy-start(f32[2,12,64]{2,0,1:T(2,128)} %copy.295) | copy-start | bytes 18436
  449.2 5.1 copy-start.11
  452.3 57.0 %collective-permute-start.3 = (bf16[1,12,64,128]{3,2,1,0:T(8,128)(2,1)S(1)}, bf16[1,12,64,128]{3,2,1,0:T(8,128)(2,1)}, u32[]{:S(2)}, u32[]{:S(2)}) collective-permute-start(bf16[1,12,64,128]{3,2,1,0:T(8,128)(2,1)S(1)} %get-tuple-element.144), channel_id=1, source_target_pairs={{4,0},{8,4},{12,8},{16,12},{20,16},{24,20},{28,24},{32,28},{36,32}... | collective-permute-start | bytes 589832 | tf_op jit(solution)/shard_map/ppermute | solution.py:27
  452.8 60.6 %collective-permute-start.2 = (bf16[1,12,64,128]{3,2,1,0:T(8,128)(2,1)S(1)}, bf16[1,12,64,128]{3,2,1,0:T(8,128)(2,1)}, u32[]{:S(2)}, u32[]{:S(2)}) collective-permute-start(bf16[1,12,64,128]{3,2,1,0:T(8,128)(2,1)S(1)} %get-tuple-element.143), channel_id=1, source_target_pairs={{0,4},{4,8},{8,12},{12,16},{16,20},{20,24},{24,28},{28,32},{32,36}... | collective-permute-start | bytes 589832 | tf_op jit(solution)/shard_map/ppermute | solution.py:24
  570.6 6.4 %copy-start.36 = (s32[8,12]{1,0:T(8,128)S(1)}, s32[8,12]{1,0:T(8,128)}, u32[]{:S(2)}) copy-start(s32[8,12]{1,0:T(8,128)} %multiply_add_fusion.1) | copy-start | bytes 1156
  570.6 6.4 %copy-start.37 = (s32[448]{0:T(512)S(1)}, s32[448]{0:T(512)}, u32[]{:S(2)}) copy-start(s32[448]{0:T(512)} %eq.123) | copy-start | bytes 5380
  (17 other events, 42.3 us)

commit v6 on v5

--- a/solution.py
+++ b/solution.py
@@ -111,7 +111,7 @@
     return (result, dquery, jnp.concatenate([dkey, dvalue], axis=-1), stats)
 
 
-def sparse_kernel(q_ref, g_ref, kv_ref, allow_ref, out_ref, dq_ref, terms_ref, *, factor):
+def sparse_kernel(q_ref, g_ref, kv_ref, allow_ref, out_ref, dq_ref, win_ref, glob_ref, rand_ref, *, factor):
     nt = (((1,), (1,)), ((), ()))
     for head in range(q_ref.shape[1]):
         query = q_ref[0, head]
@@ -139,8 +139,12 @@
         dvalue = jnp.dot(probs.astype(jnp.bfloat16).T, grad, preferred_element_type=jnp.float32)
         out_ref[0, head] = result
         dq_ref[0, head] = dq
-        terms_ref[0, head, :, :HD] = dkey
-        terms_ref[0, head, :, HD:] = dvalue
+        kinds = ((win_ref, 0, jnp.float32), (glob_ref, 3, jnp.float32), (rand_ref, 5, jnp.bfloat16))
+        for target, first, kind in kinds:
+            for slot in range(target.shape[2]):
+                rows = slice((first + slot) * BLK, (first + slot + 1) * BLK)
+                target[0, head, slot, :, :HD] = dkey[rows].astype(kind)
+                target[0, head, slot, :, HD:] = dvalue[rows].astype(kind)
 
 
 def sparse_call(query_h, grad_h, keyvals, allowed_f, factor, interpret=False, per_step=6):
@@ -159,12 +163,16 @@
         out_specs=[
             small,
             small,
-            pl.BlockSpec((1, per_step, keys_n, 2 * HD), lambda i, h: (i, h, 0, 0)),
+            pl.BlockSpec((1, per_step, 3, BLK, 2 * HD), lambda i, h: (i, h, 0, 0, 0)),
+            pl.BlockSpec((1, per_step, NG, BLK, 2 * HD), lambda i, h: (i, h, 0, 0, 0)),
+            pl.BlockSpec((1, per_step, R, BLK, 2 * HD), lambda i, h: (i, h, 0, 0, 0)),
         ],
         out_shape=[
             jax.ShapeDtypeStruct((blocks, heads, rows, HD), jnp.float32),
             jax.ShapeDtypeStruct((blocks, heads, rows, HD), jnp.float32),
-            jax.ShapeDtypeStruct((blocks, heads, keys_n, 2 * HD), jnp.float32),
+            jax.ShapeDtypeStruct((blocks, heads, 3, BLK, 2 * HD), jnp.float32),
+            jax.ShapeDtypeStruct((blocks, heads, NG, BLK, 2 * HD), jnp.float32),
+            jax.ShapeDtypeStruct((blocks, heads, R, BLK, 2 * HD), jnp.bfloat16),
         ],
         interpret=interpret,
     )(query_h, grad_h, keyvals, allowed_f)
@@ -250,18 +258,16 @@
         keyvals = jnp.concatenate([win_slots, glob_slots, rand_kv], axis=2).reshape(
             group, H, SLOTS * BLK, 2 * HD
         )
-        result, dquery, terms = sparse_call(
+        result, dquery, win_terms, glob_terms, random_out = sparse_call(
             query_heads, grad_heads, keyvals, allowed.astype(jnp.float32)[:, :, None, :], factor
         )
-        terms = terms.reshape(group, H, SLOTS, BLK, 2 * HD)
         spacing = ((0, 0), (0, 0), (0, 0), (0, 0))
         window_sum = (
-            jnp.pad(terms[:, :, 0], ((0, 2),) + spacing[1:])
-            + jnp.pad(terms[:, :, 1], ((1, 1),) + spacing[1:])
-            + jnp.pad(terms[:, :, 2], ((2, 0),) + spacing[1:])
-        )
-        global_sum = jnp.sum(terms[:, :, 3 : 3 + NG], axis=0)
-        random_out = terms[:, :, 3 + NG :].astype(jnp.bfloat16)
+            jnp.pad(win_terms[:, :, 0], ((0, 2),) + spacing[1:])
+            + jnp.pad(win_terms[:, :, 1], ((1, 1),) + spacing[1:])
+            + jnp.pad(win_terms[:, :, 2], ((2, 0),) + spacing[1:])
+        )
+        global_sum = jnp.sum(glob_terms, axis=0)
         return (result, dquery, window_sum, global_sum, random_out)
 
     if groups == 1:

time: 614 us -> 607 us (0.989)
  local copies, waits for them, and re-layouts: 219 us -> 210 us
    slice x1 -> x0, local copies, waits for them, and re-layouts: 7.16 us -> none  [run_group(): random_out = terms[:, :, 3 + NG:].astype(jnp.bfloat16)]
    unnamed x97 -> x101, local copies, waits for them, and re-layouts: 41.9 us -> 41.4 us
where the time goes in v6:
time: 607 us; the launch traced here: 598 us
  local copies, waits for them, and re-layouts  210 us (35%)
  blocking collectives  131 us (22%)
  Pallas kernels  65.7 us (11%)
  other arithmetic  60.1 us (10%)
  waiting for transfers between devices  53.1 us (9%)
  starting transfers between devices  40.8 us (7%)
  matrix products  26.5 us (4%)
  between operations  10.6 us (2%)
    all_gather x1, blocking collectives, per_device(): lax.all_gather(jnp.concatenate([top[:, None], tot[:, None], acc], axis=-1...  67 us
    pallas_call x1, Pallas kernels, sparse_call(): pl.pallas_call(lambda *refs: sparse_kernel(*refs, factor=factor), grid=(b...  65.7 us
    ppermute x2, waiting for transfers between devices, padded_2(): lax.ppermute(lax.slice_in_dim(block, 0, width, axis=dim), axis, backward)  49.1 us
    unnamed x101, local copies, waits for them, and re-layouts  41.4 us
    all_gather x1, blocking collectives, summed_to_all(): full = lax.all_gather(total, 'seq', axis=0, tiled=True)  38.2 us
    all_gather x1, blocking collectives, from_owners(): full = lax.all_gather(mine, 'seq', axis=0, tiled=False)  25.8 us
    another operation x3, local copies, waits for them, and re-layouts, run_group(): jnp.stack([kv_heads[0:group], kv_heads[1:group + 1], kv_heads[2:group + 2...  15.4 us
    concatenate x5, local copies, waits for them, and re-layouts, per_device(): jnp.concatenate([left_rows[None, :, :2 * width], kv_rows.reshape(per_dev,...  14.7 us
  transfers between devices with their start and end apart: 9, of which 2 were waited for; matrix products, arithmetic and copies ran while one was open for 34% of the time, Pallas kernels for 0%

profile of v6, /device:TPU:19, one launch (start us, length us, event | category | flops | bytes accessed | tf_op | source)
XLA Modules:
  0.0 598.1 jit_solution(17347216049394407428)
XLA Ops:
  20.6 8.9 %all-to-all-start = ((bf16[32,2,6151]{2,1,0:T(2,128)(2,1)}), bf16[32,2,6151]{2,1,0:T(2,128)(2,1)}, u32[]{:S(2)}, u32[]{:S(2)}) async-start(bf16[32,2,6151]{2,1,0:T(2,128)(2,1)} %reshape.638), calls=%async_computation | async-start | bytes 1605632 | tf_op jit(solution)/shard_map/all_to_all | solution.py:38
  39.5 3.9 concatenate.78
  55.5 6.5 %maximum_bitcast_fusion = bf16[10,12,64,2,64]{2,0,4,1,3:T(8,128)(2,1)} fusion(bf16[1,64,2,12,64]{1,0,4,3,2:T(2,128)(2,1)} %copy.258, bf16[8,64,2,12,64]{1,0,4,3,2:T(8,128)(2,1)S(1)} %concatenate.78, bf16[1,64,2,12,64]{1,0,4,3,2:T(2,128)(2,1)} %copy.257), kind=kLoop, calls=%fused_computation.6 | loop fusion | flops 5898240 | bytes 3932160 | tf_op jit(solution)/shard_map/transpose | solution.py:65
  62.0 5.2 reshape.639
  68.9 25.8 %all-gather.1 = bf16[32,2,6144]{2,1,0:T(2,128)(2,1)S(1)} all-gather(bf16[1,2,6144]{2,1,0:T(2,128)(2,1)S(1)} %maximum_bitcast_fusion.2), channel_id=2, replica_groups=mesh['seq'=32,'grp'=4] {'seq'}, dimensions={0}, use_global_device_ids=true | all-gather | bytes 811008 | tf_op jit(solution)/shard_map/all_gather | solution.py:41
  102.3 6.9 %all-to-all-start.2 = ((f32[32,48,66]{2,1,0:T(8,128)}), f32[32,48,66]{2,1,0:T(8,128)S(1)}, u32[]{:S(2)}, u32[]{:S(2)}) async-start(f32[32,48,66]{2,1,0:T(8,128)} %pad_maximum_fusion.1), calls=%async_computation.2 | async-start | bytes 1572864 | tf_op jit(solution)/shard_map/all_to_all | solution.py:331
  109.2 8.5 %fusion.60 = (bf16[8,12,64,2,64]{2,0,4,1,3:T(8,128)(2,1)}, bf16[8,12,64,2,64]{2,0,4,1,3:T(8,128)(2,1)}, bf16[8,12,64,2,64]{2,0,4,1,3:T(8,128)(2,1)}) fusion(bf16[10,12,64,2,64]{2,0,4,1,3:T(8,128)(2,1)} %maximum_bitcast_fusion), kind=kLoop, calls=%fused_computation.183 | loop fusion | bytes 9437184 | tf_op jit(solution)/shard_map/slice | solution.py:256
  117.7 9.4 %copy.260 = bf16[8,12,64,2,64]{4,3,2,1,0:T(2,128)(2,1)} copy(bf16[8,12,64,2,64]{2,0,4,1,3:T(8,128)(2,1)} %get-tuple-element.142) | data formatting | bytes 3145728 | tf_op jit(solution)/shard_map/slice | solution.py:256
  127.2 5.3 reshape.583
  133.3 13.3 %gather_fusion = bf16[448,64,128]{2,1,0:T(8,128)(2,1)} fusion(bf16[96,64,128]{2,1,0:T(8,128)(2,1)S(1)} %reshape.583, s32[1024]{0:T(1024)S(1)} %pad_clamp_fusion), kind=kCustom, calls=%fused_computation | custom fusion | bytes 14681856 | tf_op jit(solution)/shard_map/gather | solution.py:231
  147.5 7.9 %all-to-all-start.1 = ((bf16[32,14,64,128]{3,2,1,0:T(8,128)(2,1)}), bf16[32,14,64,128]{3,2,1,0:T(8,128)(2,1)}, u32[]{:S(2)}, u32[]{:S(2)}) async-start(bf16[32,14,64,128]{3,2,1,0:T(8,128)(2,1)} %bitcast.207), calls=%async_computation.1 | async-start | bytes 14680064 | tf_op jit(solution)/shard_map/all_to_all | solution.py:235
  162.8 4.9 copy_bitcast_fusion
  170.3 9.4 %copy.259 = bf16[8,12,64,2,64]{4,3,2,1,0:T(2,128)(2,1)} copy(bf16[8,12,64,2,64]{2,0,4,1,3:T(8,128)(2,1)} %get-tuple-element.143) | data formatting | bytes 3145728 | tf_op jit(solution)/shard_map/slice | solution.py:256
  179.7 6.4 %stack.23 = bf16[8,12,1,64,128]{4,3,1,0,2:T(8,128)(2,1)} reshape(bf16[8,12,64,2,64]{4,3,2,1,0:T(2,128)(2,1)} %copy.259) | data formatting | bytes 3145728 | tf_op jit(solution)/shard_map/stack | solution.py:255
  186.1 5.9 copy.261
  192.0 6.4 %stack.25 = bf16[8,12,1,64,128]{4,3,1,0,2:T(8,128)(2,1)} reshape(bf16[8,12,64,2,64]{4,3,2,1,0:T(2,128)(2,1)} %copy.261) | data formatting | bytes 3145728 | tf_op jit(solution)/shard_map/stack | solution.py:255
  214.9 67.0 %all_gather.14 = f32[1536,66]{1,0:T(8,128)S(1)} all-gather(f32[48,66]{1,0:T(8,128)S(1)} %pad_maximum_fusion.8), channel_id=1, replica_groups=mesh['seq'=32,'grp'=4] {'seq'}, dimensions={0}, use_global_device_ids=true | all-gather | bytes 418176 | tf_op jit(solution)/shard_map/all_gather | solution.py:336
  297.6 8.0 %gather_fusion.1 = bf16[288,64,128]{2,1,0:T(8,128)(2,1)} fusion(bf16[32,14,64,128]{3,2,1,0:T(8,128)(2,1)} %all-to-all-done.1, s32[288]{0:T(512)S(1)} %fusion.56), kind=kCustom, calls=%fused_computation.1 | custom fusion | bytes 9439488 | tf_op jit(solution)/shard_map/gather | solution.py:236
  305.6 5.9 constant_dynamic-update-slice_fusion.2
  311.5 65.7 %shard_map.93 = (f32[8,12,64,64]{3,2,1,0:T(8,128)}, f32[8,12,64,64]{3,2,1,0:T(8,128)}, f32[8,12,3,64,128]{4,3,2,1,0:T(8,128)}, f32[8,12,2,64,128]{4,3,2,1,0:T(8,128)}, bf16[8,12,3,64,128]{4,3,2,1,0:T(8,128)(2,1)}) custom-call(bf16[8,12,64,64]{3,2,1,0:T(8,128)(2,1)} %get-tuple-element.175.refs_0_, bf16[8,12,64,64]{3,2,1,0:T(8,128)(2,1)} %get-tuple-element.174.refs_1_, ...), custom_call_target="tpu_custom_call" | custom-call | tf_op jit(solution)/shard_map/pallas_call | solution.py:154
  377.2 4.3 reduce_sum.88
  383.9 4.6 convert_element_type.123
  388.5 6.0 %reduce.46 = bf16[32,9216]{1,0:T(8,128)(2,1)} reduce(bf16[32,1,9216]{2,1,0:T(2,128)(2,1)} %convert_element_type.123, bf16[]{:T(256)} %broadcast.398), dimensions={1}, to_apply=%convert_element_type.123.reduce_sub_computation | reduce | bytes 1179650 | tf_op jit(solution)/shard_map/convert_element_type | solution.py:47
  396.9 5.4 all-to-all-start.3
  402.3 9.5 %fusion.2 = bf16[32,14,64,128]{3,0,2,1:T(8,128)(2,1)S(1)} fusion(s32[288]{0:T(512)S(1)} %multiply_add_fusion.2, s32[32,14]{0,1:T(8,128)S(1)} %copy-done.32, bf16[36,8,64,128]{3,2,1,0:T(8,128)(2,1)} %bitcast.230), kind=kOutput, calls=%fused_computation.9 | convolution fusion | flops 2114058240 | bytes 12061568 | tf_op jit(solution)/shard_map/se,ef->sf/dot_general | solution.py:297
  411.7 5.8 copy.301
  417.5 7.6 %all-to-all-start.4 = ((bf16[32,14,64,128]{3,2,1,0:T(8,128)(2,1)}), bf16[32,14,64,128]{3,2,1,0:T(8,128)(2,1)}, u32[]{:S(2)}, u32[]{:S(2)}) async-start(bf16[32,14,64,128]{3,2,1,0:T(8,128)(2,1)} %copy.301), calls=%async_computation.4 | async-start | bytes 14680064 | tf_op jit(solution)/shard_map/all_to_all | solution.py:303
  452.9 49.1 %collective-permute-done.3 = bf16[1,12,64,128]{3,2,1,0:T(8,128)(2,1)} collective-permute-done((bf16[1,12,64,128]{3,2,1,0:T(8,128)(2,1)S(1)}, bf16[1,12,64,128]{3,2,1,0:T(8,128)(2,1)}, u32[]{:S(2)}, u32[]{:S(2)}) %collective-permute-start.3) | collective-permute-done | bytes 196640 | tf_op jit(solution)/shard_map/ppermute | solution.py:27
  502.0 4.0 collective-permute-done.2
  508.1 4.7 reshape.641
  515.0 38.2 %all_gather.15 = bf16[294912]{0:T(1024)(128)(2,1)} all-gather(bf16[9216]{0:T(1024)(128)(2,1)S(1)} %reduce_sum.89), channel_id=1, replica_groups=mesh['seq'=32,'grp'=4] {'seq'}, dimensions={0}, use_global_device_ids=true | all-gather | bytes 608256 | tf_op jit(solution)/shard_map/all_gather | solution.py:50
  569.5 6.7 %fusion = f32[8,12,64,128]{3,1,2,0:T(8,128)S(1)} fusion(s32[8,12]{1,0:T(8,128)S(1)} %copy-done.35, s32[448]{0:T(512)S(1)} %copy-done.36, bf16[56,8,64,128]{3,2,1,0:T(8,128)(2,1)} %bitcast.92), kind=kOutput, calls=%fused_computation.4 | convolution fusion | flops 704686080 | bytes 10487936 | tf_op jit(solution)/shard_map/sc,sf->cf/dot_general | solution.py:307
  (250 shorter events, 160.4 us)
Async XLA Ops:
  6.6 5.2 copy-start.25
  14.7 14.8 %copy-start.15 = (bf16[512,768]{1,0:T(8,128)(2,1)S(1)}, bf16[512,768]{1,0:T(8,128)(2,1)}, u32[]{:S(2)}) copy-start(bf16[512,768]{1,0:T(8,128)(2,1)} %param.23) | copy-start | bytes 2359300
  15.4 14.2 %copy-start.14 = (bf16[512,768]{1,0:T(8,128)(2,1)S(1)}, bf16[512,768]{1,0:T(8,128)(2,1)}, u32[]{:S(2)}) copy-start(bf16[512,768]{1,0:T(8,128)(2,1)} %param.24) | copy-start | bytes 2359300
  20.6 12.0 %copy-start.33 = (s32[2]{0:T(128)S(1)}, s32[2]{0:T(128)}, u32[]{:S(2)}) copy-start(s32[2]{0:T(128)} %param.27) | copy-start | bytes 28
  20.6 41.4 %all-to-all-start = ((bf16[32,2,6151]{2,1,0:T(2,128)(2,1)}), bf16[32,2,6151]{2,1,0:T(2,128)(2,1)}, u32[]{:S(2)}, u32[]{:S(2)}) async-start(bf16[32,2,6151]{2,1,0:T(2,128)(2,1)} %reshape.638), calls=%async_computation | async-start | bytes 1605632 | tf_op jit(solution)/shard_map/all_to_all | solution.py:38
  30.3 14.3 %collective-permute-start.1 = (bf16[64,1536]{1,0:T(8,128)(2,1)}, bf16[64,1536]{1,0:T(8,128)(2,1)}, u32[]{:S(2)}, u32[]{:S(2)}) collective-permute-start(bf16[64,1536]{1,0:T(8,128)(2,1)} %get-tuple-element.149), channel_id=1, source_target_pairs={{4,0},{8,4},{12,8},{16,12},{20,16},{24,20},{28,24},{32,28},{36,32}... | collective-permute-start | bytes 589832 | tf_op jit(solution)/shard_map/ppermute | solution.py:27
  30.7 19.8 %collective-permute-start = (bf16[64,1536]{1,0:T(8,128)(2,1)S(1)}, bf16[64,1536]{1,0:T(8,128)(2,1)S(1)}, u32[]{:S(2)}, u32[]{:S(2)}) collective-permute-start(bf16[64,1536]{1,0:T(8,128)(2,1)S(1)} %get-tuple-element.148), channel_id=1, source_target_pairs={{0,4},{4,8},{8,12},{12,16},{16,20},{20,24},{24,28},{28,32},{32,36}... | collective-permute-start | bytes 589832 | tf_op jit(solution)/shard_map/ppermute | solution.py:24
  68.9 27.9 %copy-start.17 = (bf16[512,768]{0,1:T(8,128)(2,1)S(1)}, bf16[512,768]{0,1:T(8,128)(2,1)}, u32[]{:S(2)}) copy-start(bf16[512,768]{0,1:T(8,128)(2,1)} %copy.278) | copy-start | bytes 2359300
  102.3 44.4 %all-to-all-start.2 = ((f32[32,48,66]{2,1,0:T(8,128)}), f32[32,48,66]{2,1,0:T(8,128)S(1)}, u32[]{:S(2)}, u32[]{:S(2)}) async-start(f32[32,48,66]{2,1,0:T(8,128)} %pad_maximum_fusion.1), calls=%async_computation.2 | async-start | bytes 1572864 | tf_op jit(solution)/shard_map/all_to_all | solution.py:331
  146.7 8.8 %copy-start.23 = (bf16[512,768]{1,0:T(8,128)(2,1)S(1)}, bf16[512,768]{1,0:T(8,128)(2,1)}, u32[]{:S(2)}) copy-start(bf16[512,768]{1,0:T(8,128)(2,1)} %param.22) | copy-start | bytes 2359300
  146.7 11.0 %copy-start.26 = (s32[8,12,3]{2,1,0:T(8,128)S(1)}, s32[8,12,3]{2,1,0:T(8,128)}, u32[]{:S(2)}) copy-start(s32[8,12,3]{2,1,0:T(8,128)} %copy-done.25) | copy-start | bytes 3460
  146.7 11.2 %copy-start.34 = (s32[2]{0:T(128)S(1)}, s32[2]{0:T(128)}, u32[]{:S(2)}) copy-start(s32[2]{0:T(128)} %param.27) | copy-start | bytes 28
  147.5 150.0 %all-to-all-start.1 = ((bf16[32,14,64,128]{3,2,1,0:T(8,128)(2,1)}), bf16[32,14,64,128]{3,2,1,0:T(8,128)(2,1)}, u32[]{:S(2)}, u32[]{:S(2)}) async-start(bf16[32,14,64,128]{3,2,1,0:T(8,128)(2,1)} %bitcast.207), calls=%async_computation.1 | async-start | bytes 14680064 | tf_op jit(solution)/shard_map/all_to_all | solution.py:235
  155.4 5.3 copy-start.28
  162.8 4.9 copy-start
  179.7 6.4 %copy-start.6 = (bf16[8,12,64,2,64]{2,0,4,1,3:T(8,128)(2,1)S(1)}, bf16[8,12,64,2,64]{2,0,4,1,3:T(8,128)(2,1)}, u32[]{:S(2)}) copy-start(bf16[8,12,64,2,64]{2,0,4,1,3:T(8,128)(2,1)} %get-tuple-element.141) | copy-start | bytes 4718596
  192.0 6.4 %copy-start.9 = (bf16[8,12,1,64,128]{4,3,1,0,2:T(8,128)(2,1)S(1)}, bf16[8,12,1,64,128]{4,3,1,0,2:T(8,128)(2,1)}, u32[]{:S(2)}) copy-start(bf16[8,12,1,64,128]{4,3,1,0,2:T(8,128)(2,1)} %stack.23) | copy-start | bytes 4718596
  192.0 8.1 %copy-start.8 = (bf16[8,12,1,64,128]{4,3,1,0,2:T(8,128)(2,1)S(1)}, bf16[8,12,1,64,128]{4,3,1,0,2:T(8,128)(2,1)}, u32[]{:S(2)}) copy-start(bf16[8,12,1,64,128]{4,3,1,0,2:T(8,128)(2,1)} %stack.24) | copy-start | bytes 4718596
  205.6 5.2 copy-start.12
  212.2 70.8 %copy-start.13 = (bf16[2,64,12,64]{3,2,1,0:T(8,128)(2,1)S(1)}, bf16[2,64,12,64]{3,2,1,0:T(8,128)(2,1)}, u32[]{:S(2)}) copy-start(bf16[2,64,12,64]{3,2,1,0:T(8,128)(2,1)} %copy-done.12) | copy-start | bytes 589828
  212.2 80.4 %copy-start.2 = (f32[12,2,64,512]{3,2,1,0:T(8,128)S(1)}, f32[12,2,64,512]{3,2,1,0:T(8,128)}, u32[]{:S(2)}) copy-start(f32[12,2,64,512]{3,2,1,0:T(8,128)} %copy-done.1) | copy-start | bytes 9437188
  383.9 18.3 %copy-start.32 = (s32[32,14]{0,1:T(8,128)S(1)}, s32[32,14]{0,1:T(8,128)}, u32[]{:S(2)}) copy-start(s32[32,14]{0,1:T(8,128)} %multiply_add_fusion) | copy-start | bytes 5380
  396.9 20.7 %all-to-all-start.3 = ((bf16[32,2,4608]{2,1,0:T(2,128)(2,1)}), bf16[32,2,4608]{2,1,0:T(2,128)(2,1)}, u32[]{:S(2)}, u32[]{:S(2)}) async-start(bf16[32,2,4608]{2,1,0:T(2,128)(2,1)} %reshape.640), calls=%async_computation.3 | async-start | bytes 1179648 | tf_op jit(solution)/shard_map/all_to_all | solution.py:48
  417.5 9.5 %copy-start.37 = (s32[4]{0:T(128)S(1)}, s32[4]{0:T(128)}, u32[]{:S(2)}) copy-start(s32[4]{0:T(128)} %constant.301.clone.1) | copy-start | bytes 52
  417.5 152.0 %all-to-all-start.4 = ((bf16[32,14,64,128]{3,2,1,0:T(8,128)(2,1)}), bf16[32,14,64,128]{3,2,1,0:T(8,128)(2,1)}, u32[]{:S(2)}, u32[]{:S(2)}) async-start(bf16[32,14,64,128]{3,2,1,0:T(8,128)(2,1)} %copy.301), calls=%async_computation.4 | async-start | bytes 14680064 | tf_op jit(solution)/shard_map/all_to_all | solution.py:303
  425.1 10.0 %copy-start.29 = (f32[2,12,64]{2,0,1:T(2,128)S(1)}, f32[2,12,64]{2,0,1:T(2,128)}, u32[]{:S(2)}) copy-start(f32[2,12,64]{2,0,1:T(2,128)} %copy.290) | copy-start | bytes 18436
  431.9 7.6 %slice-start = ((s8[9437184]{0:T(1024)(128)(4,1)}), s8[4194304]{0:T(1024)(128)(4,1)S(1)}, s32[]{:S(2)}) async-start(s8[9437184]{0:T(1024)(128)(4,1)} %bitcast.209), calls=%async_computation.5 | async-start | bytes 8388608
  440.7 5.2 copy-start.11
  444.0 58.0 %collective-permute-start.3 = (bf16[1,12,64,128]{3,2,1,0:T(8,128)(2,1)S(1)}, bf16[1,12,64,128]{3,2,1,0:T(8,128)(2,1)}, u32[]{:S(2)}, u32[]{:S(2)}) collective-permute-start(bf16[1,12,64,128]{3,2,1,0:T(8,128)(2,1)S(1)} %get-tuple-element.147), channel_id=1, source_target_pairs={{4,0},{8,4},{12,8},{16,12},{20,16},{24,20},{28,24},{32,28},{36,32}... | collective-permute-start | bytes 589832 | tf_op jit(solution)/shard_map/ppermute | solution.py:27
  444.5 61.5 %collective-permute-start.2 = (bf16[1,12,64,128]{3,2,1,0:T(8,128)(2,1)S(1)}, bf16[1,12,64,128]{3,2,1,0:T(8,128)(2,1)}, u32[]{:S(2)}, u32[]{:S(2)}) collective-permute-start(bf16[1,12,64,128]{3,2,1,0:T(8,128)(2,1)S(1)} %get-tuple-element.146), channel_id=1, source_target_pairs={{0,4},{4,8},{8,12},{12,16},{16,20},{20,24},{24,28},{28,32},{32,36}... | collective-permute-start | bytes 589832 | tf_op jit(solution)/shard_map/ppermute | solution.py:24
  563.1 6.4 %copy-start.35 = (s32[8,12]{1,0:T(8,128)S(1)}, s32[8,12]{1,0:T(8,128)}, u32[]{:S(2)}) copy-start(s32[8,12]{1,0:T(8,128)} %multiply_add_fusion.1) | copy-start | bytes 1156
  563.1 6.4 %copy-start.36 = (s32[448]{0:T(512)S(1)}, s32[448]{0:T(512)}, u32[]{:S(2)}) copy-start(s32[448]{0:T(512)} %eq.123) | copy-start | bytes 5380
  (19 other events, 51.0 us)

commit v7 on v6

--- a/solution.py
+++ b/solution.py
@@ -44,7 +44,7 @@
 
 def summed_to_all(value):
     devices = lax.axis_size("seq")
-    chunks = value.astype(jnp.bfloat16).reshape(devices, -1)
+    chunks = value.astype(jnp.bfloat16).reshape(devices, -1, value.shape[-1])
     got = lax.all_to_all(chunks, "seq", 0, 0, tiled=True)
     total = jnp.sum(got.astype(jnp.float32), axis=0).astype(jnp.bfloat16)
     full = lax.all_gather(total, "seq", axis=0, tiled=True)

time: 607 us -> 584 us (0.962)
  local copies, waits for them, and re-layouts: 210 us -> 197 us
  other arithmetic: 60.1 us -> 48.6 us
    unnamed x101 -> x103, local copies, waits for them, and re-layouts: 41.4 us -> 34.3 us
    convert_element_type x2 -> x0, local copies, waits for them, and re-layouts: 7.11 us -> none  [the longest x1 4.58 us: summed_to_all(): chunks = value.astype(jnp.bfloat16).reshape(devices, -1)]
  transfers between devices with their start and end apart: 9 -> 9, of which waited for: 2 -> 2; matrix products, arithmetic and copies ran while one was open for 34% -> 33% of each run, Pallas kernels for 0% -> 0%
where the time goes in v7:
time: 584 us; the launch traced here: 575 us
  local copies, waits for them, and re-layouts  197 us (34%)
  blocking collectives  135 us (23%)
  Pallas kernels  65.5 us (11%)
  waiting for transfers between devices  53.3 us (9%)
  other arithmetic  48.6 us (8%)
  starting transfers between devices  40 us (7%)
  matrix products  25.7 us (4%)
  between operations  10.3 us (2%)
    all_gather x1, blocking collectives, per_device(): lax.all_gather(jnp.concatenate([top[:, None], tot[:, None], acc], axis=-1...  67 us
    pallas_call x1, Pallas kernels, sparse_call(): pl.pallas_call(lambda *refs: sparse_kernel(*refs, factor=factor), grid=(b...  65.5 us
    ppermute x2, waiting for transfers between devices, padded_2(): lax.ppermute(lax.slice_in_dim(block, 0, width, axis=dim), axis, backward)  49.2 us
    all_gather x1, blocking collectives, summed_to_all(): full = lax.all_gather(total, 'seq', axis=0, tiled=True)  41.9 us
    unnamed x103, local copies, waits for them, and re-layouts  34.3 us
    all_gather x1, blocking collectives, from_owners(): full = lax.all_gather(mine, 'seq', axis=0, tiled=False)  26.2 us
    another operation x3, local copies, waits for them, and re-layouts, run_group(): jnp.stack([kv_heads[0:group], kv_heads[1:group + 1], kv_heads[2:group + 2...  15.4 us
    concatenate x5, local copies, waits for them, and re-layouts, per_device(): jnp.concatenate([left_rows[None, :, :2 * width], kv_rows.reshape(per_dev,...  14.8 us
  transfers between devices with their start and end apart: 9, of which 2 were waited for; matrix products, arithmetic and copies ran while one was open for 33% of the time, Pallas kernels for 0%

profile of v7, /device:TPU:19, one launch (start us, length us, event | category | flops | bytes accessed | tf_op | source)
XLA Modules:
  0.0 575.4 jit_solution(431511707885423164)
XLA Ops:
  20.2 8.9 %all-to-all-start = ((bf16[32,2,6151]{2,1,0:T(2,128)(2,1)}), bf16[32,2,6151]{2,1,0:T(2,128)(2,1)}, u32[]{:S(2)}, u32[]{:S(2)}) async-start(bf16[32,2,6151]{2,1,0:T(2,128)(2,1)} %reshape.628), calls=%async_computation | async-start | bytes 1605632 | tf_op jit(solution)/shard_map/all_to_all | solution.py:38
  38.9 3.9 concatenate.83
  46.2 3.7 copy.258
  54.8 6.5 %maximum_bitcast_fusion = bf16[10,12,64,2,64]{2,0,4,1,3:T(8,128)(2,1)} fusion(bf16[1,64,2,12,64]{1,0,4,3,2:T(2,128)(2,1)} %copy.258, bf16[8,64,2,12,64]{1,0,4,3,2:T(8,128)(2,1)S(1)} %concatenate.83, bf16[1,64,2,12,64]{1,0,4,3,2:T(2,128)(2,1)} %copy.257), kind=kLoop, calls=%fused_computation.6 | loop fusion | flops 5898240 | bytes 3932160 | tf_op jit(solution)/shard_map/transpose | solution.py:65
  61.4 5.2 reshape.629
  68.3 26.2 %all-gather.1 = bf16[32,2,6144]{2,1,0:T(2,128)(2,1)S(1)} all-gather(bf16[1,2,6144]{2,1,0:T(2,128)(2,1)S(1)} %maximum_bitcast_fusion.2), channel_id=2, replica_groups=mesh['seq'=32,'grp'=4] {'seq'}, dimensions={0}, use_global_device_ids=true | all-gather | bytes 811008 | tf_op jit(solution)/shard_map/all_gather | solution.py:41
  102.0 6.9 %all-to-all-start.2 = ((f32[32,48,66]{2,1,0:T(8,128)}), f32[32,48,66]{2,1,0:T(8,128)S(1)}, u32[]{:S(2)}, u32[]{:S(2)}) async-start(f32[32,48,66]{2,1,0:T(8,128)} %pad_maximum_fusion.1), calls=%async_computation.2 | async-start | bytes 1572864 | tf_op jit(solution)/shard_map/all_to_all | solution.py:331
  108.9 8.5 %fusion.60 = (bf16[8,12,64,2,64]{2,0,4,1,3:T(8,128)(2,1)}, bf16[8,12,64,2,64]{2,0,4,1,3:T(8,128)(2,1)}, bf16[8,12,64,2,64]{2,0,4,1,3:T(8,128)(2,1)}) fusion(bf16[10,12,64,2,64]{2,0,4,1,3:T(8,128)(2,1)} %maximum_bitcast_fusion), kind=kLoop, calls=%fused_computation.183 | loop fusion | bytes 9437184 | tf_op jit(solution)/shard_map/slice | solution.py:256
  117.5 9.4 %copy.260 = bf16[8,12,64,2,64]{4,3,2,1,0:T(2,128)(2,1)} copy(bf16[8,12,64,2,64]{2,0,4,1,3:T(8,128)(2,1)} %get-tuple-element.142) | data formatting | bytes 3145728 | tf_op jit(solution)/shard_map/slice | solution.py:256
  126.9 5.3 reshape.573
  133.1 13.3 %gather_fusion = bf16[448,64,128]{2,1,0:T(8,128)(2,1)} fusion(bf16[96,64,128]{2,1,0:T(8,128)(2,1)S(1)} %reshape.573, s32[1024]{0:T(1024)S(1)} %pad_clamp_fusion), kind=kCustom, calls=%fused_computation | custom fusion | bytes 14681856 | tf_op jit(solution)/shard_map/gather | solution.py:231
  147.3 7.8 %all-to-all-start.1 = ((bf16[32,14,64,128]{3,2,1,0:T(8,128)(2,1)}), bf16[32,14,64,128]{3,2,1,0:T(8,128)(2,1)}, u32[]{:S(2)}, u32[]{:S(2)}) async-start(bf16[32,14,64,128]{3,2,1,0:T(8,128)(2,1)} %bitcast.209), calls=%async_computation.1 | async-start | bytes 14680064 | tf_op jit(solution)/shard_map/all_to_all | solution.py:235
  162.4 4.9 copy_bitcast_fusion
  169.9 9.4 %copy.259 = bf16[8,12,64,2,64]{4,3,2,1,0:T(2,128)(2,1)} copy(bf16[8,12,64,2,64]{2,0,4,1,3:T(8,128)(2,1)} %get-tuple-element.143) | data formatting | bytes 3145728 | tf_op jit(solution)/shard_map/slice | solution.py:256
  179.3 6.4 %stack.23 = bf16[8,12,1,64,128]{4,3,1,0,2:T(8,128)(2,1)} reshape(bf16[8,12,64,2,64]{4,3,2,1,0:T(2,128)(2,1)} %copy.259) | data formatting | bytes 3145728 | tf_op jit(solution)/shard_map/stack | solution.py:255
  185.7 6.0 %copy.261 = bf16[8,12,64,2,64]{4,3,2,1,0:T(2,128)(2,1)} copy(bf16[8,12,64,2,64]{2,0,4,1,3:T(8,128)(2,1)S(1)} %copy-done.6) | data formatting | bytes 3145728 | tf_op jit(solution)/shard_map/slice | solution.py:256
  191.8 6.4 %stack.25 = bf16[8,12,1,64,128]{4,3,1,0,2:T(8,128)(2,1)} reshape(bf16[8,12,64,2,64]{4,3,2,1,0:T(2,128)(2,1)} %copy.261) | data formatting | bytes 3145728 | tf_op jit(solution)/shard_map/stack | solution.py:255
  214.6 67.0 %all_gather.14 = f32[1536,66]{1,0:T(8,128)S(1)} all-gather(f32[48,66]{1,0:T(8,128)S(1)} %pad_maximum_fusion.8), channel_id=1, replica_groups=mesh['seq'=32,'grp'=4] {'seq'}, dimensions={0}, use_global_device_ids=true | all-gather | bytes 418176 | tf_op jit(solution)/shard_map/all_gather | solution.py:336
  296.8 7.9 %gather_fusion.1 = bf16[288,64,128]{2,1,0:T(8,128)(2,1)} fusion(bf16[32,14,64,128]{3,2,1,0:T(8,128)(2,1)} %all-to-all-done.1, s32[288]{0:T(512)S(1)} %fusion.56), kind=kCustom, calls=%fused_computation.1 | custom fusion | bytes 9439488 | tf_op jit(solution)/shard_map/gather | solution.py:236
  304.7 6.0 %constant_dynamic-update-slice_fusion.2 = bf16[8,12,8,64,128]{4,3,2,1,0:T(8,128)(2,1)} fusion(bf16[8,12,8,64,128]{4,3,2,1,0:T(8,128)(2,1)} %broadcast_dynamic-update-slice_fusion, bf16[8,12,3,64,128]{4,3,2,1,0:T(8,128)(2,1)} %bitcast.210), kind=kLoop, calls=%fused_computation.129 | loop fusion | bytes 9437184 | tf_op jit(solution)/shard_map/concatenate | solution.py:258
  310.7 65.5 %shard_map.93 = (f32[8,12,64,64]{3,2,1,0:T(8,128)}, f32[8,12,64,64]{3,2,1,0:T(8,128)}, f32[8,12,3,64,128]{4,3,2,1,0:T(8,128)}, f32[8,12,2,64,128]{4,3,2,1,0:T(8,128)}, bf16[8,12,3,64,128]{4,3,2,1,0:T(8,128)(2,1)}) custom-call(bf16[8,12,64,64]{3,2,1,0:T(8,128)(2,1)} %get-tuple-element.175.refs_0_, bf16[8,12,64,64]{3,2,1,0:T(8,128)(2,1)} %get-tuple-element.174.refs_1_, ...), custom_call_target="tpu_custom_call" | custom-call | tf_op jit(solution)/shard_map/pallas_call | solution.py:154
  376.3 4.3 reduce_sum.88
  383.8 5.0 all-to-all-start.3
  388.8 9.5 %fusion.2 = bf16[32,14,64,128]{3,0,2,1:T(8,128)(2,1)S(1)} fusion(s32[288]{0:T(512)S(1)} %multiply_add_fusion.2, s32[32,14]{0,1:T(8,128)S(1)} %copy-done.34, bf16[36,8,64,128]{3,2,1,0:T(8,128)(2,1)} %bitcast.235), kind=kOutput, calls=%fused_computation.9 | convolution fusion | flops 2114058240 | bytes 12061568 | tf_op jit(solution)/shard_map/se,ef->sf/dot_general | solution.py:297
  398.3 5.8 %copy.301 = bf16[32,14,64,128]{3,2,1,0:T(8,128)(2,1)} copy(bf16[32,14,64,128]{3,0,2,1:T(8,128)(2,1)S(1)} %fusion.2) | data formatting | bytes 14680064 | tf_op jit(solution)/shard_map/se,ef->sf/dot_general | solution.py:297
  404.1 7.5 %all-to-all-start.4 = ((bf16[32,14,64,128]{3,2,1,0:T(8,128)(2,1)}), bf16[32,14,64,128]{3,2,1,0:T(8,128)(2,1)}, u32[]{:S(2)}, u32[]{:S(2)}) async-start(bf16[32,14,64,128]{3,2,1,0:T(8,128)(2,1)} %copy.301), calls=%async_computation.4 | async-start | bytes 14680064 | tf_op jit(solution)/shard_map/all_to_all | solution.py:303
  439.3 49.2 %collective-permute-done.3 = bf16[1,12,64,128]{3,2,1,0:T(8,128)(2,1)} collective-permute-done((bf16[1,12,64,128]{3,2,1,0:T(8,128)(2,1)S(1)}, bf16[1,12,64,128]{3,2,1,0:T(8,128)(2,1)}, u32[]{:S(2)}, u32[]{:S(2)}) %collective-permute-start.3) | collective-permute-done | bytes 196640 | tf_op jit(solution)/shard_map/ppermute | solution.py:27
  488.5 4.0 collective-permute-done.2
  495.9 41.9 %all_gather.15 = bf16[1536,192]{1,0:T(8,128)(2,1)S(1)} all-gather(bf16[48,192]{1,0:T(8,128)(2,1)S(1)} %reduce_sum.89), channel_id=1, replica_groups=mesh['seq'=32,'grp'=4] {'seq'}, dimensions={0}, use_global_device_ids=true | all-gather | bytes 608256 | tf_op jit(solution)/shard_map/all_gather | solution.py:50
  542.8 3.9 reshape.620
  546.7 6.7 %fusion = f32[8,12,64,128]{3,1,2,0:T(8,128)S(1)} fusion(s32[8,12]{1,0:T(8,128)S(1)} %copy-done.37, s32[448]{0:T(512)S(1)} %copy-done.38, bf16[56,8,64,128]{3,2,1,0:T(8,128)(2,1)} %bitcast.95), kind=kOutput, calls=%fused_computation.4 | convolution fusion | flops 704686080 | bytes 10487936 | tf_op jit(solution)/shard_map/sc,sf->cf/dot_general | solution.py:307
  556.4 3.8 slice_bitcast_fusion
  (251 shorter events, 138.1 us)
Async XLA Ops:
  6.4 5.2 copy-start.27
  14.5 14.7 %copy-start.17 = (bf16[512,768]{1,0:T(8,128)(2,1)S(1)}, bf16[512,768]{1,0:T(8,128)(2,1)}, u32[]{:S(2)}) copy-start(bf16[512,768]{1,0:T(8,128)(2,1)} %param.23) | copy-start | bytes 2359300
  15.1 14.1 %copy-start.16 = (bf16[512,768]{1,0:T(8,128)(2,1)S(1)}, bf16[512,768]{1,0:T(8,128)(2,1)}, u32[]{:S(2)}) copy-start(bf16[512,768]{1,0:T(8,128)(2,1)} %param.24) | copy-start | bytes 2359300
  20.2 11.8 %copy-start.35 = (s32[2]{0:T(128)S(1)}, s32[2]{0:T(128)}, u32[]{:S(2)}) copy-start(s32[2]{0:T(128)} %param.27) | copy-start | bytes 28
  20.2 41.2 %all-to-all-start = ((bf16[32,2,6151]{2,1,0:T(2,128)(2,1)}), bf16[32,2,6151]{2,1,0:T(2,128)(2,1)}, u32[]{:S(2)}, u32[]{:S(2)}) async-start(bf16[32,2,6151]{2,1,0:T(2,128)(2,1)} %reshape.628), calls=%async_computation | async-start | bytes 1605632 | tf_op jit(solution)/shard_map/all_to_all | solution.py:38
  30.0 14.0 %collective-permute-start.1 = (bf16[64,1536]{1,0:T(8,128)(2,1)}, bf16[64,1536]{1,0:T(8,128)(2,1)}, u32[]{:S(2)}, u32[]{:S(2)}) collective-permute-start(bf16[64,1536]{1,0:T(8,128)(2,1)} %get-tuple-element.149), channel_id=1, source_target_pairs={{4,0},{8,4},{12,8},{16,12},{20,16},{24,20},{28,24},{32,28},{36,32}... | collective-permute-start | bytes 589832 | tf_op jit(solution)/shard_map/ppermute | solution.py:27
  30.4 19.5 %collective-permute-start = (bf16[64,1536]{1,0:T(8,128)(2,1)S(1)}, bf16[64,1536]{1,0:T(8,128)(2,1)S(1)}, u32[]{:S(2)}, u32[]{:S(2)}) collective-permute-start(bf16[64,1536]{1,0:T(8,128)(2,1)S(1)} %get-tuple-element.148), channel_id=1, source_target_pairs={{0,4},{4,8},{8,12},{12,16},{16,20},{20,24},{24,28},{28,32},{32,36}... | collective-permute-start | bytes 589832 | tf_op jit(solution)/shard_map/ppermute | solution.py:24
  68.3 28.3 %copy-start.19 = (bf16[512,768]{0,1:T(8,128)(2,1)S(1)}, bf16[512,768]{0,1:T(8,128)(2,1)}, u32[]{:S(2)}) copy-start(bf16[512,768]{0,1:T(8,128)(2,1)} %copy.278) | copy-start | bytes 2359300
  102.0 44.3 %all-to-all-start.2 = ((f32[32,48,66]{2,1,0:T(8,128)}), f32[32,48,66]{2,1,0:T(8,128)S(1)}, u32[]{:S(2)}, u32[]{:S(2)}) async-start(f32[32,48,66]{2,1,0:T(8,128)} %pad_maximum_fusion.1), calls=%async_computation.2 | async-start | bytes 1572864 | tf_op jit(solution)/shard_map/all_to_all | solution.py:331
  146.4 8.7 %copy-start.25 = (bf16[512,768]{1,0:T(8,128)(2,1)S(1)}, bf16[512,768]{1,0:T(8,128)(2,1)}, u32[]{:S(2)}) copy-start(bf16[512,768]{1,0:T(8,128)(2,1)} %param.22) | copy-start | bytes 2359300
  146.4 11.0 %copy-start.28 = (s32[8,12,3]{2,1,0:T(8,128)S(1)}, s32[8,12,3]{2,1,0:T(8,128)}, u32[]{:S(2)}) copy-start(s32[8,12,3]{2,1,0:T(8,128)} %copy-done.27) | copy-start | bytes 3460
  146.4 11.1 %copy-start.36 = (s32[2]{0:T(128)S(1)}, s32[2]{0:T(128)}, u32[]{:S(2)}) copy-start(s32[2]{0:T(128)} %param.27) | copy-start | bytes 28
  147.3 149.5 %all-to-all-start.1 = ((bf16[32,14,64,128]{3,2,1,0:T(8,128)(2,1)}), bf16[32,14,64,128]{3,2,1,0:T(8,128)(2,1)}, u32[]{:S(2)}, u32[]{:S(2)}) async-start(bf16[32,14,64,128]{3,2,1,0:T(8,128)(2,1)} %bitcast.209), calls=%async_computation.1 | async-start | bytes 14680064 | tf_op jit(solution)/shard_map/all_to_all | solution.py:235
  155.1 5.3 copy-start.30
  179.3 6.4 %copy-start.6 = (bf16[8,12,64,2,64]{2,0,4,1,3:T(8,128)(2,1)S(1)}, bf16[8,12,64,2,64]{2,0,4,1,3:T(8,128)(2,1)}, u32[]{:S(2)}) copy-start(bf16[8,12,64,2,64]{2,0,4,1,3:T(8,128)(2,1)} %get-tuple-element.141) | copy-start | bytes 4718596
  191.7 6.4 %copy-start.10 = (bf16[8,12,1,64,128]{4,3,1,0,2:T(8,128)(2,1)S(1)}, bf16[8,12,1,64,128]{4,3,1,0,2:T(8,128)(2,1)}, u32[]{:S(2)}) copy-start(bf16[8,12,1,64,128]{4,3,1,0,2:T(8,128)(2,1)} %stack.23) | copy-start | bytes 4718596
  191.8 8.1 %copy-start.9 = (bf16[8,12,1,64,128]{4,3,1,0,2:T(8,128)(2,1)S(1)}, bf16[8,12,1,64,128]{4,3,1,0,2:T(8,128)(2,1)}, u32[]{:S(2)}) copy-start(bf16[8,12,1,64,128]{4,3,1,0,2:T(8,128)(2,1)} %stack.24) | copy-start | bytes 4718596
  205.3 5.2 copy-start.14
  211.9 70.8 %copy-start.15 = (bf16[2,64,12,64]{3,2,1,0:T(8,128)(2,1)S(1)}, bf16[2,64,12,64]{3,2,1,0:T(8,128)(2,1)}, u32[]{:S(2)}) copy-start(bf16[2,64,12,64]{3,2,1,0:T(8,128)(2,1)} %copy-done.14) | copy-start | bytes 589828
  211.9 80.4 %copy-start.2 = (f32[12,2,64,512]{3,2,1,0:T(8,128)S(1)}, f32[12,2,64,512]{3,2,1,0:T(8,128)}, u32[]{:S(2)}) copy-start(f32[12,2,64,512]{3,2,1,0:T(8,128)} %copy-done.1) | copy-start | bytes 9437188
  380.6 8.2 %copy-start.34 = (s32[32,14]{0,1:T(8,128)S(1)}, s32[32,14]{0,1:T(8,128)}, u32[]{:S(2)}) copy-start(s32[32,14]{0,1:T(8,128)} %multiply_add_fusion) | copy-start | bytes 5380
  383.8 20.2 %all-to-all-start.3 = ((bf16[32,48,192]{2,1,0:T(8,128)(2,1)}), bf16[32,48,192]{2,1,0:T(8,128)(2,1)}, u32[]{:S(2)}, u32[]{:S(2)}) async-start(bf16[32,48,192]{2,1,0:T(8,128)(2,1)} %pad_maximum_fusion.2), calls=%async_computation.3 | async-start | bytes 1572864 | tf_op jit(solution)/shard_map/all_to_all | solution.py:48
  404.1 9.4 %copy-start.39 = (s32[4]{0:T(128)S(1)}, s32[4]{0:T(128)}, u32[]{:S(2)}) copy-start(s32[4]{0:T(128)} %constant.301.clone.1) | copy-start | bytes 52
  404.1 142.6 %all-to-all-start.4 = ((bf16[32,14,64,128]{3,2,1,0:T(8,128)(2,1)}), bf16[32,14,64,128]{3,2,1,0:T(8,128)(2,1)}, u32[]{:S(2)}, u32[]{:S(2)}) async-start(bf16[32,14,64,128]{3,2,1,0:T(8,128)(2,1)} %copy.301), calls=%async_computation.4 | async-start | bytes 14680064 | tf_op jit(solution)/shard_map/all_to_all | solution.py:303
  411.6 9.9 %copy-start.31 = (f32[2,12,64]{2,0,1:T(2,128)S(1)}, f32[2,12,64]{2,0,1:T(2,128)}, u32[]{:S(2)}) copy-start(f32[2,12,64]{2,0,1:T(2,128)} %copy.290) | copy-start | bytes 18436
  418.4 7.6 %slice-start = ((s8[9437184]{0:T(1024)(128)(4,1)}), s8[4194304]{0:T(1024)(128)(4,1)S(1)}, s32[]{:S(2)}) async-start(s8[9437184]{0:T(1024)(128)(4,1)} %bitcast.211), calls=%async_computation.5 | async-start | bytes 8388608
  427.2 5.1 copy-start.13
  430.4 58.0 %collective-permute-start.3 = (bf16[1,12,64,128]{3,2,1,0:T(8,128)(2,1)S(1)}, bf16[1,12,64,128]{3,2,1,0:T(8,128)(2,1)}, u32[]{:S(2)}, u32[]{:S(2)}) collective-permute-start(bf16[1,12,64,128]{3,2,1,0:T(8,128)(2,1)S(1)} %get-tuple-element.147), channel_id=1, source_target_pairs={{4,0},{8,4},{12,8},{16,12},{20,16},{24,20},{28,24},{32,28},{36,32}... | collective-permute-start | bytes 589832 | tf_op jit(solution)/shard_map/ppermute | solution.py:27
  430.9 61.6 %collective-permute-start.2 = (bf16[1,12,64,128]{3,2,1,0:T(8,128)(2,1)S(1)}, bf16[1,12,64,128]{3,2,1,0:T(8,128)(2,1)}, u32[]{:S(2)}, u32[]{:S(2)}) collective-permute-start(bf16[1,12,64,128]{3,2,1,0:T(8,128)(2,1)S(1)} %get-tuple-element.146), channel_id=1, source_target_pairs={{0,4},{4,8},{8,12},{12,16},{16,20},{20,24},{24,28},{28,32},{32,36}... | collective-permute-start | bytes 589832 | tf_op jit(solution)/shard_map/ppermute | solution.py:24
  495.9 42.1 %copy-start.12 = (f32[8,12,64,64]{3,2,1,0:T(8,128)S(1)}, f32[8,12,64,64]{3,2,1,0:T(8,128)}, u32[]{:S(2)}) copy-start(f32[8,12,64,64]{3,2,1,0:T(8,128)} %get-tuple-element.106) | copy-start | bytes 4718596
  540.3 6.4 %copy-start.37 = (s32[8,12]{1,0:T(8,128)S(1)}, s32[8,12]{1,0:T(8,128)}, u32[]{:S(2)}) copy-start(s32[8,12]{1,0:T(8,128)} %multiply_add_fusion.1) | copy-start | bytes 1156
  540.3 6.4 %copy-start.38 = (s32[448]{0:T(512)S(1)}, s32[448]{0:T(512)}, u32[]{:S(2)}) copy-start(s32[448]{0:T(512)} %eq.123) | copy-start | bytes 5380
  (21 other events, 55.7 us)

commit v8 on v7

--- a/solution.py
+++ b/solution.py
@@ -31,15 +31,19 @@
 
 def from_owners(value, owners, extra):
     devices = lax.axis_size("seq")
-    count = value.shape[0]
-    chunks = value.reshape(count, devices, -1).transpose(1, 0, 2).reshape(devices, -1)
-    width = chunks.shape[1]
-    packed = jnp.concatenate([chunks, extra.astype(value.dtype)], axis=1)
-    got = lax.all_to_all(packed, "seq", 0, 0, tiled=True)
-    rows = got[:, :width].reshape(devices, count, -1)
+    count, rows_all, width = value.shape
+    per = rows_all // devices
+    chunks = value.reshape(count, devices, per, width).transpose(1, 0, 2, 3)
+    chunks = chunks.reshape(devices, count * per, width)
+    side = jnp.pad(extra.astype(value.dtype), ((0, 0), (0, width - extra.shape[1])))
+    got = lax.all_to_all(
+        jnp.concatenate([chunks, side[:, None, :]], axis=1), "seq", 0, 0, tiled=True
+    )
+    rows = got[:, : count * per].reshape(devices, count, per, width)
     mine = jnp.stack([rows[owners[i], i] for i in range(count)])
     full = lax.all_gather(mine, "seq", axis=0, tiled=False)
-    return full.transpose(1, 0, 2).reshape(value.shape), got[:, width:].astype(extra.dtype)
+    wanted = got[:, count * per, : extra.shape[1]].astype(extra.dtype)
+    return full.transpose(1, 0, 2, 3).reshape(value.shape), wanted
 
 
 def summed_to_all(value):

time: 584 us -> 580 us (level)
  waiting for transfers between devices: 53.3 us -> 61.5 us
    unnamed x103 -> x97, local copies, waits for them, and re-layouts: 34.3 us -> 25.6 us
    ppermute x2, waiting for transfers between devices: 49.2 us -> 57.4 us  [padded_2(): lax.ppermute(lax.slice_in_dim(block, 0, width, axis=dim), axis, backward)]
  transfers between devices with their start and end apart: 9 -> 9, of which waited for: 2 -> 3; matrix products, arithmetic and copies ran while one was open for 33% -> 33% of each run, Pallas kernels for 0% -> 0%
where the time goes in v8:
time: 580 us; the launch traced here: 570 us
  local copies, waits for them, and re-layouts  192 us (33%)
  blocking collectives  131 us (23%)
  Pallas kernels  65.5 us (11%)
  waiting for transfers between devices  61.5 us (11%)
  other arithmetic  45.3 us (8%)
  starting transfers between devices  38.9 us (7%)
  matrix products  25.7 us (4%)
  between operations  10.7 us (2%)
    all_gather x1, blocking collectives, per_device(): lax.all_gather(jnp.concatenate([top[:, None], tot[:, None], acc], axis=-1...  65.7 us
    pallas_call x1, Pallas kernels, sparse_call(): pl.pallas_call(lambda *refs: sparse_kernel(*refs, factor=factor), grid=(b...  65.5 us
    ppermute x2, waiting for transfers between devices, padded_2(): lax.ppermute(lax.slice_in_dim(block, 0, width, axis=dim), axis, backward)  57.4 us
    all_gather x1, blocking collectives, summed_to_all(): full = lax.all_gather(total, 'seq', axis=0, tiled=True)  41.9 us
    unnamed x97, local copies, waits for them, and re-layouts  25.6 us
    all_gather x1, blocking collectives, from_owners(): full = lax.all_gather(mine, 'seq', axis=0, tiled=False)  23.2 us
    another operation x3, local copies, waits for them, and re-layouts, run_group(): jnp.stack([kv_heads[0:group], kv_heads[1:group + 1], kv_heads[2:group + 2...  15.4 us
    concatenate x5, local copies, waits for them, and re-layouts, per_device(): jnp.concatenate([left_rows[None, :, :2 * width], kv_rows.reshape(per_dev,...  14.7 us
  transfers between devices with their start and end apart: 9, of which 3 were waited for; matrix products, arithmetic and copies ran while one was open for 33% of the time, Pallas kernels for 0%

profile of v8, /device:TPU:19, one launch (start us, length us, event | category | flops | bytes accessed | tf_op | source)
XLA Modules:
  0.0 570.5 jit_solution(15242248578048328108)
XLA Ops:
  15.4 8.9 %all-to-all-start = ((bf16[32,5,3072]{2,1,0:T(8,128)(2,1)}), bf16[32,5,3072]{2,1,0:T(8,128)(2,1)}, u32[]{:S(2)}, u32[]{:S(2)}) async-start(bf16[32,5,3072]{2,1,0:T(8,128)(2,1)} %copy.214), calls=%async_computation | async-start | bytes 3145728 | tf_op jit(solution)/shard_map/all_to_all | solution.py:39
  33.9 3.9 concatenate.83
  39.1 6.9 %collective-permute-done.1 = bf16[64,1536]{1,0:T(8,128)(2,1)} collective-permute-done((bf16[64,1536]{1,0:T(8,128)(2,1)}, bf16[64,1536]{1,0:T(8,128)(2,1)}, u32[]{:S(2)}, u32[]{:S(2)}) %collective-permute-start.1) | collective-permute-done | bytes 196640 | tf_op jit(solution)/shard_map/ppermute | solution.py:27
  48.1 3.7 copy.205
  56.7 6.5 %maximum_bitcast_fusion = bf16[10,12,64,2,64]{2,0,4,1,3:T(8,128)(2,1)} fusion(bf16[1,64,2,12,64]{1,0,4,3,2:T(2,128)(2,1)} %copy.205, bf16[8,64,2,12,64]{1,0,4,3,2:T(8,128)(2,1)S(1)} %concatenate.83, bf16[1,64,2,12,64]{1,0,4,3,2:T(2,128)(2,1)} %copy.204), kind=kLoop, calls=%fused_computation.6 | loop fusion | flops 5898240 | bytes 3932160 | tf_op jit(solution)/shard_map/transpose | solution.py:69
  65.3 23.2 %all-gather = bf16[64,2,3072]{2,1,0:T(2,128)(2,1)S(1)} all-gather(bf16[2,2,3072]{2,1,0:T(2,128)(2,1)S(1)} %pad_maximum_fusion.8), channel_id=2, replica_groups=mesh['seq'=32,'grp'=4] {'seq'}, dimensions={0}, use_global_device_ids=true | all-gather | bytes 811008 | tf_op jit(solution)/shard_map/all_gather | solution.py:44
  97.2 6.0 %all-to-all-start.2 = ((f32[32,48,66]{2,1,0:T(8,128)}), f32[32,48,66]{2,1,0:T(8,128)S(1)}, u32[]{:S(2)}, u32[]{:S(2)}) async-start(f32[32,48,66]{2,1,0:T(8,128)} %pad_maximum_fusion.1), calls=%async_computation.2 | async-start | bytes 1572864 | tf_op jit(solution)/shard_map/all_to_all | solution.py:335
  103.3 8.5 %fusion.61 = (bf16[8,12,64,2,64]{2,0,4,1,3:T(8,128)(2,1)}, bf16[8,12,64,2,64]{2,0,4,1,3:T(8,128)(2,1)}, bf16[8,12,64,2,64]{2,0,4,1,3:T(8,128)(2,1)}) fusion(bf16[10,12,64,2,64]{2,0,4,1,3:T(8,128)(2,1)} %maximum_bitcast_fusion), kind=kLoop, calls=%fused_computation.184 | loop fusion | bytes 9437184 | tf_op jit(solution)/shard_map/slice | solution.py:260
  111.8 9.4 %copy.207 = bf16[8,12,64,2,64]{4,3,2,1,0:T(2,128)(2,1)} copy(bf16[8,12,64,2,64]{2,0,4,1,3:T(8,128)(2,1)} %get-tuple-element.140) | data formatting | bytes 3145728 | tf_op jit(solution)/shard_map/slice | solution.py:260
  121.2 5.3 reshape.592
  128.2 13.3 %gather_fusion = bf16[448,64,128]{2,1,0:T(8,128)(2,1)} fusion(bf16[96,64,128]{2,1,0:T(8,128)(2,1)S(1)} %reshape.592, s32[1024]{0:T(1024)S(1)} %pad_clamp_fusion), kind=kCustom, calls=%fused_computation | custom fusion | bytes 14681856 | tf_op jit(solution)/shard_map/gather | solution.py:235
  142.4 7.8 %all-to-all-start.1 = ((bf16[32,14,64,128]{3,2,1,0:T(8,128)(2,1)}), bf16[32,14,64,128]{3,2,1,0:T(8,128)(2,1)}, u32[]{:S(2)}, u32[]{:S(2)}) async-start(bf16[32,14,64,128]{3,2,1,0:T(8,128)(2,1)} %bitcast.209), calls=%async_computation.1 | async-start | bytes 14680064 | tf_op jit(solution)/shard_map/all_to_all | solution.py:239
  157.6 4.9 copy_bitcast_fusion
  165.1 9.4 %copy.206 = bf16[8,12,64,2,64]{4,3,2,1,0:T(2,128)(2,1)} copy(bf16[8,12,64,2,64]{2,0,4,1,3:T(8,128)(2,1)} %get-tuple-element.141) | data formatting | bytes 3145728 | tf_op jit(solution)/shard_map/slice | solution.py:260
  174.5 6.4 %stack.23 = bf16[8,12,1,64,128]{4,3,1,0,2:T(8,128)(2,1)} reshape(bf16[8,12,64,2,64]{4,3,2,1,0:T(2,128)(2,1)} %copy.206) | data formatting | bytes 3145728 | tf_op jit(solution)/shard_map/stack | solution.py:259
  180.9 5.9 %copy.208 = bf16[8,12,64,2,64]{4,3,2,1,0:T(2,128)(2,1)} copy(bf16[8,12,64,2,64]{2,0,4,1,3:T(8,128)(2,1)S(1)} %copy-done.6) | data formatting | bytes 3145728 | tf_op jit(solution)/shard_map/slice | solution.py:260
  186.8 6.4 %stack.25 = bf16[8,12,1,64,128]{4,3,1,0,2:T(8,128)(2,1)} reshape(bf16[8,12,64,2,64]{4,3,2,1,0:T(2,128)(2,1)} %copy.208) | data formatting | bytes 3145728 | tf_op jit(solution)/shard_map/stack | solution.py:259
  211.0 65.7 %all_gather.14 = f32[1536,66]{1,0:T(8,128)S(1)} all-gather(f32[48,66]{1,0:T(8,128)S(1)} %pad_maximum_fusion.9), channel_id=1, replica_groups=mesh['seq'=32,'grp'=4] {'seq'}, dimensions={0}, use_global_device_ids=true | all-gather | bytes 418176 | tf_op jit(solution)/shard_map/all_gather | solution.py:340
  291.9 8.0 %gather_fusion.1 = bf16[288,64,128]{2,1,0:T(8,128)(2,1)} fusion(bf16[32,14,64,128]{3,2,1,0:T(8,128)(2,1)} %all-to-all-done.1, s32[288]{0:T(512)S(1)} %fusion.57), kind=kCustom, calls=%fused_computation.1 | custom fusion | bytes 9439488 | tf_op jit(solution)/shard_map/gather | solution.py:240
  299.8 5.9 %constant_dynamic-update-slice_fusion.2 = bf16[8,12,8,64,128]{4,3,2,1,0:T(8,128)(2,1)} fusion(bf16[8,12,8,64,128]{4,3,2,1,0:T(8,128)(2,1)} %broadcast_dynamic-update-slice_fusion, bf16[8,12,3,64,128]{4,3,2,1,0:T(8,128)(2,1)} %bitcast.210), kind=kLoop, calls=%fused_computation.129 | loop fusion | bytes 9437184 | tf_op jit(solution)/shard_map/concatenate | solution.py:262
  305.8 65.5 %shard_map.93 = (f32[8,12,64,64]{3,2,1,0:T(8,128)}, f32[8,12,64,64]{3,2,1,0:T(8,128)}, f32[8,12,3,64,128]{4,3,2,1,0:T(8,128)}, f32[8,12,2,64,128]{4,3,2,1,0:T(8,128)}, bf16[8,12,3,64,128]{4,3,2,1,0:T(8,128)(2,1)}) custom-call(bf16[8,12,64,64]{3,2,1,0:T(8,128)(2,1)} %get-tuple-element.173.refs_0_, bf16[8,12,64,64]{3,2,1,0:T(8,128)(2,1)} %get-tuple-element.172.refs_1_, ...), custom_call_target="tpu_custom_call" | custom-call | tf_op jit(solution)/shard_map/pallas_call | solution.py:158
  371.3 4.3 reduce_sum.88
  378.9 5.0 all-to-all-start.3
  383.9 9.4 %fusion.2 = bf16[32,14,64,128]{3,0,2,1:T(8,128)(2,1)S(1)} fusion(s32[288]{0:T(512)S(1)} %multiply_add_fusion.2, s32[32,14]{0,1:T(8,128)S(1)} %copy-done.33, bf16[36,8,64,128]{3,2,1,0:T(8,128)(2,1)} %bitcast.233), kind=kOutput, calls=%fused_computation.9 | convolution fusion | flops 2114058240 | bytes 12061568 | tf_op jit(solution)/shard_map/se,ef->sf/dot_general | solution.py:301
  393.3 5.8 %copy.250 = bf16[32,14,64,128]{3,2,1,0:T(8,128)(2,1)} copy(bf16[32,14,64,128]{3,0,2,1:T(8,128)(2,1)S(1)} %fusion.2) | data formatting | bytes 14680064 | tf_op jit(solution)/shard_map/se,ef->sf/dot_general | solution.py:301
  399.1 7.6 %all-to-all-start.4 = ((bf16[32,14,64,128]{3,2,1,0:T(8,128)(2,1)}), bf16[32,14,64,128]{3,2,1,0:T(8,128)(2,1)}, u32[]{:S(2)}, u32[]{:S(2)}) async-start(bf16[32,14,64,128]{3,2,1,0:T(8,128)(2,1)} %copy.250), calls=%async_computation.4 | async-start | bytes 14680064 | tf_op jit(solution)/shard_map/all_to_all | solution.py:307
  433.0 50.6 %collective-permute-done.3 = bf16[1,12,64,128]{3,2,1,0:T(8,128)(2,1)} collective-permute-done((bf16[1,12,64,128]{3,2,1,0:T(8,128)(2,1)S(1)}, bf16[1,12,64,128]{3,2,1,0:T(8,128)(2,1)}, u32[]{:S(2)}, u32[]{:S(2)}) %collective-permute-start.3) | collective-permute-done | bytes 196640 | tf_op jit(solution)/shard_map/ppermute | solution.py:27
  483.6 4.0 collective-permute-done.2
  491.0 41.9 %all_gather.15 = bf16[1536,192]{1,0:T(8,128)(2,1)S(1)} all-gather(bf16[48,192]{1,0:T(8,128)(2,1)S(1)} %reduce_sum.89), channel_id=1, replica_groups=mesh['seq'=32,'grp'=4] {'seq'}, dimensions={0}, use_global_device_ids=true | all-gather | bytes 608256 | tf_op jit(solution)/shard_map/all_gather | solution.py:54
  537.8 3.9 reshape.637
  541.7 6.7 %fusion = f32[8,12,64,128]{3,1,2,0:T(8,128)S(1)} fusion(s32[8,12]{1,0:T(8,128)S(1)} %copy-done.36, s32[448]{0:T(512)S(1)} %copy-done.37, bf16[56,8,64,128]{3,2,1,0:T(8,128)(2,1)} %bitcast.96), kind=kOutput, calls=%fused_computation.4 | convolution fusion | flops 704686080 | bytes 10487936 | tf_op jit(solution)/shard_map/sc,sf->cf/dot_general | solution.py:311
  551.4 3.7 slice_bitcast_fusion
  (245 shorter events, 135.1 us)
Async XLA Ops:
  6.6 5.3 copy-start.26
  13.7 10.7 %copy-start.17 = (bf16[512,768]{1,0:T(8,128)(2,1)S(1)}, bf16[512,768]{1,0:T(8,128)(2,1)}, u32[]{:S(2)}) copy-start(bf16[512,768]{1,0:T(8,128)(2,1)} %param.23) | copy-start | bytes 2359300
  13.7 10.7 %copy-start.16 = (bf16[512,768]{1,0:T(8,128)(2,1)S(1)}, bf16[512,768]{1,0:T(8,128)(2,1)}, u32[]{:S(2)}) copy-start(bf16[512,768]{1,0:T(8,128)(2,1)} %param.24) | copy-start | bytes 2359300
  15.4 11.5 %copy-start.34 = (s32[2]{0:T(128)S(1)}, s32[2]{0:T(128)}, u32[]{:S(2)}) copy-start(s32[2]{0:T(128)} %param.27) | copy-start | bytes 28
  15.4 47.8 %all-to-all-start = ((bf16[32,5,3072]{2,1,0:T(8,128)(2,1)}), bf16[32,5,3072]{2,1,0:T(8,128)(2,1)}, u32[]{:S(2)}, u32[]{:S(2)}) async-start(bf16[32,5,3072]{2,1,0:T(8,128)(2,1)} %copy.214), calls=%async_computation | async-start | bytes 3145728 | tf_op jit(solution)/shard_map/all_to_all | solution.py:39
  25.2 20.7 %collective-permute-start.1 = (bf16[64,1536]{1,0:T(8,128)(2,1)}, bf16[64,1536]{1,0:T(8,128)(2,1)}, u32[]{:S(2)}, u32[]{:S(2)}) collective-permute-start(bf16[64,1536]{1,0:T(8,128)(2,1)} %get-tuple-element.147), channel_id=1, source_target_pairs={{4,0},{8,4},{12,8},{16,12},{20,16},{24,20},{28,24},{32,28},{36,32}... | collective-permute-start | bytes 589832 | tf_op jit(solution)/shard_map/ppermute | solution.py:27
  25.6 26.2 %collective-permute-start = (bf16[64,1536]{1,0:T(8,128)(2,1)S(1)}, bf16[64,1536]{1,0:T(8,128)(2,1)S(1)}, u32[]{:S(2)}, u32[]{:S(2)}) collective-permute-start(bf16[64,1536]{1,0:T(8,128)(2,1)S(1)} %get-tuple-element.146), channel_id=1, source_target_pairs={{0,4},{4,8},{8,12},{12,16},{16,20},{20,24},{24,28},{28,32},{32,36}... | collective-permute-start | bytes 589832 | tf_op jit(solution)/shard_map/ppermute | solution.py:24
  64.9 26.9 %copy-start.18 = (bf16[512,768]{0,1:T(8,128)(2,1)S(1)}, bf16[512,768]{0,1:T(8,128)(2,1)}, u32[]{:S(2)}) copy-start(bf16[512,768]{0,1:T(8,128)(2,1)} %copy.226) | copy-start | bytes 2359300
  97.2 44.3 %all-to-all-start.2 = ((f32[32,48,66]{2,1,0:T(8,128)}), f32[32,48,66]{2,1,0:T(8,128)S(1)}, u32[]{:S(2)}, u32[]{:S(2)}) async-start(f32[32,48,66]{2,1,0:T(8,128)} %pad_maximum_fusion.1), calls=%async_computation.2 | async-start | bytes 1572864 | tf_op jit(solution)/shard_map/all_to_all | solution.py:335
  141.6 8.7 %copy-start.25 = (bf16[512,768]{1,0:T(8,128)(2,1)S(1)}, bf16[512,768]{1,0:T(8,128)(2,1)}, u32[]{:S(2)}) copy-start(bf16[512,768]{1,0:T(8,128)(2,1)} %param.22) | copy-start | bytes 2359300
  141.6 10.9 %copy-start.27 = (s32[8,12,3]{2,1,0:T(8,128)S(1)}, s32[8,12,3]{2,1,0:T(8,128)}, u32[]{:S(2)}) copy-start(s32[8,12,3]{2,1,0:T(8,128)} %copy-done.26) | copy-start | bytes 3460
  141.6 11.1 %copy-start.35 = (s32[2]{0:T(128)S(1)}, s32[2]{0:T(128)}, u32[]{:S(2)}) copy-start(s32[2]{0:T(128)} %param.27) | copy-start | bytes 28
  142.4 149.4 %all-to-all-start.1 = ((bf16[32,14,64,128]{3,2,1,0:T(8,128)(2,1)}), bf16[32,14,64,128]{3,2,1,0:T(8,128)(2,1)}, u32[]{:S(2)}, u32[]{:S(2)}) async-start(bf16[32,14,64,128]{3,2,1,0:T(8,128)(2,1)} %bitcast.209), calls=%async_computation.1 | async-start | bytes 14680064 | tf_op jit(solution)/shard_map/all_to_all | solution.py:239
  150.3 5.3 copy-start.29
  174.5 6.4 %copy-start.6 = (bf16[8,12,64,2,64]{2,0,4,1,3:T(8,128)(2,1)S(1)}, bf16[8,12,64,2,64]{2,0,4,1,3:T(8,128)(2,1)}, u32[]{:S(2)}) copy-start(bf16[8,12,64,2,64]{2,0,4,1,3:T(8,128)(2,1)} %get-tuple-element.139) | copy-start | bytes 4718596
  186.8 6.4 %copy-start.10 = (bf16[8,12,1,64,128]{4,3,1,0,2:T(8,128)(2,1)S(1)}, bf16[8,12,1,64,128]{4,3,1,0,2:T(8,128)(2,1)}, u32[]{:S(2)}) copy-start(bf16[8,12,1,64,128]{4,3,1,0,2:T(8,128)(2,1)} %stack.23) | copy-start | bytes 4718596
  186.8 8.1 %copy-start.9 = (bf16[8,12,1,64,128]{4,3,1,0,2:T(8,128)(2,1)S(1)}, bf16[8,12,1,64,128]{4,3,1,0,2:T(8,128)(2,1)}, u32[]{:S(2)}) copy-start(bf16[8,12,1,64,128]{4,3,1,0,2:T(8,128)(2,1)} %stack.24) | copy-start | bytes 4718596
  200.0 5.4 copy-start.5
  201.6 5.2 copy-start.14
  208.3 69.6 %copy-start.15 = (bf16[2,64,12,64]{3,2,1,0:T(8,128)(2,1)S(1)}, bf16[2,64,12,64]{3,2,1,0:T(8,128)(2,1)}, u32[]{:S(2)}) copy-start(bf16[2,64,12,64]{3,2,1,0:T(8,128)(2,1)} %copy-done.14) | copy-start | bytes 589828
  208.3 79.1 %copy-start.2 = (f32[12,2,64,512]{3,2,1,0:T(8,128)S(1)}, f32[12,2,64,512]{3,2,1,0:T(8,128)}, u32[]{:S(2)}) copy-start(f32[12,2,64,512]{3,2,1,0:T(8,128)} %copy-done.1) | copy-start | bytes 9437188
  375.6 8.3 %copy-start.33 = (s32[32,14]{0,1:T(8,128)S(1)}, s32[32,14]{0,1:T(8,128)}, u32[]{:S(2)}) copy-start(s32[32,14]{0,1:T(8,128)} %multiply_add_fusion) | copy-start | bytes 5380
  378.9 20.3 %all-to-all-start.3 = ((bf16[32,48,192]{2,1,0:T(8,128)(2,1)}), bf16[32,48,192]{2,1,0:T(8,128)(2,1)}, u32[]{:S(2)}, u32[]{:S(2)}) async-start(bf16[32,48,192]{2,1,0:T(8,128)(2,1)} %pad_maximum_fusion.2), calls=%async_computation.3 | async-start | bytes 1572864 | tf_op jit(solution)/shard_map/all_to_all | solution.py:52
  399.1 9.5 %copy-start.38 = (s32[4]{0:T(128)S(1)}, s32[4]{0:T(128)}, u32[]{:S(2)}) copy-start(s32[4]{0:T(128)} %constant.302.clone.1) | copy-start | bytes 52
  399.1 142.5 %all-to-all-start.4 = ((bf16[32,14,64,128]{3,2,1,0:T(8,128)(2,1)}), bf16[32,14,64,128]{3,2,1,0:T(8,128)(2,1)}, u32[]{:S(2)}, u32[]{:S(2)}) async-start(bf16[32,14,64,128]{3,2,1,0:T(8,128)(2,1)} %copy.250), calls=%async_computation.4 | async-start | bytes 14680064 | tf_op jit(solution)/shard_map/all_to_all | solution.py:307
  406.7 8.7 %copy-start.30 = (f32[2,12,64]{2,0,1:T(2,128)S(1)}, f32[2,12,64]{2,0,1:T(2,128)}, u32[]{:S(2)}) copy-start(f32[2,12,64]{2,0,1:T(2,128)} %copy.238) | copy-start | bytes 18436
  412.2 7.6 %slice-start = ((s8[9437184]{0:T(1024)(128)(4,1)}), s8[4194304]{0:T(1024)(128)(4,1)S(1)}, s32[]{:S(2)}) async-start(s8[9437184]{0:T(1024)(128)(4,1)} %bitcast.211), calls=%async_computation.5 | async-start | bytes 8388608
  424.3 59.3 %collective-permute-start.3 = (bf16[1,12,64,128]{3,2,1,0:T(8,128)(2,1)S(1)}, bf16[1,12,64,128]{3,2,1,0:T(8,128)(2,1)}, u32[]{:S(2)}, u32[]{:S(2)}) collective-permute-start(bf16[1,12,64,128]{3,2,1,0:T(8,128)(2,1)S(1)} %get-tuple-element.145), channel_id=1, source_target_pairs={{4,0},{8,4},{12,8},{16,12},{20,16},{24,20},{28,24},{32,28},{36,32}... | collective-permute-start | bytes 589832 | tf_op jit(solution)/shard_map/ppermute | solution.py:27
  424.7 62.9 %collective-permute-start.2 = (bf16[1,12,64,128]{3,2,1,0:T(8,128)(2,1)S(1)}, bf16[1,12,64,128]{3,2,1,0:T(8,128)(2,1)}, u32[]{:S(2)}, u32[]{:S(2)}) collective-permute-start(bf16[1,12,64,128]{3,2,1,0:T(8,128)(2,1)S(1)} %get-tuple-element.144), channel_id=1, source_target_pairs={{0,4},{4,8},{8,12},{12,16},{16,20},{20,24},{24,28},{28,32},{32,36}... | collective-permute-start | bytes 589832 | tf_op jit(solution)/shard_map/ppermute | solution.py:24
  491.0 42.1 %copy-start.12 = (f32[8,12,64,64]{3,2,1,0:T(8,128)S(1)}, f32[8,12,64,64]{3,2,1,0:T(8,128)}, u32[]{:S(2)}) copy-start(f32[8,12,64,64]{3,2,1,0:T(8,128)} %get-tuple-element.106) | copy-start | bytes 4718596
  535.3 6.4 %copy-start.36 = (s32[8,12]{1,0:T(8,128)S(1)}, s32[8,12]{1,0:T(8,128)}, u32[]{:S(2)}) copy-start(s32[8,12]{1,0:T(8,128)} %multiply_add_fusion.1) | copy-start | bytes 1156
  535.3 6.4 %copy-start.37 = (s32[448]{0:T(512)S(1)}, s32[448]{0:T(512)}, u32[]{:S(2)}) copy-start(s32[448]{0:T(512)} %reshape.608) | copy-start | bytes 5380
  (19 other events, 52.0 us)
